TPU v7x, 256 devices: a whole 4x4x8 slice. The times are simulated.
256 devices in a mesh: lon: 64 (over y, z, x_hi), lat: 4 (over x_lo, core).
Axes of the slice: x: 4 (x_hi: 2, x_lo: 2; x = x_hi * 2 + x_lo), y: 4, z: 8, core: 2. Of those that a mesh axis runs over, the one named last changes fastest.
Arguments:
- initial_state: float32 [4, 32, 1024, 512], P(None, None, 'lon', 'lat'), may hold values from -6 to 6
- coefficients: float32 [4, 32, 1024, 512], P(None, None, 'lon', 'lat'), may hold values from 0.02 to 0.24
- coupling: float32 [32, 4, 4], replicated, may hold values from -3 to 3
- obs_band: int32 [4, 32768, 1], P('lat', 'lon'), may hold values from 0 to 63; in each aligned block of 512 rows (0 to 511, 512 to 1023, ..., all dimensions but the last counted through in order) at most 32 rows name the same one
- obs_cell: int32 [4, 32768], P('lat', 'lon'), may hold values from 0 to 262143
- obs_value: float32 [4, 32768], P('lat', 'lon'), may hold values from -6 to 6
- obs_weight: float32 [4, 32768], P('lat', 'lon'), may hold values from 0.5 to 4
- obs_count: int32 [4, 64], P('lat', 'lon'), may hold values from 256 to 512
Outputs:
- final_state: float32 [4, 32, 1024, 512], P(None, None, 'lon', 'lat')
- gradient: float32 [4, 32, 1024, 512], P(None, None, 'lon', 'lat')
Inputs may be any that keep to these rules, and one draw needn't show every extreme that they name: `obs_band`: in the 512 rows of one device no band is named more than 32 times, a bound that some block reaches.
All inputs are finite; a program needn't handle non-finite values.
Results may differ from a plain program's by a relative error of at most 0.0003.
Values sent between devices are 32-bit elements; how exact they have to be, the bound alone decides.
No kernel may reach another device: no remote copies, remote signals or barrier semaphores. Data moves between devices by JAX's collectives and lax.ppermute only.
A program may use at most 128 MiB of HBM per device.

v0:
```python
import jax
import jax.numpy as jnp
from jax import lax
from jax.sharding import PartitionSpec as P
from jax.experimental import pallas as pl
from jax.experimental.pallas import tpu as pltpu

STEPS = 2
CAP = 32


def ring_pairs(n_lon, n_lat):
    half = n_lon // 2
    pairs = []
    for i in range(half):
        ring = [(i, j) for j in range(n_lat)] + [(i + half, j) for j in range(n_lat - 1, -1, -1)]
        for k in range(len(ring)):
            a, b = ring[k], ring[(k + 1) % len(ring)]
            pairs.append((a[0] * n_lat + a[1], b[0] * n_lat + b[1]))
    return pairs


def halos(x, flip):
    n_lon = lax.axis_size("lon")
    n_lat = lax.axis_size("lat")
    lon_i = lax.axis_index("lon")
    lat_j = lax.axis_index("lat")
    up = [(i, (i + 1) % n_lon) for i in range(n_lon)]
    down = [(b, a) for a, b in up]
    from_west = lax.ppermute(x[:, :, -1, :], "lon", up)
    from_east = lax.ppermute(x[:, :, 0, :], "lon", down)
    low = lon_i < n_lon // 2
    first_row = x[:, :, :, 0]
    last_row = x[:, :, :, -1]
    cw_pairs = ring_pairs(n_lon, n_lat)
    ccw_pairs = [(b, a) for a, b in cw_pairs]
    cw = lax.ppermute(jnp.where(low, last_row, first_row), ("lon", "lat"), cw_pairs)
    ccw = lax.ppermute(jnp.where(low, first_row, last_row), ("lon", "lat"), ccw_pairs)
    north_row = jnp.where(low, cw, ccw)
    south_row = jnp.where(low, ccw, cw)
    north_row = jnp.where(lat_j == 0, flip * north_row, north_row)
    south_row = jnp.where(lat_j == n_lat - 1, flip * south_row, south_row)
    return north_row, south_row, from_west, from_east


def shifted(x, halo):
    north_row, south_row, from_west, from_east = halo
    north = jnp.concatenate([north_row[..., None], x[..., :-1]], axis=3)
    south = jnp.concatenate([x[..., 1:], south_row[..., None]], axis=3)
    west = jnp.concatenate([from_west[:, :, None, :], x[:, :, :-1, :]], axis=2)
    east = jnp.concatenate([x[:, :, 1:, :], from_east[:, :, None, :]], axis=2)
    return north, south, west, east


def mix(coupling, v, transpose):
    out = []
    for g in range(v.shape[0]):
        acc = None
        for f in range(v.shape[0]):
            c = coupling[:, f, g] if transpose else coupling[:, g, f]
            term = c[:, None, None] * v[f]
            acc = term if acc is None else acc + term
        out.append(acc)
    return jnp.stack(out)


def edge_halos(first_col, last_col, first_row, last_row, flip):
    n_lon = lax.axis_size("lon")
    n_lat = lax.axis_size("lat")
    lon_i = lax.axis_index("lon")
    lat_j = lax.axis_index("lat")
    up = [(i, (i + 1) % n_lon) for i in range(n_lon)]
    down = [(b, a) for a, b in up]
    from_west = lax.ppermute(last_col, "lon", up)
    from_east = lax.ppermute(first_col, "lon", down)
    low = lon_i < n_lon // 2
    cw_pairs = ring_pairs(n_lon, n_lat)
    ccw_pairs = [(b, a) for a, b in cw_pairs]
    cw = lax.ppermute(jnp.where(low, last_row, first_row), ("lon", "lat"), cw_pairs)
    ccw = lax.ppermute(jnp.where(low, first_row, last_row), ("lon", "lat"), ccw_pairs)
    north_row = jnp.where(low, cw, ccw)
    south_row = jnp.where(low, ccw, cw)
    north_row = jnp.where(lat_j == 0, flip * north_row, north_row)
    south_row = jnp.where(lat_j == n_lat - 1, flip * south_row, south_row)
    return (north_row[..., None], south_row[..., None], from_west[:, :, None, :], from_east[:, :, None, :])


def neighbours_2d(v, hn, hs, hw, he):
    c_n, r_n = v.shape
    rows = lax.broadcasted_iota(jnp.int32, v.shape, 1)
    cols = lax.broadcasted_iota(jnp.int32, v.shape, 0)
    north = jnp.where(rows == 0, hn, pltpu.roll(v, 1, 1))
    south = jnp.where(rows == r_n - 1, hs, pltpu.roll(v, r_n - 1, 1))
    west = jnp.where(cols == 0, hw, pltpu.roll(v, 1, 0))
    east = jnp.where(cols == c_n - 1, he, pltpu.roll(v, c_n - 1, 0))
    return north, south, west, east


def write_edges(v, f, l, fc, lc, fr, lr):
    fc[f, l] = v[0:1, :]
    lc[f, l] = v[-1:, :]
    fr[f, l] = v[:, 0:1]
    lr[f, l] = v[:, -1:]


def forward_kernel(cpl, x_ref, c_ref, hn, hs, hw, he, xn_ref, d_ref, fc, lc, fr, lr):
    nf = x_ref.shape[0]

    def body(l, carry):
        xs = [x_ref[f, l] for f in range(nf)]
        cs = [c_ref[d, l] for d in range(4)]
        total = cs[0] + cs[1] + cs[2] + cs[3]
        for g in range(nf):
            v = xs[g]
            north, south, west, east = neighbours_2d(v, hn[g, l], hs[g, l], hw[g, l], he[g, l])
            mixed = cpl[l * nf * nf + g * nf] * xs[0]
            for f in range(1, nf):
                mixed = mixed + cpl[l * nf * nf + g * nf + f] * xs[f]
            y = v + cs[0] * north + cs[1] * south + cs[2] * west + cs[3] * east - total * v + 0.25 * mixed
            t = jnp.tanh(y)
            xn = y - 0.5 * t
            xn_ref[g, l] = xn
            d_ref[g, l] = 1.0 - 0.5 * (1.0 - t * t)
            write_edges(xn, g, l, fc, lc, fr, lr)
        return carry

    lax.fori_loop(0, x_ref.shape[1], body, 0)


def backward_kernel(cpl, ly_ref, c_ref, b_ref, dp_ref, hn, hs, hw, he, out_ref, fc, lc, fr, lr, *, last):
    nf = ly_ref.shape[0]

    def body(l, carry):
        ls = [ly_ref[f, l] for f in range(nf)]
        cs = [c_ref[d, l] for d in range(4)]
        total = cs[0] + cs[1] + cs[2] + cs[3]
        bs = [b_ref[d, l] for d in range(4)]
        for o in range(nf):
            v = ls[o]
            north, south, west, east = neighbours_2d(v, hn[o, l], hs[o, l], hw[o, l], he[o, l])
            back = cpl[l * nf * nf + o] * ls[0]
            for g in range(1, nf):
                back = back + cpl[l * nf * nf + g * nf + o] * ls[g]
            lam = v - total * v + 0.25 * back + bs[0] * north + bs[1] * south + bs[2] * west + bs[3] * east
            if last:
                out_ref[o, l] = lam
            else:
                nxt = lam * dp_ref[o, l]
                out_ref[o, l] = nxt
                write_edges(nxt, o, l, fc, lc, fr, lr)
        return carry

    lax.fori_loop(0, ly_ref.shape[1], body, 0)


def edge_shapes(x):
    f, l, c, r = x.shape
    return [
        jax.ShapeDtypeStruct((f, l, 1, r), x.dtype),
        jax.ShapeDtypeStruct((f, l, 1, r), x.dtype),
        jax.ShapeDtypeStruct((f, l, c, 1), x.dtype),
        jax.ShapeDtypeStruct((f, l, c, 1), x.dtype),
    ]


def vmem_specs(n):
    return [pl.BlockSpec(memory_space=pltpu.VMEM) for _ in range(n)]


def forward_step(cpl, x, coef, halo):
    outs = [jax.ShapeDtypeStruct(x.shape, x.dtype)] * 2 + edge_shapes(x)
    return pl.pallas_call(
        forward_kernel,
        out_shape=outs,
        in_specs=[pl.BlockSpec(memory_space=pltpu.SMEM)] + vmem_specs(6),
        out_specs=vmem_specs(6),
    )(cpl, x, coef, *halo)


def backward_step(cpl, ly, coef, back_coef, dprev, halo, last):
    outs = [jax.ShapeDtypeStruct(ly.shape, ly.dtype)] + edge_shapes(ly)
    return pl.pallas_call(
        lambda *refs: backward_kernel(*refs, last=last),
        out_shape=outs,
        in_specs=[pl.BlockSpec(memory_space=pltpu.SMEM)] + vmem_specs(8),
        out_specs=vmem_specs(5),
    )(cpl, ly, coef, back_coef, dprev, *halo)


def edges_of(x):
    return (x[:, :, 0, :], x[:, :, -1, :], x[:, :, :, 0], x[:, :, :, -1])


def squeezed(edges):
    fc, lc, fr, lr = edges
    return (fc[:, :, 0, :], lc[:, :, 0, :], fr[..., 0], lr[..., 0])


def on_device(
    initial_state, coefficients, coupling, obs_band, obs_cell, obs_value, obs_weight, obs_count
):
    wind_flip = jnp.array([-1.0, -1.0, 1.0, 1.0], dtype=jnp.float32).reshape(4, 1, 1)
    plain_flip = jnp.ones((4, 1, 1), jnp.float32)
    cpl = coupling.reshape(-1)
    factors = []
    x = initial_state
    edges = edges_of(x)
    for step in range(STEPS):
        x, dfac, *kernel_edges = forward_step(cpl, x, coefficients, edge_halos(*edges, wind_flip))
        factors.append(dfac)
        edges = squeezed(kernel_edges)

    n_lon = lax.axis_size("lon")
    rows = obs_cell.shape[1]
    band = obs_band[0, :, 0]
    valid = jnp.arange(rows, dtype=jnp.int32) < obs_count[0, 0]
    weight = jnp.where(valid, obs_weight[0], 0.0)
    ids = jnp.arange(rows, dtype=jnp.int32)
    same = (band[:, None] == band[None, :]) & (ids[None, :] < ids[:, None])
    rank = jnp.sum(same.astype(jnp.int32), axis=1)
    slot = band * CAP + rank
    payload = jnp.stack([obs_value[0], weight, obs_cell[0].astype(jnp.float32)], axis=1)
    slots = jnp.arange(n_lon * CAP, dtype=jnp.int32)
    hit = slot[None, :] == slots[:, None]
    send = jnp.sum(jnp.where(hit[:, :, None], payload[None, :, :], 0.0), axis=1)
    arrived = lax.all_to_all(send, "lon", 0, 0, tiled=True)
    values = arrived[:, 0]
    weights = arrived[:, 1]
    cells = arrived[:, 2].astype(jnp.int32)
    lanes = x.shape[3]
    row_of = cells // lanes
    lane_of = cells % lanes
    table = x.reshape(-1, lanes)
    lane_hit = lane_of[:, None] == jnp.arange(lanes, dtype=jnp.int32)[None, :]
    picked = jnp.sum(jnp.where(lane_hit, table[row_of], 0.0), axis=1)
    forcing = weights * (picked - values)
    spread = jnp.where(lane_hit, forcing[:, None], 0.0)
    lam = jnp.zeros_like(table).at[row_of].add(spread).reshape(x.shape)

    near_n, near_s, near_w, near_e = shifted(coefficients, halos(coefficients, plain_flip))
    row_ids = jnp.arange(coefficients.shape[3], dtype=jnp.int32)[None, :]
    polar_top = (lax.axis_index("lat") == 0) & (row_ids == 0)
    polar_bottom = (lax.axis_index("lat") == lax.axis_size("lat") - 1) & (
        row_ids == coefficients.shape[3] - 1
    )
    back_coef = jnp.stack([
        jnp.where(polar_top, near_n[0], near_n[1]),
        jnp.where(polar_bottom, near_s[1], near_s[0]),
        near_w[3],
        near_e[2],
    ])
    lam_y = lam * factors[STEPS - 1]
    edges = edges_of(lam_y)
    for step in range(STEPS - 1, -1, -1):
        last = step == 0
        dprev = factors[step - 1] if not last else factors[0]
        lam_y, *kernel_edges = backward_step(
            cpl, lam_y, coefficients, back_coef, dprev, edge_halos(*edges, wind_flip), last
        )
        edges = squeezed(kernel_edges)
    return (x, lam_y)


def solution(mesh):
    in_specs = (
        P(None, None, "lon", "lat"),
        P(None, None, "lon", "lat"),
        P(),
        P("lat", "lon", None),
        P("lat", "lon"),
        P("lat", "lon"),
        P("lat", "lon"),
        P("lat", "lon"),
    )
    out_specs = (P(None, None, "lon", "lat"), P(None, None, "lon", "lat"))
    return jax.shard_map(
        on_device, mesh=mesh, in_specs=in_specs, out_specs=out_specs, check_vma=False
    )
```

profile of v0, /device:TPU:0, one launch (start us, length us, event | category | flops | bytes accessed | tf_op | source)
XLA Modules:
  0.0 172.4 jit_solution(13228474693447710987)
XLA Ops:
  0.6 1.9 %slice_select_fusion.4 = (f32[4,32,16,1]{3,2,1,0:T(8,128)S(1)}, f32[4,32,16,1]{3,2,1,0:T(8,128)S(1)}) fusion(f32[4,32,16,128]{3,2,1,0:T(8,128)} %x_ref.1, pred[]{:T(512)S(6)} %lt.44), kind=kLoop, calls=%fused_computation.23 | loop fusion | flops 4096 | bytes 32769 | tf_op jit(solution)/shard_map/jit(_where)/select_n | solution.py:80
  3.6 3.6 %collective-permute-start.1 = (f32[4,32,16]{1,2,0:T(8,128)S(1)}, f32[4,32,16]{1,2,0:T(8,128)S(1)}, u32[]{:S(2)}, u32[]{:S(2)}) collective-permute-start(f32[4,32,16]{1,2,0:T(8,128)S(1)} %bitcast.91), channel_id=1, source_target_pairs={{1,0},{2,1},{3,2},{131,3},{130,131},{129,130},{128,129},{0,128},{5... | collective-permute-start | bytes 24584 | tf_op jit(solution)/shard_map/ppermute | solution.py:80
  8.7 3.6 %collective-permute-start.9 = (f32[4,32,16]{1,2,0:T(8,128)S(1)}, f32[4,32,16]{1,2,0:T(8,128)S(1)}, u32[]{:S(2)}, u32[]{:S(2)}) collective-permute-start(f32[4,32,16]{1,2,0:T(8,128)S(1)} %bitcast.90), channel_id=1, source_target_pairs={{1,0},{2,1},{3,2},{131,3},{130,131},{129,130},{128,129},{0,128},{5... | collective-permute-start | bytes 24584 | tf_op jit(solution)/shard_map/ppermute | solution.py:38
  12.2 1.9 %fusion.25 = (f32[4,32,1,128]{3,2,1,0:T(1,128)}, f32[4,32,1,128]{3,2,1,0:T(1,128)}) fusion(f32[4,32,16,128]{3,2,1,0:T(8,128)} %x_ref.1), kind=kLoop, calls=%fused_computation.74 | loop fusion | bytes 262144 | tf_op jit(solution)/shard_map/slice | solution.py:191
  17.3 1.9 %select_reduce_fusion = f32[2048,3]{0,1:T(4,128)S(1)} fusion(f32[512,3]{0,1:T(4,128)S(1)} %pad_maximum_fusion.2, pred[2048,512]{1,0:T(8,128)(4,1)S(1)} %iota_compare_fusion), kind=kLoop, calls=%fused_computation.2 | loop fusion | flops 6285312 | bytes 1079296 | tf_op jit(solution)/shard_map/reduce_sum | solution.py:225
  20.0 10.9 %all-to-all-start = ((f32[64,32,3]{1,2,0:T(4,128)}), f32[64,32,3]{1,2,0:T(4,128)S(1)}, u32[]{:S(2)}, u32[]{:S(2)}) async-start(f32[64,32,3]{1,2,0:T(4,128)} %copy.863), calls=%async_computation | async-start | bytes 262144 | tf_op jit(solution)/shard_map/all_to_all | solution.py:226
  32.2 1.5 fusion.24
  35.3 7.6 %collective-permute-start.3 = (f32[4,32,128]{2,1,0:T(8,128)}, f32[4,32,128]{2,1,0:T(8,128)}, u32[]{:S(2)}, u32[]{:S(2)}) collective-permute-start(f32[4,32,128]{2,1,0:T(8,128)} %bitcast.6), channel_id=1, source_target_pairs={{4,0},{8,4},{12,8},{16,12},{20,16},{24,20},{28,24},{32,28},{36,32}... | collective-permute-start | bytes 196616 | tf_op jit(solution)/shard_map/ppermute | solution.py:75
  42.9 7.7 %collective-permute-start.11 = (f32[4,32,128]{2,1,0:T(8,128)}, f32[4,32,128]{2,1,0:T(8,128)}, u32[]{:S(2)}, u32[]{:S(2)}) collective-permute-start(f32[4,32,128]{2,1,0:T(8,128)} %bitcast.33), channel_id=1, source_target_pairs={{4,0},{8,4},{12,8},{16,12},{20,16},{24,20},{28,24},{32,28},{36,32}... | collective-permute-start | bytes 196616 | tf_op jit(solution)/shard_map/ppermute | solution.py:31
  54.6 1.4 copy.857.hn
  56.1 1.4 copy.858.hs
  58.3 10.0 %shard_map.104 = (f32[4,32,16,128]{3,2,1,0:T(8,128)}, f32[4,32,16,128]{3,2,1,0:T(8,128)}, f32[4,32,1,128]{3,2,1,0:T(1,128)}, f32[4,32,1,128]{3,2,1,0:T(1,128)}, ...) custom-call(f32[512]{0:T(512)} %reshape.106.cpl.refs_0_, f32[4,32,16,128]{3,2,1,0:T(8,128)} %x_ref.1, ...), custom_call_target="tpu_custom_call" | custom-call | tf_op jit(solution)/shard_map/pallas_call | solution.py:172
  68.3 1.7 %broadcast_select_fusion.2 = (f32[4,32,16,1]{3,2,1,0:T(8,128)S(1)}, f32[4,32,16,1]{3,2,1,0:T(8,128)S(1)}) fusion(f32[4,32,16,1]{3,2,1,0:T(8,128)} %get-tuple-element.18, f32[4,32,16,1]{3,2,1,0:T(8,128)} %get-tuple-element.17, pred[]{:T(512)S(6)} %lt.44), kind=kLoop, calls=%fused_computation.30 | loop fusion | flops 4096 | bytes 32769 | tf_op jit(solution)/shard_map/jit(_where)/select_n | solution.py:80
  71.2 3.6 %collective-permute-start.5 = (f32[4,32,16]{1,2,0:T(8,128)S(1)}, f32[4,32,16]{1,2,0:T(8,128)S(1)}, u32[]{:S(2)}, u32[]{:S(2)}) collective-permute-start(f32[4,32,16]{1,2,0:T(8,128)S(1)} %bitcast.95), channel_id=1, source_target_pairs={{1,0},{2,1},{3,2},{131,3},{130,131},{129,130},{128,129},{0,128},{5... | collective-permute-start | bytes 24584 | tf_op jit(solution)/shard_map/ppermute | solution.py:80
  74.8 7.7 %collective-permute-start.7 = (f32[4,32,128]{2,1,0:T(8,128)}, f32[4,32,128]{2,1,0:T(8,128)S(1)}, u32[]{:S(2)}, u32[]{:S(2)}) collective-permute-start(f32[4,32,128]{2,1,0:T(8,128)} %bitcast.105), channel_id=1, source_target_pairs={{4,0},{8,4},{12,8},{16,12},{20,16},{24,20},{28,24},{32,28},{36,32}... | collective-permute-start | bytes 196616 | tf_op jit(solution)/shard_map/ppermute | solution.py:75
  82.5 2.1 %fusion.refs_3_ = f32[4,32,16,128]{3,2,1,0:T(8,128)} fusion(f32[4,32,1,128]{3,2,1,0:T(1,128)} %bitcast.34, f32[4,32,15,128]{3,2,1,0:T(8,128)S(1)} %copy-done.3, f32[4,32,15,128]{3,2,1,0:T(8,128)S(1)} %copy-done.2, f32[4,32,1,128]{3,2,1,0:T(1,128)} %bitcast.32, f32[1,32,16,128]{3,2,1,0:T(8,128)S(1)} %fusion.10, f32[1,32,16,128]{3,2,1,0:T(8,128)} %fusion.11), kind=kLoop, calls=%fused_computation.7 | loop fusion | flops 3407872 | bytes 3670016 | tf_op jit(solution)/shard_map/stack | solution.py:246
  84.7 1.4 copy.861.hn
  86.2 1.4 copy.862.hs
  88.3 10.1 %shard_map.105 = (f32[4,32,16,128]{3,2,1,0:T(8,128)}, f32[4,32,16,128]{3,2,1,0:T(8,128)}, f32[4,32,1,128]{3,2,1,0:T(1,128)}, f32[4,32,1,128]{3,2,1,0:T(1,128)}, ...) custom-call(f32[512]{0:T(512)} %reshape.106.cpl.refs_0_, f32[4,32,16,128]{3,2,1,0:T(8,128)} %get-tuple-element.16.x_ref, ...), custom_call_target="tpu_custom_call" | custom-call | tf_op jit(solution)/shard_map/pallas_call | solution.py:172
  98.3 6.7 %gather_fusion = f32[2048,128]{1,0:T(8,128)S(1)} fusion(f32[2048,128]{1,0:T(8,128)} %bitcast.76, s32[2048]{0:T(1024)S(1)} %copy-done.13), kind=kCustom, calls=%fused_computation | custom fusion | bytes 2105344 | tf_op jit(solution)/shard_map/gather | solution.py:235
  105.7 14.2 %scatter_custom_fusion = f32[2048,128]{1,0:T(8,128)S(1)} fusion(s32[2048]{0:T(1024)S(1)} %bitcast.101, f32[2048]{0:T(1024)S(1)} %bitcast.88, s32[2048]{0:T(1024)S(1)} %bitcast.79, f32[]{:T(128)} %constant.46.clone.1), kind=kCustom, calls=%fused_computation.14 | custom fusion | flops 786432 | bytes 1065984 | tf_op jit(solution)/shard_map/scatter-add | solution.py:238
  121.5 3.6 %collective-permute-start.13 = (f32[4,32,16]{1,2,0:T(8,128)S(1)}, f32[4,32,16]{1,2,0:T(8,128)S(1)}, u32[]{:S(2)}, u32[]{:S(2)}) collective-permute-start(f32[4,32,16]{1,2,0:T(8,128)S(1)} %bitcast.97), channel_id=1, source_target_pairs={{1,0},{2,1},{3,2},{131,3},{130,131},{129,130},{128,129},{0,128},{5... | collective-permute-start | bytes 24584 | tf_op jit(solution)/shard_map/ppermute | solution.py:80
  125.3 7.7 %collective-permute-start.15 = (f32[4,32,128]{2,1,0:T(8,128)S(1)}, f32[4,32,128]{2,1,0:T(8,128)S(1)}, u32[]{:S(2)}, u32[]{:S(2)}) collective-permute-start(f32[4,32,128]{2,1,0:T(8,128)S(1)} %bitcast.86), channel_id=1, source_target_pairs={{4,0},{8,4},{12,8},{16,12},{20,16},{24,20},{28,24},{32,28},{36,32}... | collective-permute-start | bytes 196616 | tf_op jit(solution)/shard_map/ppermute | solution.py:75
  133.1 1.5 copy.873.refs_5_
  134.6 1.5 copy.874.refs_6_
  136.7 10.0 %shard_map.106 = (f32[4,32,16,128]{3,2,1,0:T(8,128)}, f32[4,32,1,128]{3,2,1,0:T(1,128)}, f32[4,32,1,128]{3,2,1,0:T(1,128)}, f32[4,32,16,1]{3,2,1,0:T(8,128)}, f32[4,32,16,1]{3,2,1,0:T(8,128)}) custom-call(f32[512]{0:T(512)} %reshape.106.cpl.refs_0_, f32[4,32,16,128]{3,2,1,0:T(8,128)} %copy-done.1, f32[4,32,16,128]{3,2,1,0:T(8,128)} %refs_2_.3, ...), custom_call_target="tpu_custom_call" | custom-call | tf_op jit(solution)/shard_map/pallas_call | solution.py:182
  146.7 1.7 %broadcast_select_fusion = (f32[4,32,16,1]{3,2,1,0:T(8,128)S(1)}, f32[4,32,16,1]{3,2,1,0:T(8,128)S(1)}) fusion(f32[4,32,16,1]{3,2,1,0:T(8,128)} %get-tuple-element.26, f32[4,32,16,1]{3,2,1,0:T(8,128)} %get-tuple-element.25, pred[]{:T(512)S(6)} %lt.44), kind=kLoop, calls=%fused_computation.28 | loop fusion | flops 4096 | bytes 32769 | tf_op jit(solution)/shard_map/jit(_where)/select_n | solution.py:80
  149.5 3.6 %collective-permute-start.17 = (f32[4,32,16]{1,2,0:T(8,128)S(1)}, f32[4,32,16]{1,2,0:T(8,128)S(1)}, u32[]{:S(2)}, u32[]{:S(2)}) collective-permute-start(f32[4,32,16]{1,2,0:T(8,128)S(1)} %bitcast.99), channel_id=1, source_target_pairs={{1,0},{2,1},{3,2},{131,3},{130,131},{129,130},{128,129},{0,128},{5... | collective-permute-start | bytes 24584 | tf_op jit(solution)/shard_map/ppermute | solution.py:80
  153.1 7.7 %collective-permute-start.19 = (f32[4,32,128]{2,1,0:T(8,128)S(1)}, f32[4,32,128]{2,1,0:T(8,128)S(1)}, u32[]{:S(2)}, u32[]{:S(2)}) collective-permute-start(f32[4,32,128]{2,1,0:T(8,128)S(1)} %bitcast.107), channel_id=1, source_target_pairs={{4,0},{8,4},{12,8},{16,12},{20,16},{24,20},{28,24},{32,28},{36,32}... | collective-permute-start | bytes 196616 | tf_op jit(solution)/shard_map/ppermute | solution.py:75
  161.0 1.5 copy.877.refs_5_
  162.4 1.5 copy.878.refs_6_
  164.5 7.9 %shard_map.107 = (f32[4,32,16,128]{3,2,1,0:T(8,128)}, f32[4,32,1,128]{3,2,1,0:T(1,128)}, f32[4,32,1,128]{3,2,1,0:T(1,128)}, f32[4,32,16,1]{3,2,1,0:T(8,128)}, f32[4,32,16,1]{3,2,1,0:T(8,128)}) custom-call(f32[512]{0:T(512)} %reshape.106.cpl.refs_0_, f32[4,32,16,128]{3,2,1,0:T(8,128)} %get-tuple-element.24.refs_1_, f32[4,32,16,128]{3,2,1,0:T(8,128)} %refs_2_.3, ...), custom_call_target="tpu_custom_call" | custom-call | tf_op jit(solution)/shard_map/pallas_call | solution.py:182
  (122 shorter events, 20.2 us)
Async XLA Ops:
  3.0 32.3 %collective-permute-start = (f32[4,32,16]{1,2,0:T(8,128)S(1)}, f32[4,32,16]{1,2,0:T(8,128)S(1)}, u32[]{:S(2)}, u32[]{:S(2)}) collective-permute-start(f32[4,32,16]{1,2,0:T(8,128)S(1)} %bitcast.93), channel_id=1, source_target_pairs={{0,1},{1,2},{2,3},{3,131},{131,130},{130,129},{129,128},{128,0},{4... | collective-permute-start | bytes 24584 | tf_op jit(solution)/shard_map/ppermute | solution.py:79
  3.6 39.3 %collective-permute-start.1 = (f32[4,32,16]{1,2,0:T(8,128)S(1)}, f32[4,32,16]{1,2,0:T(8,128)S(1)}, u32[]{:S(2)}, u32[]{:S(2)}) collective-permute-start(f32[4,32,16]{1,2,0:T(8,128)S(1)} %bitcast.91), channel_id=1, source_target_pairs={{1,0},{2,1},{3,2},{131,3},{130,131},{129,130},{128,129},{0,128},{5... | collective-permute-start | bytes 24584 | tf_op jit(solution)/shard_map/ppermute | solution.py:80
  7.5 7.9 %copy-start.14 = (s32[1,512,1]{1,2,0:T(1,128)S(1)}, s32[1,512,1]{1,2,0:T(1,128)}, u32[]{:S(2)}) copy-start(s32[1,512,1]{1,2,0:T(1,128)} %param.12) | copy-start | bytes 6148
  8.1 34.9 %collective-permute-start.8 = (f32[4,32,16]{1,2,0:T(8,128)S(1)}, f32[4,32,16]{1,2,0:T(8,128)S(1)}, u32[]{:S(2)}, u32[]{:S(2)}) collective-permute-start(f32[4,32,16]{1,2,0:T(8,128)S(1)} %bitcast.92), channel_id=1, source_target_pairs={{0,1},{1,2},{2,3},{3,131},{131,130},{130,129},{129,128},{128,0},{4... | collective-permute-start | bytes 24584 | tf_op jit(solution)/shard_map/ppermute | solution.py:37
  8.1 9.1 %copy-start.20 = (s32[1,512]{1,0:T(1,128)S(1)}, s32[1,512]{1,0:T(1,128)}, u32[]{:S(2)}) copy-start(s32[1,512]{1,0:T(1,128)} %param.13) | copy-start | bytes 6148
  8.1 9.1 %copy-start.21 = (f32[1,512]{1,0:T(1,128)S(1)}, f32[1,512]{1,0:T(1,128)}, u32[]{:S(2)}) copy-start(f32[1,512]{1,0:T(1,128)} %param.15) | copy-start | bytes 6148
  8.2 9.1 %copy-start.19 = (f32[1,512]{1,0:T(1,128)S(1)}, f32[1,512]{1,0:T(1,128)}, u32[]{:S(2)}) copy-start(f32[1,512]{1,0:T(1,128)} %param.14) | copy-start | bytes 6148
  8.7 42.0 %collective-permute-start.9 = (f32[4,32,16]{1,2,0:T(8,128)S(1)}, f32[4,32,16]{1,2,0:T(8,128)S(1)}, u32[]{:S(2)}, u32[]{:S(2)}) collective-permute-start(f32[4,32,16]{1,2,0:T(8,128)S(1)} %bitcast.90), channel_id=1, source_target_pairs={{1,0},{2,1},{3,2},{131,3},{130,131},{129,130},{128,129},{0,128},{5... | collective-permute-start | bytes 24584 | tf_op jit(solution)/shard_map/ppermute | solution.py:38
  14.2 44.1 %collective-permute-start.2 = (f32[4,32,128]{2,1,0:T(8,128)}, f32[4,32,128]{2,1,0:T(8,128)}, u32[]{:S(2)}, u32[]{:S(2)}) collective-permute-start(f32[4,32,128]{2,1,0:T(8,128)} %bitcast.4), channel_id=1, source_target_pairs={{0,4},{4,8},{8,12},{12,16},{16,20},{20,24},{24,28},{28,32},{32,36}... | collective-permute-start | bytes 196616 | tf_op jit(solution)/shard_map/ppermute | solution.py:74
  20.0 37.5 %all-to-all-start = ((f32[64,32,3]{1,2,0:T(4,128)}), f32[64,32,3]{1,2,0:T(4,128)S(1)}, u32[]{:S(2)}, u32[]{:S(2)}) async-start(f32[64,32,3]{1,2,0:T(4,128)} %copy.863), calls=%async_computation | async-start | bytes 262144 | tf_op jit(solution)/shard_map/all_to_all | solution.py:226
  32.2 18.4 %copy-start.15 = (f32[4]{0:T(128)S(1)}, f32[4]{0:T(128)}, u32[]{:S(2)}) copy-start(f32[4]{0:T(128)} %constant.53.clone) | copy-start | bytes 52
  35.3 23.0 %collective-permute-start.3 = (f32[4,32,128]{2,1,0:T(8,128)}, f32[4,32,128]{2,1,0:T(8,128)}, u32[]{:S(2)}, u32[]{:S(2)}) collective-permute-start(f32[4,32,128]{2,1,0:T(8,128)} %bitcast.6), channel_id=1, source_target_pairs={{4,0},{8,4},{12,8},{16,12},{20,16},{24,20},{28,24},{32,28},{36,32}... | collective-permute-start | bytes 196616 | tf_op jit(solution)/shard_map/ppermute | solution.py:75
  42.9 31.9 %collective-permute-start.10 = (f32[4,32,128]{2,1,0:T(8,128)}, f32[4,32,128]{2,1,0:T(8,128)}, u32[]{:S(2)}, u32[]{:S(2)}) collective-permute-start(f32[4,32,128]{2,1,0:T(8,128)} %bitcast.31), channel_id=1, source_target_pairs={{0,4},{4,8},{8,12},{12,16},{16,20},{20,24},{24,28},{28,32},{32,36}... | collective-permute-start | bytes 196616 | tf_op jit(solution)/shard_map/ppermute | solution.py:30
  42.9 39.6 %collective-permute-start.11 = (f32[4,32,128]{2,1,0:T(8,128)}, f32[4,32,128]{2,1,0:T(8,128)}, u32[]{:S(2)}, u32[]{:S(2)}) collective-permute-start(f32[4,32,128]{2,1,0:T(8,128)} %bitcast.33), channel_id=1, source_target_pairs={{4,0},{8,4},{12,8},{16,12},{20,16},{24,20},{28,24},{32,28},{36,32}... | collective-permute-start | bytes 196616 | tf_op jit(solution)/shard_map/ppermute | solution.py:31
  70.1 12.4 %copy-start.2 = (f32[4,32,15,128]{3,2,1,0:T(8,128)S(1)}, f32[4,32,15,128]{3,2,1,0:T(8,128)}, u32[]{:S(2)}) copy-start(f32[4,32,15,128]{3,2,1,0:T(8,128)} %get-tuple-element.46) | copy-start | bytes 2949124
  70.6 11.9 %copy-start.3 = (f32[4,32,15,128]{3,2,1,0:T(8,128)S(1)}, f32[4,32,15,128]{3,2,1,0:T(8,128)}, u32[]{:S(2)}) copy-start(f32[4,32,15,128]{3,2,1,0:T(8,128)} %get-tuple-element.47) | copy-start | bytes 2949124
  70.6 14.1 %collective-permute-start.4 = (f32[4,32,16]{1,2,0:T(8,128)S(1)}, f32[4,32,16]{1,2,0:T(8,128)S(1)}, u32[]{:S(2)}, u32[]{:S(2)}) collective-permute-start(f32[4,32,16]{1,2,0:T(8,128)S(1)} %bitcast.94), channel_id=1, source_target_pairs={{0,1},{1,2},{2,3},{3,131},{131,130},{130,129},{129,128},{128,0},{4... | collective-permute-start | bytes 24584 | tf_op jit(solution)/shard_map/ppermute | solution.py:79
  71.2 13.5 %collective-permute-start.5 = (f32[4,32,16]{1,2,0:T(8,128)S(1)}, f32[4,32,16]{1,2,0:T(8,128)S(1)}, u32[]{:S(2)}, u32[]{:S(2)}) collective-permute-start(f32[4,32,16]{1,2,0:T(8,128)S(1)} %bitcast.95), channel_id=1, source_target_pairs={{1,0},{2,1},{3,2},{131,3},{130,131},{129,130},{128,129},{0,128},{5... | collective-permute-start | bytes 24584 | tf_op jit(solution)/shard_map/ppermute | solution.py:80
  74.8 12.8 %collective-permute-start.6 = (f32[4,32,128]{2,1,0:T(8,128)}, f32[4,32,128]{2,1,0:T(8,128)S(1)}, u32[]{:S(2)}, u32[]{:S(2)}) collective-permute-start(f32[4,32,128]{2,1,0:T(8,128)} %bitcast.106), channel_id=1, source_target_pairs={{0,4},{4,8},{8,12},{12,16},{16,20},{20,24},{24,28},{28,32},{32,36}... | collective-permute-start | bytes 196616 | tf_op jit(solution)/shard_map/ppermute | solution.py:74
  74.8 12.8 %collective-permute-start.7 = (f32[4,32,128]{2,1,0:T(8,128)}, f32[4,32,128]{2,1,0:T(8,128)S(1)}, u32[]{:S(2)}, u32[]{:S(2)}) collective-permute-start(f32[4,32,128]{2,1,0:T(8,128)} %bitcast.105), channel_id=1, source_target_pairs={{4,0},{8,4},{12,8},{16,12},{20,16},{24,20},{28,24},{32,28},{36,32}... | collective-permute-start | bytes 196616 | tf_op jit(solution)/shard_map/ppermute | solution.py:75
  88.3 10.1 %copy-start.13 = (s32[2048]{0:T(1024)S(1)}, s32[2048]{0:T(1024)}, u32[]{:S(2)}) copy-start(s32[2048]{0:T(1024)} %broadcast_clamp_fusion) | copy-start | bytes 24580
  105.0 14.9 %copy-start.4 = (f32[4,32,16,128]{3,2,1,0:T(8,128)S(1)}, f32[4,32,16,128]{3,2,1,0:T(8,128)}, u32[]{:S(2)}) copy-start(f32[4,32,16,128]{3,2,1,0:T(8,128)} %get-tuple-element.22) | copy-start | bytes 3145732
  120.1 5.0 %copy-start.1 = (f32[4,32,16,128]{3,2,1,0:T(8,128)}, f32[4,32,16,128]{3,2,1,0:T(8,128)S(1)}, u32[]{:S(2)}) copy-start(f32[4,32,16,128]{3,2,1,0:T(8,128)S(1)} %mul.75.refs_1_) | copy-start | bytes 3145732
  120.5 12.6 %copy-start.17 = (f32[4]{0:T(128)S(1)}, f32[4]{0:T(128)}, u32[]{:S(2)}) copy-start(f32[4]{0:T(128)} %constant.53.clone) | copy-start | bytes 52
  121.0 12.1 %collective-permute-start.12 = (f32[4,32,16]{1,2,0:T(8,128)S(1)}, f32[4,32,16]{1,2,0:T(8,128)S(1)}, u32[]{:S(2)}, u32[]{:S(2)}) collective-permute-start(f32[4,32,16]{1,2,0:T(8,128)S(1)} %bitcast.96), channel_id=1, source_target_pairs={{0,1},{1,2},{2,3},{3,131},{131,130},{130,129},{129,128},{128,0},{4... | collective-permute-start | bytes 24584 | tf_op jit(solution)/shard_map/ppermute | solution.py:79
  121.5 11.5 %collective-permute-start.13 = (f32[4,32,16]{1,2,0:T(8,128)S(1)}, f32[4,32,16]{1,2,0:T(8,128)S(1)}, u32[]{:S(2)}, u32[]{:S(2)}) collective-permute-start(f32[4,32,16]{1,2,0:T(8,128)S(1)} %bitcast.97), channel_id=1, source_target_pairs={{1,0},{2,1},{3,2},{131,3},{130,131},{129,130},{128,129},{0,128},{5... | collective-permute-start | bytes 24584 | tf_op jit(solution)/shard_map/ppermute | solution.py:80
  125.2 10.8 %collective-permute-start.14 = (f32[4,32,128]{2,1,0:T(8,128)S(1)}, f32[4,32,128]{2,1,0:T(8,128)S(1)}, u32[]{:S(2)}, u32[]{:S(2)}) collective-permute-start(f32[4,32,128]{2,1,0:T(8,128)S(1)} %bitcast.87), channel_id=1, source_target_pairs={{0,4},{4,8},{8,12},{12,16},{16,20},{20,24},{24,28},{28,32},{32,36}... | collective-permute-start | bytes 196616 | tf_op jit(solution)/shard_map/ppermute | solution.py:74
  125.3 10.7 %collective-permute-start.15 = (f32[4,32,128]{2,1,0:T(8,128)S(1)}, f32[4,32,128]{2,1,0:T(8,128)S(1)}, u32[]{:S(2)}, u32[]{:S(2)}) collective-permute-start(f32[4,32,128]{2,1,0:T(8,128)S(1)} %bitcast.86), channel_id=1, source_target_pairs={{4,0},{8,4},{12,8},{16,12},{20,16},{24,20},{28,24},{32,28},{36,32}... | collective-permute-start | bytes 196616 | tf_op jit(solution)/shard_map/ppermute | solution.py:75
  149.0 11.9 %collective-permute-start.16 = (f32[4,32,16]{1,2,0:T(8,128)S(1)}, f32[4,32,16]{1,2,0:T(8,128)S(1)}, u32[]{:S(2)}, u32[]{:S(2)}) collective-permute-start(f32[4,32,16]{1,2,0:T(8,128)S(1)} %bitcast.98), channel_id=1, source_target_pairs={{0,1},{1,2},{2,3},{3,131},{131,130},{130,129},{129,128},{128,0},{4... | collective-permute-start | bytes 24584 | tf_op jit(solution)/shard_map/ppermute | solution.py:79
  149.5 11.3 %collective-permute-start.17 = (f32[4,32,16]{1,2,0:T(8,128)S(1)}, f32[4,32,16]{1,2,0:T(8,128)S(1)}, u32[]{:S(2)}, u32[]{:S(2)}) collective-permute-start(f32[4,32,16]{1,2,0:T(8,128)S(1)} %bitcast.99), channel_id=1, source_target_pairs={{1,0},{2,1},{3,2},{131,3},{130,131},{129,130},{128,129},{0,128},{5... | collective-permute-start | bytes 24584 | tf_op jit(solution)/shard_map/ppermute | solution.py:80
  153.1 10.8 %collective-permute-start.18 = (f32[4,32,128]{2,1,0:T(8,128)S(1)}, f32[4,32,128]{2,1,0:T(8,128)S(1)}, u32[]{:S(2)}, u32[]{:S(2)}) collective-permute-start(f32[4,32,128]{2,1,0:T(8,128)S(1)} %bitcast.108), channel_id=1, source_target_pairs={{0,4},{4,8},{8,12},{12,16},{16,20},{20,24},{24,28},{28,32},{32,36}... | collective-permute-start | bytes 196616 | tf_op jit(solution)/shard_map/ppermute | solution.py:74
  153.1 10.7 %collective-permute-start.19 = (f32[4,32,128]{2,1,0:T(8,128)S(1)}, f32[4,32,128]{2,1,0:T(8,128)S(1)}, u32[]{:S(2)}, u32[]{:S(2)}) collective-permute-start(f32[4,32,128]{2,1,0:T(8,128)S(1)} %bitcast.107), channel_id=1, source_target_pairs={{4,0},{8,4},{12,8},{16,12},{20,16},{24,20},{28,24},{32,28},{36,32}... | collective-permute-start | bytes 196616 | tf_op jit(solution)/shard_map/ppermute | solution.py:75
  (13 other events, 24.6 us)
where the time goes:
time: 173 us; the launch traced here: 172 us
  starting transfers between devices  69.1 us (40%)
  Pallas kernels  37.9 us (22%)
  local copies, waits for them, and re-layouts  33.7 us (19%)
  other arithmetic  29.9 us (17%)
  between operations  1.74 us (1%)
    ppermute x4, starting transfers between devices, edge_halos(): from_east = lax.ppermute(first_col, 'lon', down)  30.8 us
    pallas_call x2, Pallas kernels, forward_step(): pl.pallas_call(forward_kernel, out_shape=outs, in_specs=[pl.BlockSpec(mem...  20.1 us
    pallas_call x2, Pallas kernels, backward_step(): pl.pallas_call(lambda *refs: backward_kernel(*refs, last=last), out_shape...  17.8 us
    ppermute x4, starting transfers between devices, edge_halos(): lax.ppermute(jnp.where(low, first_row, last_row), ('lon', 'lat'), ccw_pairs)  14.3 us
    scatter-add x1, other arithmetic, on_device(): lam = jnp.zeros_like(table).at[row_of].add(spread).reshape(x.shape)  14.2 us
    all_to_all x1, starting transfers between devices, on_device(): arrived = lax.all_to_all(send, 'lon', 0, 0, tiled=True)  10.9 us
    ppermute x1, starting transfers between devices, halos(): from_east = lax.ppermute(x[:, :, 0, :], 'lon', down)  7.74 us
    gather x1, local copies, waits for them, and re-layouts, on_device(): picked = jnp.sum(jnp.where(lane_hit, table[row_of], 0.0), axis=1)  6.68 us
  transfers between devices with their start and end apart: 21, of which 0 were waited for; matrix products, arithmetic and copies ran while one was open for 20% of the time, Pallas kernels for 6%

commit v1 on v0

--- a/solution.py
+++ b/solution.py
@@ -7,6 +7,7 @@
 
 STEPS = 2
 CAP = 32
+UNROLL = 1
 
 
 def ring_pairs(n_lon, n_lat):
@@ -82,29 +83,35 @@
     south_row = jnp.where(low, ccw, cw)
     north_row = jnp.where(lat_j == 0, flip * north_row, north_row)
     south_row = jnp.where(lat_j == n_lat - 1, flip * south_row, south_row)
-    return (north_row[..., None], south_row[..., None], from_west[:, :, None, :], from_east[:, :, None, :])
-
-
-def neighbours_2d(v, hn, hs, hw, he):
+    return (jnp.stack([north_row, south_row], axis=-1), from_west[:, :, None, :], from_east[:, :, None, :])
+
+
+def edge_masks(shape):
+    rows = lax.broadcasted_iota(jnp.int32, shape, 1)
+    cols = lax.broadcasted_iota(jnp.int32, shape, 0)
+    return rows == 0, rows == shape[1] - 1, cols == 0, cols == shape[0] - 1
+
+
+def neighbours_2d(v, masks, hn, hs, hw, he):
     c_n, r_n = v.shape
-    rows = lax.broadcasted_iota(jnp.int32, v.shape, 1)
-    cols = lax.broadcasted_iota(jnp.int32, v.shape, 0)
-    north = jnp.where(rows == 0, hn, pltpu.roll(v, 1, 1))
-    south = jnp.where(rows == r_n - 1, hs, pltpu.roll(v, r_n - 1, 1))
-    west = jnp.where(cols == 0, hw, pltpu.roll(v, 1, 0))
-    east = jnp.where(cols == c_n - 1, he, pltpu.roll(v, c_n - 1, 0))
+    top, bottom, left, right = masks
+    north = jnp.where(top, hn, pltpu.roll(v, 1, 1))
+    south = jnp.where(bottom, hs, pltpu.roll(v, r_n - 1, 1))
+    west = jnp.where(left, hw, pltpu.roll(v, 1, 0))
+    east = jnp.where(right, he, pltpu.roll(v, c_n - 1, 0))
     return north, south, west, east
 
 
-def write_edges(v, f, l, fc, lc, fr, lr):
+def write_edges(v, f, l, fc, lc, frl):
     fc[f, l] = v[0:1, :]
     lc[f, l] = v[-1:, :]
-    fr[f, l] = v[:, 0:1]
-    lr[f, l] = v[:, -1:]
-
-
-def forward_kernel(cpl, x_ref, c_ref, hn, hs, hw, he, xn_ref, d_ref, fc, lc, fr, lr):
+    frl[f, l, :, 0:1] = v[:, 0:1]
+    frl[f, l, :, 1:2] = v[:, -1:]
+
+
+def forward_kernel(cpl, x_ref, c_ref, hns, hw, he, xn_ref, d_ref, fc, lc, frl):
     nf = x_ref.shape[0]
+    masks = edge_masks(x_ref.shape[2:])
 
     def body(l, carry):
         xs = [x_ref[f, l] for f in range(nf)]
@@ -112,7 +119,7 @@
         total = cs[0] + cs[1] + cs[2] + cs[3]
         for g in range(nf):
             v = xs[g]
-            north, south, west, east = neighbours_2d(v, hn[g, l], hs[g, l], hw[g, l], he[g, l])
+            north, south, west, east = neighbours_2d(v, masks, hns[g, l, :, 0:1], hns[g, l, :, 1:2], hw[g, l], he[g, l])
             mixed = cpl[l * nf * nf + g * nf] * xs[0]
             for f in range(1, nf):
                 mixed = mixed + cpl[l * nf * nf + g * nf + f] * xs[f]
@@ -121,14 +128,15 @@
             xn = y - 0.5 * t
             xn_ref[g, l] = xn
             d_ref[g, l] = 1.0 - 0.5 * (1.0 - t * t)
-            write_edges(xn, g, l, fc, lc, fr, lr)
+            write_edges(xn, g, l, fc, lc, frl)
         return carry
 
-    lax.fori_loop(0, x_ref.shape[1], body, 0)
-
-
-def backward_kernel(cpl, ly_ref, c_ref, b_ref, dp_ref, hn, hs, hw, he, out_ref, fc, lc, fr, lr, *, last):
+    lax.fori_loop(0, x_ref.shape[1], body, 0, unroll=UNROLL)
+
+
+def backward_kernel(cpl, ly_ref, c_ref, b_ref, dp_ref, hns, hw, he, out_ref, fc, lc, frl, *, last):
     nf = ly_ref.shape[0]
+    masks = edge_masks(ly_ref.shape[2:])
 
     def body(l, carry):
         ls = [ly_ref[f, l] for f in range(nf)]
@@ -137,7 +145,7 @@
         bs = [b_ref[d, l] for d in range(4)]
         for o in range(nf):
             v = ls[o]
-            north, south, west, east = neighbours_2d(v, hn[o, l], hs[o, l], hw[o, l], he[o, l])
+            north, south, west, east = neighbours_2d(v, masks, hns[o, l, :, 0:1], hns[o, l, :, 1:2], hw[o, l], he[o, l])
             back = cpl[l * nf * nf + o] * ls[0]
             for g in range(1, nf):
                 back = back + cpl[l * nf * nf + g * nf + o] * ls[g]
@@ -147,10 +155,10 @@
             else:
                 nxt = lam * dp_ref[o, l]
                 out_ref[o, l] = nxt
-                write_edges(nxt, o, l, fc, lc, fr, lr)
+                write_edges(nxt, o, l, fc, lc, frl)
         return carry
 
-    lax.fori_loop(0, ly_ref.shape[1], body, 0)
+    lax.fori_loop(0, ly_ref.shape[1], body, 0, unroll=UNROLL)
 
 
 def edge_shapes(x):
@@ -158,8 +166,7 @@
     return [
         jax.ShapeDtypeStruct((f, l, 1, r), x.dtype),
         jax.ShapeDtypeStruct((f, l, 1, r), x.dtype),
-        jax.ShapeDtypeStruct((f, l, c, 1), x.dtype),
-        jax.ShapeDtypeStruct((f, l, c, 1), x.dtype),
+        jax.ShapeDtypeStruct((f, l, c, 2), x.dtype),
     ]
 
 
@@ -172,8 +179,8 @@
     return pl.pallas_call(
         forward_kernel,
         out_shape=outs,
-        in_specs=[pl.BlockSpec(memory_space=pltpu.SMEM)] + vmem_specs(6),
-        out_specs=vmem_specs(6),
+        in_specs=[pl.BlockSpec(memory_space=pltpu.SMEM)] + vmem_specs(5),
+        out_specs=vmem_specs(5),
     )(cpl, x, coef, *halo)
 
 
@@ -182,8 +189,8 @@
     return pl.pallas_call(
         lambda *refs: backward_kernel(*refs, last=last),
         out_shape=outs,
-        in_specs=[pl.BlockSpec(memory_space=pltpu.SMEM)] + vmem_specs(8),
-        out_specs=vmem_specs(5),
+        in_specs=[pl.BlockSpec(memory_space=pltpu.SMEM)] + vmem_specs(7),
+        out_specs=vmem_specs(4),
     )(cpl, ly, coef, back_coef, dprev, *halo)
 
 
@@ -192,8 +199,8 @@
 
 
 def squeezed(edges):
-    fc, lc, fr, lr = edges
-    return (fc[:, :, 0, :], lc[:, :, 0, :], fr[..., 0], lr[..., 0])
+    fc, lc, frl = edges
+    return (fc[:, :, 0, :], lc[:, :, 0, :], frl[..., 0], frl[..., 1])
 
 
 def on_device(

time: 173 us -> 163 us (0.942)
  starting transfers between devices: 69.1 us -> 60.6 us
  local copies, waits for them, and re-layouts: 33.7 us -> 28.5 us
  waiting for transfers between devices: 0.06 us -> 4.17 us
  Pallas kernels: 37.9 us -> 36.1 us
    broadcast_in_dim x8 -> x0, local copies, waits for them, and re-layouts: 11.6 us -> none  [the longest x4 5.78 us: edge_halos(): south_row[..., None]]
    ppermute x4, starting transfers between devices: 14.3 us -> 6.56 us  [edge_halos(): lax.ppermute(jnp.where(low, first_row, last_row), ('lon', 'lat'), ccw_pairs)]
    ppermute x1, starting transfers between devices: 7.74 us -> 0.56 us  [halos(): from_east = lax.ppermute(x[:, :, 0, :], 'lon', down)]
    another operation x0 -> x4, local copies, waits for them, and re-layouts: none -> 5.76 us  [edge_halos(): jnp.stack([north_row, south_row], axis=-1)]
    ppermute x1, starting transfers between devices: 0.01 us -> 2.97 us  [halos(): from_west = lax.ppermute(x[:, :, -1, :], 'lon', up)]
    ppermute x4, waiting for transfers between devices: 0.01 us -> 2.78 us  [edge_halos(): lax.ppermute(jnp.where(low, last_row, first_row), ('lon', 'lat'), cw_pairs)]
  transfers between devices with their start and end apart: 21 -> 21, of which waited for: 0 -> 3; matrix products, arithmetic and copies ran while one was open for 20% -> 19% of each run, Pallas kernels for 6% -> 6%
where the time goes in v1:
time: 163 us; the launch traced here: 162 us
  starting transfers between devices  60.6 us (37%)
  Pallas kernels  36.1 us (22%)
  other arithmetic  30.7 us (19%)
  local copies, waits for them, and re-layouts  28.5 us (17%)
  waiting for transfers between devices  4.17 us (3%)
  between operations  1.69 us (1%)
    ppermute x4, starting transfers between devices, edge_halos(): from_east = lax.ppermute(first_col, 'lon', down)  32.4 us
    pallas_call x2, Pallas kernels, forward_step(): pl.pallas_call(forward_kernel, out_shape=outs, in_specs=[pl.BlockSpec(mem...  19.2 us
    pallas_call x2, Pallas kernels, backward_step(): pl.pallas_call(lambda *refs: backward_kernel(*refs, last=last), out_shape...  16.8 us
    scatter-add x1, other arithmetic, on_device(): lam = jnp.zeros_like(table).at[row_of].add(spread).reshape(x.shape)  13.3 us
    all_to_all x1, starting transfers between devices, on_device(): arrived = lax.all_to_all(send, 'lon', 0, 0, tiled=True)  12.5 us
    gather x1, local copies, waits for them, and re-layouts, on_device(): picked = jnp.sum(jnp.where(lane_hit, table[row_of], 0.0), axis=1)  6.68 us
    ppermute x4, starting transfers between devices, edge_halos(): lax.ppermute(jnp.where(low, first_row, last_row), ('lon', 'lat'), ccw_pairs)  6.56 us
    another operation x4, local copies, waits for them, and re-layouts, edge_halos(): jnp.stack([north_row, south_row], axis=-1)  5.76 us
  transfers between devices with their start and end apart: 21, of which 3 were waited for; matrix products, arithmetic and copies ran while one was open for 19% of the time, Pallas kernels for 6%

profile of v1, /device:TPU:0, one launch (start us, length us, event | category | flops | bytes accessed | tf_op | source)
XLA Modules:
  0.0 161.8 jit_solution(17169658616144119588)
XLA Ops:
  0.6 1.9 %fusion.25 = (f32[4,32,1,128]{3,2,1,0:T(1,128)}, f32[4,32,1,128]{3,2,1,0:T(1,128)}) fusion(f32[4,32,16,128]{3,2,1,0:T(8,128)} %x_ref.1), kind=kLoop, calls=%fused_computation.78 | loop fusion | bytes 262144 | tf_op jit(solution)/shard_map/slice | solution.py:198
  2.6 1.3 collective-permute-start.2
  4.6 1.0 convert_reduce_fusion
  7.8 1.9 %select_reduce_fusion = f32[2048,3]{0,1:T(4,128)S(1)} fusion(f32[512,3]{0,1:T(4,128)S(1)} %pad_maximum_fusion.6, pred[2048,512]{1,0:T(8,128)(4,1)S(1)} %iota_compare_fusion), kind=kLoop, calls=%fused_computation.2 | loop fusion | flops 6285312 | bytes 1079296 | tf_op jit(solution)/shard_map/reduce_sum | solution.py:232
  10.5 12.5 %all-to-all-start = ((f32[64,32,3]{1,2,0:T(4,128)}), f32[64,32,3]{1,2,0:T(4,128)S(1)}, u32[]{:S(2)}, u32[]{:S(2)}) async-start(f32[64,32,3]{1,2,0:T(4,128)} %copy.783), calls=%async_computation | async-start | bytes 262144 | tf_op jit(solution)/shard_map/all_to_all | solution.py:233
  23.9 3.2 %collective-permute-start.1 = (f32[4,32,16]{1,2,0:T(8,128)S(1)}, f32[4,32,16]{1,2,0:T(8,128)S(1)}, u32[]{:S(2)}, u32[]{:S(2)}) collective-permute-start(f32[4,32,16]{1,2,0:T(8,128)S(1)} %bitcast.92), channel_id=1, source_target_pairs={{1,0},{2,1},{3,2},{131,3},{130,131},{129,130},{128,129},{0,128},{5... | collective-permute-start | bytes 24584 | tf_op jit(solution)/shard_map/ppermute | solution.py:81
  28.6 3.6 %collective-permute-start.9 = (f32[4,32,16]{1,2,0:T(8,128)S(1)}, f32[4,32,16]{1,2,0:T(8,128)}, u32[]{:S(2)}, u32[]{:S(2)}) collective-permute-start(f32[4,32,16]{1,2,0:T(8,128)S(1)} %bitcast.91), channel_id=1, source_target_pairs={{1,0},{2,1},{3,2},{131,3},{130,131},{129,130},{128,129},{0,128},{5... | collective-permute-start | bytes 24584 | tf_op jit(solution)/shard_map/ppermute | solution.py:39
  33.5 1.5 fusion.24
  34.9 1.3 fusion.22
  37.1 7.9 %collective-permute-start.3 = (f32[4,32,128]{2,1,0:T(8,128)}, f32[4,32,128]{2,1,0:T(8,128)}, u32[]{:S(2)}, u32[]{:S(2)}) collective-permute-start(f32[4,32,128]{2,1,0:T(8,128)} %bitcast.6), channel_id=1, source_target_pairs={{4,0},{8,4},{12,8},{16,12},{20,16},{24,20},{28,24},{32,28},{36,32}... | collective-permute-start | bytes 196616 | tf_op jit(solution)/shard_map/ppermute | solution.py:76
  45.6 3.0 %collective-permute-start.10 = (f32[4,32,128]{2,1,0:T(8,128)}, f32[4,32,128]{2,1,0:T(8,128)}, u32[]{:S(2)}, u32[]{:S(2)}) collective-permute-start(f32[4,32,128]{2,1,0:T(8,128)} %bitcast.31), channel_id=1, source_target_pairs={{0,4},{4,8},{8,12},{12,16},{16,20},{20,24},{24,28},{28,32},{32,36}... | collective-permute-start | bytes 196616 | tf_op jit(solution)/shard_map/ppermute | solution.py:31
  48.6 1.4 fusion.12
  51.2 1.2 fusion.10
  53.4 1.4 copy.779.hns
  55.6 9.6 %shard_map.104 = (f32[4,32,16,128]{3,2,1,0:T(8,128)}, f32[4,32,16,128]{3,2,1,0:T(8,128)}, f32[4,32,1,128]{3,2,1,0:T(1,128)}, f32[4,32,1,128]{3,2,1,0:T(1,128)}, f32[4,32,16,2]{3,2,1,0:T(8,128)}) custom-call(f32[512]{0:T(512)} %reshape.106.cpl.refs_0_, f32[4,32,16,128]{3,2,1,0:T(8,128)} %x_ref.1, f32[4,32,16,128]{3,2,1,0:T(8,128)} %refs_2_.3, ...), custom_call_target="tpu_custom_call" | custom-call | tf_op jit(solution)/shard_map/pallas_call | solution.py:179
  65.2 7.7 %collective-permute-start.7 = (f32[4,32,128]{2,1,0:T(8,128)}, f32[4,32,128]{2,1,0:T(8,128)}, u32[]{:S(2)}, u32[]{:S(2)}) collective-permute-start(f32[4,32,128]{2,1,0:T(8,128)} %bitcast.104), channel_id=1, source_target_pairs={{4,0},{8,4},{12,8},{16,12},{20,16},{24,20},{28,24},{32,28},{36,32}... | collective-permute-start | bytes 196616 | tf_op jit(solution)/shard_map/ppermute | solution.py:76
  73.0 2.0 %slice_select_fusion.7 = (f32[4,32,16,1]{3,2,1,0:T(8,128)S(1)}, f32[4,32,16,1]{3,2,1,0:T(8,128)S(1)}) fusion(f32[4,32,16,2]{3,2,1,0:T(8,128)} %get-tuple-element.15, pred[]{:T(512)S(6)} %lt.44), kind=kLoop, calls=%fused_computation.26 | loop fusion | flops 4096 | bytes 32769 | tf_op jit(solution)/shard_map/jit(_where)/select_n | solution.py:80
  75.5 1.1 copy.781
  77.1 2.1 %fusion.refs_3_ = f32[4,32,16,128]{3,2,1,0:T(8,128)} fusion(f32[4,32,1,128]{3,2,1,0:T(1,128)} %bitcast.34, f32[4,32,15,128]{3,2,1,0:T(8,128)S(1)} %copy-done.4, f32[4,32,15,128]{3,2,1,0:T(8,128)S(1)} %copy-done.3, f32[4,32,1,128]{3,2,1,0:T(1,128)} %bitcast.32, f32[1,32,16,128]{3,2,1,0:T(8,128)S(1)} %fusion.10, f32[1,32,16,128]{3,2,1,0:T(8,128)} %fusion.11), kind=kLoop, calls=%fused_computation.7 | loop fusion | flops 3407872 | bytes 3670016 | tf_op jit(solution)/shard_map/stack | solution.py:253
  79.2 2.8 %collective-permute-done.4 = f32[4,32,16]{1,2,0:T(8,128)S(1)} collective-permute-done((f32[4,32,16]{1,2,0:T(8,128)S(1)}, f32[4,32,16]{1,2,0:T(8,128)S(1)}, u32[]{:S(2)}, u32[]{:S(2)}) %collective-permute-start.4) | collective-permute-done | bytes 8224 | tf_op jit(solution)/shard_map/ppermute | solution.py:80
  82.1 1.4 copy.782.hns
  84.2 9.6 %shard_map.105 = (f32[4,32,16,128]{3,2,1,0:T(8,128)}, f32[4,32,16,128]{3,2,1,0:T(8,128)}, f32[4,32,1,128]{3,2,1,0:T(1,128)}, f32[4,32,1,128]{3,2,1,0:T(1,128)}, f32[4,32,16,2]{3,2,1,0:T(8,128)}) custom-call(f32[512]{0:T(512)} %reshape.106.cpl.refs_0_, f32[4,32,16,128]{3,2,1,0:T(8,128)} %get-tuple-element.14.x_ref, f32[4,32,16,128]{3,2,1,0:T(8,128)} %refs_2_.3, ...), custom_call_target="tpu_custom_call" | custom-call | tf_op jit(solution)/shard_map/pallas_call | solution.py:179
  93.8 6.7 %gather_fusion = f32[2048,128]{1,0:T(8,128)S(1)} fusion(f32[2048,128]{1,0:T(8,128)} %bitcast.76, s32[2048]{0:T(1024)S(1)} %copy-done.13), kind=kCustom, calls=%fused_computation | custom fusion | bytes 2105344 | tf_op jit(solution)/shard_map/gather | solution.py:242
  101.2 13.3 %scatter_custom_fusion = f32[2048,128]{1,0:T(8,128)S(1)} fusion(s32[2048]{0:T(1024)S(1)} %bitcast.100, f32[2048]{0:T(1024)S(1)} %bitcast.87, s32[2048]{0:T(1024)S(1)} %bitcast.79, f32[]{:T(128)} %constant.46.clone.1), kind=kCustom, calls=%fused_computation.14 | custom fusion | flops 786432 | bytes 1065984 | tf_op jit(solution)/shard_map/scatter-add | solution.py:245
  117.2 7.7 %collective-permute-start.15 = (f32[4,32,128]{2,1,0:T(8,128)S(1)}, f32[4,32,128]{2,1,0:T(8,128)S(1)}, u32[]{:S(2)}, u32[]{:S(2)}) collective-permute-start(f32[4,32,128]{2,1,0:T(8,128)S(1)} %bitcast.85), channel_id=1, source_target_pairs={{4,0},{8,4},{12,8},{16,12},{20,16},{24,20},{28,24},{32,28},{36,32}... | collective-permute-start | bytes 196616 | tf_op jit(solution)/shard_map/ppermute | solution.py:76
  125.0 1.4 copy.793.refs_5_
  127.8 9.6 %shard_map.106 = (f32[4,32,16,128]{3,2,1,0:T(8,128)}, f32[4,32,1,128]{3,2,1,0:T(1,128)}, f32[4,32,1,128]{3,2,1,0:T(1,128)}, f32[4,32,16,2]{3,2,1,0:T(8,128)}) custom-call(f32[512]{0:T(512)} %reshape.106.cpl.refs_0_, f32[4,32,16,128]{3,2,1,0:T(8,128)} %copy-done.1, f32[4,32,16,128]{3,2,1,0:T(8,128)} %refs_2_.3, f32[4,32,16,128]{3,2,1,0:T(8,128)} %fusion.refs_3_, ...), custom_call_target="tpu_custom_call" | custom-call | tf_op jit(solution)/shard_map/pallas_call | solution.py:189
  137.4 1.9 %slice_select_fusion.3 = (f32[4,32,16,1]{3,2,1,0:T(8,128)S(1)}, f32[4,32,16,1]{3,2,1,0:T(8,128)S(1)}) fusion(f32[4,32,16,2]{3,2,1,0:T(8,128)} %get-tuple-element.22, pred[]{:T(512)S(6)} %lt.44), kind=kLoop, calls=%fused_computation.22 | loop fusion | flops 4096 | bytes 32769 | tf_op jit(solution)/shard_map/jit(_where)/select_n | solution.py:80
  140.3 2.3 %collective-permute-start.17 = (f32[4,32,16]{1,2,0:T(8,128)S(1)}, f32[4,32,16]{1,2,0:T(8,128)S(1)}, u32[]{:S(2)}, u32[]{:S(2)}) collective-permute-start(f32[4,32,16]{1,2,0:T(8,128)S(1)} %bitcast.98), channel_id=1, source_target_pairs={{1,0},{2,1},{3,2},{131,3},{130,131},{129,130},{128,129},{0,128},{5... | collective-permute-start | bytes 24584 | tf_op jit(solution)/shard_map/ppermute | solution.py:81
  142.7 9.0 %collective-permute-start.19 = (f32[4,32,128]{2,1,0:T(8,128)S(1)}, f32[4,32,128]{2,1,0:T(8,128)S(1)}, u32[]{:S(2)}, u32[]{:S(2)}) collective-permute-start(f32[4,32,128]{2,1,0:T(8,128)S(1)} %bitcast.106), channel_id=1, source_target_pairs={{4,0},{8,4},{12,8},{16,12},{20,16},{24,20},{28,24},{32,28},{36,32}... | collective-permute-start | bytes 196616 | tf_op jit(solution)/shard_map/ppermute | solution.py:76
  151.8 1.4 copy.796.refs_5_
  154.5 7.3 %shard_map.107 = (f32[4,32,16,128]{3,2,1,0:T(8,128)}, f32[4,32,1,128]{3,2,1,0:T(1,128)}, f32[4,32,1,128]{3,2,1,0:T(1,128)}, f32[4,32,16,2]{3,2,1,0:T(8,128)}) custom-call(f32[512]{0:T(512)} %reshape.106.cpl.refs_0_, f32[4,32,16,128]{3,2,1,0:T(8,128)} %get-tuple-element.21.refs_1_, f32[4,32,16,128]{3,2,1,0:T(8,128)} %refs_2_.3, ...), custom_call_target="tpu_custom_call" | custom-call | tf_op jit(solution)/shard_map/pallas_call | solution.py:189
  (118 shorter events, 19.7 us)
Async XLA Ops:
  0.6 7.2 %copy-start.19 = (f32[1,512]{1,0:T(1,128)S(1)}, f32[1,512]{1,0:T(1,128)}, u32[]{:S(2)}) copy-start(f32[1,512]{1,0:T(1,128)} %param.15) | copy-start | bytes 6148
  0.6 7.2 %copy-start.18 = (f32[1,512]{1,0:T(1,128)S(1)}, f32[1,512]{1,0:T(1,128)}, u32[]{:S(2)}) copy-start(f32[1,512]{1,0:T(1,128)} %param.14) | copy-start | bytes 6148
  2.6 53.0 %collective-permute-start.2 = (f32[4,32,128]{2,1,0:T(8,128)}, f32[4,32,128]{2,1,0:T(8,128)}, u32[]{:S(2)}, u32[]{:S(2)}) collective-permute-start(f32[4,32,128]{2,1,0:T(8,128)} %bitcast.4), channel_id=1, source_target_pairs={{0,4},{4,8},{8,12},{12,16},{16,20},{20,24},{24,28},{28,32},{32,36}... | collective-permute-start | bytes 196616 | tf_op jit(solution)/shard_map/ppermute | solution.py:75
  7.8 15.3 %copy-start.2 = (f32[4,32,16,128]{3,2,1,0:T(8,128)S(1)}, f32[4,32,16,128]{3,2,1,0:T(8,128)}, u32[]{:S(2)}) copy-start(f32[4,32,16,128]{3,2,1,0:T(8,128)} %x_ref.1) | copy-start | bytes 3145732
  10.5 44.3 %all-to-all-start = ((f32[64,32,3]{1,2,0:T(4,128)}), f32[64,32,3]{1,2,0:T(4,128)S(1)}, u32[]{:S(2)}, u32[]{:S(2)}) async-start(f32[64,32,3]{1,2,0:T(4,128)} %copy.783), calls=%async_computation | async-start | bytes 262144 | tf_op jit(solution)/shard_map/all_to_all | solution.py:233
  23.4 4.3 %copy-start = (f32[4,32,16,128]{3,2,1,0:T(8,128)S(1)}, f32[4,32,16,128]{3,2,1,0:T(8,128)}, u32[]{:S(2)}) copy-start(f32[4,32,16,128]{3,2,1,0:T(8,128)} %refs_2_.3) | copy-start | bytes 3145732
  23.9 13.2 %collective-permute-start.1 = (f32[4,32,16]{1,2,0:T(8,128)S(1)}, f32[4,32,16]{1,2,0:T(8,128)S(1)}, u32[]{:S(2)}, u32[]{:S(2)}) collective-permute-start(f32[4,32,16]{1,2,0:T(8,128)S(1)} %bitcast.92), channel_id=1, source_target_pairs={{1,0},{2,1},{3,2},{131,3},{130,131},{129,130},{128,129},{0,128},{5... | collective-permute-start | bytes 24584 | tf_op jit(solution)/shard_map/ppermute | solution.py:81
  27.6 17.4 %collective-permute-start = (f32[4,32,16]{1,2,0:T(8,128)S(1)}, f32[4,32,16]{1,2,0:T(8,128)S(1)}, u32[]{:S(2)}, u32[]{:S(2)}) collective-permute-start(f32[4,32,16]{1,2,0:T(8,128)S(1)} %bitcast.90), channel_id=1, source_target_pairs={{0,1},{1,2},{2,3},{3,131},{131,130},{130,129},{129,128},{128,0},{4... | collective-permute-start | bytes 24584 | tf_op jit(solution)/shard_map/ppermute | solution.py:80
  28.6 17.1 %collective-permute-start.9 = (f32[4,32,16]{1,2,0:T(8,128)S(1)}, f32[4,32,16]{1,2,0:T(8,128)}, u32[]{:S(2)}, u32[]{:S(2)}) collective-permute-start(f32[4,32,16]{1,2,0:T(8,128)S(1)} %bitcast.91), channel_id=1, source_target_pairs={{1,0},{2,1},{3,2},{131,3},{130,131},{129,130},{128,129},{0,128},{5... | collective-permute-start | bytes 24584 | tf_op jit(solution)/shard_map/ppermute | solution.py:39
  32.7 16.0 %collective-permute-start.8 = (f32[4,32,16]{1,2,0:T(8,128)S(1)}, f32[4,32,16]{1,2,0:T(8,128)S(1)}, u32[]{:S(2)}, u32[]{:S(2)}) collective-permute-start(f32[4,32,16]{1,2,0:T(8,128)S(1)} %bitcast.89), channel_id=1, source_target_pairs={{0,1},{1,2},{2,3},{3,131},{131,130},{130,129},{129,128},{128,0},{4... | collective-permute-start | bytes 24584 | tf_op jit(solution)/shard_map/ppermute | solution.py:38
  34.9 13.7 %copy-start.14 = (f32[4]{0:T(128)S(1)}, f32[4]{0:T(128)}, u32[]{:S(2)}) copy-start(f32[4]{0:T(128)} %constant.53.clone) | copy-start | bytes 52
  37.1 18.5 %collective-permute-start.3 = (f32[4,32,128]{2,1,0:T(8,128)}, f32[4,32,128]{2,1,0:T(8,128)}, u32[]{:S(2)}, u32[]{:S(2)}) collective-permute-start(f32[4,32,128]{2,1,0:T(8,128)} %bitcast.6), channel_id=1, source_target_pairs={{4,0},{8,4},{12,8},{16,12},{20,16},{24,20},{28,24},{32,28},{36,32}... | collective-permute-start | bytes 196616 | tf_op jit(solution)/shard_map/ppermute | solution.py:76
  45.1 31.5 %collective-permute-start.11 = (f32[4,32,128]{2,1,0:T(8,128)}, f32[4,32,128]{2,1,0:T(8,128)}, u32[]{:S(2)}, u32[]{:S(2)}) collective-permute-start(f32[4,32,128]{2,1,0:T(8,128)} %bitcast.33), channel_id=1, source_target_pairs={{4,0},{8,4},{12,8},{16,12},{20,16},{24,20},{28,24},{32,28},{36,32}... | collective-permute-start | bytes 196616 | tf_op jit(solution)/shard_map/ppermute | solution.py:32
  45.6 31.5 %collective-permute-start.10 = (f32[4,32,128]{2,1,0:T(8,128)}, f32[4,32,128]{2,1,0:T(8,128)}, u32[]{:S(2)}, u32[]{:S(2)}) collective-permute-start(f32[4,32,128]{2,1,0:T(8,128)} %bitcast.31), channel_id=1, source_target_pairs={{0,4},{4,8},{8,12},{12,16},{16,20},{20,24},{24,28},{28,32},{32,36}... | collective-permute-start | bytes 196616 | tf_op jit(solution)/shard_map/ppermute | solution.py:31
  65.2 18.3 %collective-permute-start.6 = (f32[4,32,128]{2,1,0:T(8,128)}, f32[4,32,128]{2,1,0:T(8,128)S(1)}, u32[]{:S(2)}, u32[]{:S(2)}) collective-permute-start(f32[4,32,128]{2,1,0:T(8,128)} %bitcast.105), channel_id=1, source_target_pairs={{0,4},{4,8},{8,12},{12,16},{16,20},{20,24},{24,28},{28,32},{32,36}... | collective-permute-start | bytes 196616 | tf_op jit(solution)/shard_map/ppermute | solution.py:75
  65.2 18.3 %collective-permute-start.7 = (f32[4,32,128]{2,1,0:T(8,128)}, f32[4,32,128]{2,1,0:T(8,128)}, u32[]{:S(2)}, u32[]{:S(2)}) collective-permute-start(f32[4,32,128]{2,1,0:T(8,128)} %bitcast.104), channel_id=1, source_target_pairs={{4,0},{8,4},{12,8},{16,12},{20,16},{24,20},{28,24},{32,28},{36,32}... | collective-permute-start | bytes 196616 | tf_op jit(solution)/shard_map/ppermute | solution.py:76
  76.6 2.7 %collective-permute-start.5 = (f32[4,32,16]{1,2,0:T(8,128)}, f32[4,32,16]{1,2,0:T(8,128)S(1)}, u32[]{:S(2)}, u32[]{:S(2)}) collective-permute-start(f32[4,32,16]{1,2,0:T(8,128)} %bitcast.95), channel_id=1, source_target_pairs={{1,0},{2,1},{3,2},{131,3},{130,131},{129,130},{128,129},{0,128},{5... | collective-permute-start | bytes 24584 | tf_op jit(solution)/shard_map/ppermute | solution.py:81
  76.6 5.4 %collective-permute-start.4 = (f32[4,32,16]{1,2,0:T(8,128)S(1)}, f32[4,32,16]{1,2,0:T(8,128)S(1)}, u32[]{:S(2)}, u32[]{:S(2)}) collective-permute-start(f32[4,32,16]{1,2,0:T(8,128)S(1)} %bitcast.93), channel_id=1, source_target_pairs={{0,1},{1,2},{2,3},{3,131},{131,130},{130,129},{129,128},{128,0},{4... | collective-permute-start | bytes 24584 | tf_op jit(solution)/shard_map/ppermute | solution.py:80
  77.1 4.9 %copy-start.15 = (f32[4]{0:T(128)S(1)}, f32[4]{0:T(128)}, u32[]{:S(2)}) copy-start(f32[4]{0:T(128)} %constant.53.clone) | copy-start | bytes 52
  84.2 9.6 %copy-start.13 = (s32[2048]{0:T(1024)S(1)}, s32[2048]{0:T(1024)}, u32[]{:S(2)}) copy-start(s32[2048]{0:T(1024)} %broadcast_clamp_fusion) | copy-start | bytes 24580
  100.5 14.0 %copy-start.5 = (f32[4,32,16,128]{3,2,1,0:T(8,128)S(1)}, f32[4,32,16,128]{3,2,1,0:T(8,128)}, u32[]{:S(2)}) copy-start(f32[4,32,16,128]{3,2,1,0:T(8,128)} %get-tuple-element.19) | copy-start | bytes 3145732
  115.0 9.9 %copy-start.16 = (f32[4]{0:T(128)S(1)}, f32[4]{0:T(128)}, u32[]{:S(2)}) copy-start(f32[4]{0:T(128)} %constant.53.clone) | copy-start | bytes 52
  116.0 8.9 %collective-permute-start.13 = (f32[4,32,16]{1,2,0:T(8,128)S(1)}, f32[4,32,16]{1,2,0:T(8,128)S(1)}, u32[]{:S(2)}, u32[]{:S(2)}) collective-permute-start(f32[4,32,16]{1,2,0:T(8,128)S(1)} %bitcast.97), channel_id=1, source_target_pairs={{1,0},{2,1},{3,2},{131,3},{130,131},{129,130},{128,129},{0,128},{5... | collective-permute-start | bytes 24584 | tf_op jit(solution)/shard_map/ppermute | solution.py:81
  117.0 7.9 %collective-permute-start.12 = (f32[4,32,16]{1,2,0:T(8,128)S(1)}, f32[4,32,16]{1,2,0:T(8,128)S(1)}, u32[]{:S(2)}, u32[]{:S(2)}) collective-permute-start(f32[4,32,16]{1,2,0:T(8,128)S(1)} %bitcast.94), channel_id=1, source_target_pairs={{0,1},{1,2},{2,3},{3,131},{131,130},{130,129},{129,128},{128,0},{4... | collective-permute-start | bytes 24584 | tf_op jit(solution)/shard_map/ppermute | solution.py:80
  117.1 10.1 %collective-permute-start.14 = (f32[4,32,128]{2,1,0:T(8,128)S(1)}, f32[4,32,128]{2,1,0:T(8,128)S(1)}, u32[]{:S(2)}, u32[]{:S(2)}) collective-permute-start(f32[4,32,128]{2,1,0:T(8,128)S(1)} %bitcast.86), channel_id=1, source_target_pairs={{0,4},{4,8},{8,12},{12,16},{16,20},{20,24},{24,28},{28,32},{32,36}... | collective-permute-start | bytes 196616 | tf_op jit(solution)/shard_map/ppermute | solution.py:75
  117.2 10.0 %collective-permute-start.15 = (f32[4,32,128]{2,1,0:T(8,128)S(1)}, f32[4,32,128]{2,1,0:T(8,128)S(1)}, u32[]{:S(2)}, u32[]{:S(2)}) collective-permute-start(f32[4,32,128]{2,1,0:T(8,128)S(1)} %bitcast.85), channel_id=1, source_target_pairs={{4,0},{8,4},{12,8},{16,12},{20,16},{24,20},{28,24},{32,28},{36,32}... | collective-permute-start | bytes 196616 | tf_op jit(solution)/shard_map/ppermute | solution.py:76
  139.3 3.4 %copy-start.21 = (f32[4,32,1,128]{3,2,1,0:T(1,128)S(1)}, f32[4,32,1,128]{3,2,1,0:T(1,128)}, u32[]{:S(2)}) copy-start(f32[4,32,1,128]{3,2,1,0:T(1,128)} %get-tuple-element.23) | copy-start | bytes 196612
  139.3 3.4 %copy-start.20 = (f32[4,32,1,128]{3,2,1,0:T(1,128)S(1)}, f32[4,32,1,128]{3,2,1,0:T(1,128)}, u32[]{:S(2)}) copy-start(f32[4,32,1,128]{3,2,1,0:T(1,128)} %get-tuple-element.24) | copy-start | bytes 196612
  140.3 11.4 %collective-permute-start.17 = (f32[4,32,16]{1,2,0:T(8,128)S(1)}, f32[4,32,16]{1,2,0:T(8,128)S(1)}, u32[]{:S(2)}, u32[]{:S(2)}) collective-permute-start(f32[4,32,16]{1,2,0:T(8,128)S(1)} %bitcast.98), channel_id=1, source_target_pairs={{1,0},{2,1},{3,2},{131,3},{130,131},{129,130},{128,129},{0,128},{5... | collective-permute-start | bytes 24584 | tf_op jit(solution)/shard_map/ppermute | solution.py:81
  142.7 9.0 %collective-permute-start.16 = (f32[4,32,16]{1,2,0:T(8,128)S(1)}, f32[4,32,16]{1,2,0:T(8,128)S(1)}, u32[]{:S(2)}, u32[]{:S(2)}) collective-permute-start(f32[4,32,16]{1,2,0:T(8,128)S(1)} %bitcast.96), channel_id=1, source_target_pairs={{0,1},{1,2},{2,3},{3,131},{131,130},{130,129},{129,128},{128,0},{4... | collective-permute-start | bytes 24584 | tf_op jit(solution)/shard_map/ppermute | solution.py:80
  142.7 11.2 %collective-permute-start.18 = (f32[4,32,128]{2,1,0:T(8,128)S(1)}, f32[4,32,128]{2,1,0:T(8,128)S(1)}, u32[]{:S(2)}, u32[]{:S(2)}) collective-permute-start(f32[4,32,128]{2,1,0:T(8,128)S(1)} %bitcast.107), channel_id=1, source_target_pairs={{0,4},{4,8},{8,12},{12,16},{16,20},{20,24},{24,28},{28,32},{32,36}... | collective-permute-start | bytes 196616 | tf_op jit(solution)/shard_map/ppermute | solution.py:75
  142.7 11.2 %collective-permute-start.19 = (f32[4,32,128]{2,1,0:T(8,128)S(1)}, f32[4,32,128]{2,1,0:T(8,128)S(1)}, u32[]{:S(2)}, u32[]{:S(2)}) collective-permute-start(f32[4,32,128]{2,1,0:T(8,128)S(1)} %bitcast.106), channel_id=1, source_target_pairs={{4,0},{8,4},{12,8},{16,12},{20,16},{24,20},{28,24},{32,28},{36,32}... | collective-permute-start | bytes 196616 | tf_op jit(solution)/shard_map/ppermute | solution.py:76
  (11 other events, 12.5 us)

commit v2 on v1

--- a/solution.py
+++ b/solution.py
@@ -8,6 +8,7 @@
 STEPS = 2
 CAP = 32
 UNROLL = 1
+LEVEL_BLOCK = 8
 
 
 def ring_pairs(n_lon, n_lat):
@@ -114,15 +115,16 @@
     masks = edge_masks(x_ref.shape[2:])
 
     def body(l, carry):
+        lev = pl.program_id(0) * x_ref.shape[1] + l
         xs = [x_ref[f, l] for f in range(nf)]
         cs = [c_ref[d, l] for d in range(4)]
         total = cs[0] + cs[1] + cs[2] + cs[3]
         for g in range(nf):
             v = xs[g]
             north, south, west, east = neighbours_2d(v, masks, hns[g, l, :, 0:1], hns[g, l, :, 1:2], hw[g, l], he[g, l])
-            mixed = cpl[l * nf * nf + g * nf] * xs[0]
+            mixed = cpl[lev * nf * nf + g * nf] * xs[0]
             for f in range(1, nf):
-                mixed = mixed + cpl[l * nf * nf + g * nf + f] * xs[f]
+                mixed = mixed + cpl[lev * nf * nf + g * nf + f] * xs[f]
             y = v + cs[0] * north + cs[1] * south + cs[2] * west + cs[3] * east - total * v + 0.25 * mixed
             t = jnp.tanh(y)
             xn = y - 0.5 * t
@@ -139,6 +141,7 @@
     masks = edge_masks(ly_ref.shape[2:])
 
     def body(l, carry):
+        lev = pl.program_id(0) * ly_ref.shape[1] + l
         ls = [ly_ref[f, l] for f in range(nf)]
         cs = [c_ref[d, l] for d in range(4)]
         total = cs[0] + cs[1] + cs[2] + cs[3]
@@ -146,9 +149,9 @@
         for o in range(nf):
             v = ls[o]
             north, south, west, east = neighbours_2d(v, masks, hns[o, l, :, 0:1], hns[o, l, :, 1:2], hw[o, l], he[o, l])
-            back = cpl[l * nf * nf + o] * ls[0]
+            back = cpl[lev * nf * nf + o] * ls[0]
             for g in range(1, nf):
-                back = back + cpl[l * nf * nf + g * nf + o] * ls[g]
+                back = back + cpl[lev * nf * nf + g * nf + o] * ls[g]
             lam = v - total * v + 0.25 * back + bs[0] * north + bs[1] * south + bs[2] * west + bs[3] * east
             if last:
                 out_ref[o, l] = lam
@@ -170,28 +173,36 @@
     ]
 
 
-def vmem_specs(n):
-    return [pl.BlockSpec(memory_space=pltpu.VMEM) for _ in range(n)]
+def level_specs(arrays):
+    specs = []
+    for a in arrays:
+        block = (a.shape[0], LEVEL_BLOCK) + tuple(a.shape[2:])
+        specs.append(pl.BlockSpec(block, lambda i: (0, i, 0, 0)))
+    return specs
 
 
 def forward_step(cpl, x, coef, halo):
     outs = [jax.ShapeDtypeStruct(x.shape, x.dtype)] * 2 + edge_shapes(x)
+    ins = [x, coef, *halo]
     return pl.pallas_call(
         forward_kernel,
         out_shape=outs,
-        in_specs=[pl.BlockSpec(memory_space=pltpu.SMEM)] + vmem_specs(5),
-        out_specs=vmem_specs(5),
-    )(cpl, x, coef, *halo)
+        grid=(x.shape[1] // LEVEL_BLOCK,),
+        in_specs=[pl.BlockSpec(memory_space=pltpu.SMEM)] + level_specs(ins),
+        out_specs=level_specs(outs),
+    )(cpl, *ins)
 
 
 def backward_step(cpl, ly, coef, back_coef, dprev, halo, last):
     outs = [jax.ShapeDtypeStruct(ly.shape, ly.dtype)] + edge_shapes(ly)
+    ins = [ly, coef, back_coef, dprev, *halo]
     return pl.pallas_call(
         lambda *refs: backward_kernel(*refs, last=last),
         out_shape=outs,
-        in_specs=[pl.BlockSpec(memory_space=pltpu.SMEM)] + vmem_specs(7),
-        out_specs=vmem_specs(4),
-    )(cpl, ly, coef, back_coef, dprev, *halo)
+        grid=(ly.shape[1] // LEVEL_BLOCK,),
+        in_specs=[pl.BlockSpec(memory_space=pltpu.SMEM)] + level_specs(ins),
+        out_specs=level_specs(outs),
+    )(cpl, *ins)
 
 
 def edges_of(x):

time: 163 us -> 159 us (0.975)
  Pallas kernels: 36.1 us -> 31 us
    pallas_call x2, Pallas kernels: 19.2 us -> 16.5 us  [forward_step(): pl.pallas_call(forward_kernel, out_shape=outs, grid=(x.shape[1] // LEVEL_...]
    pallas_call x2, Pallas kernels: 16.8 us -> 14.5 us  [backward_step(): pl.pallas_call(lambda *refs: backward_kernel(*refs, last=last), out_shape...]
  transfers between devices with their start and end apart: 21 -> 21, of which waited for: 3 -> 3; matrix products, arithmetic and copies ran while one was open for 19% -> 19% of each run, Pallas kernels for 6% -> 5%
where the time goes in v2:
time: 159 us; the launch traced here: 158 us
  starting transfers between devices  60.7 us (38%)
  other arithmetic  32.2 us (20%)
  Pallas kernels  31 us (19%)
  local copies, waits for them, and re-layouts  28.5 us (18%)
  waiting for transfers between devices  4.13 us (3%)
  between operations  1.81 us (1%)
    ppermute x4, starting transfers between devices, edge_halos(): from_east = lax.ppermute(first_col, 'lon', down)  32.4 us
    pallas_call x2, Pallas kernels, forward_step(): pl.pallas_call(forward_kernel, out_shape=outs, grid=(x.shape[1] // LEVEL_...  16.5 us
    scatter-add x1, other arithmetic, on_device(): lam = jnp.zeros_like(table).at[row_of].add(spread).reshape(x.shape)  14.8 us
    pallas_call x2, Pallas kernels, backward_step(): pl.pallas_call(lambda *refs: backward_kernel(*refs, last=last), out_shape...  14.5 us
    all_to_all x1, starting transfers between devices, on_device(): arrived = lax.all_to_all(send, 'lon', 0, 0, tiled=True)  12.5 us
    gather x1, local copies, waits for them, and re-layouts, on_device(): picked = jnp.sum(jnp.where(lane_hit, table[row_of], 0.0), axis=1)  6.68 us
    ppermute x4, starting transfers between devices, edge_halos(): lax.ppermute(jnp.where(low, first_row, last_row), ('lon', 'lat'), ccw_pairs)  6.57 us
    another operation x4, local copies, waits for them, and re-layouts, edge_halos(): jnp.stack([north_row, south_row], axis=-1)  5.76 us
  transfers between devices with their start and end apart: 21, of which 3 were waited for; matrix products, arithmetic and copies ran while one was open for 19% of the time, Pallas kernels for 5%

profile of v2, /device:TPU:0, one launch (start us, length us, event | category | flops | bytes accessed | tf_op | source)
XLA Modules:
  0.0 158.3 jit_solution(9506585853784919733)
XLA Ops:
  0.6 1.9 %fusion.25 = (f32[4,32,1,128]{3,2,1,0:T(1,128)}, f32[4,32,1,128]{3,2,1,0:T(1,128)}) fusion(f32[4,32,16,128]{3,2,1,0:T(8,128)} %x_ref.1), kind=kLoop, calls=%fused_computation.78 | loop fusion | bytes 262144 | tf_op jit(solution)/shard_map/slice | solution.py:209
  2.6 1.3 collective-permute-start.2
  4.6 1.0 convert_reduce_fusion
  7.8 1.9 %select_reduce_fusion = f32[2048,3]{0,1:T(4,128)S(1)} fusion(f32[512,3]{0,1:T(4,128)S(1)} %pad_maximum_fusion.6, pred[2048,512]{1,0:T(8,128)(4,1)S(1)} %iota_compare_fusion), kind=kLoop, calls=%fused_computation.2 | loop fusion | flops 6285312 | bytes 1079296 | tf_op jit(solution)/shard_map/reduce_sum | solution.py:243
  10.5 12.5 %all-to-all-start = ((f32[64,32,3]{1,2,0:T(4,128)}), f32[64,32,3]{1,2,0:T(4,128)S(1)}, u32[]{:S(2)}, u32[]{:S(2)}) async-start(f32[64,32,3]{1,2,0:T(4,128)} %copy.783), calls=%async_computation | async-start | bytes 262144 | tf_op jit(solution)/shard_map/all_to_all | solution.py:244
  23.9 3.2 %collective-permute-start.1 = (f32[4,32,16]{1,2,0:T(8,128)S(1)}, f32[4,32,16]{1,2,0:T(8,128)S(1)}, u32[]{:S(2)}, u32[]{:S(2)}) collective-permute-start(f32[4,32,16]{1,2,0:T(8,128)S(1)} %bitcast.92), channel_id=1, source_target_pairs={{1,0},{2,1},{3,2},{131,3},{130,131},{129,130},{128,129},{0,128},{5... | collective-permute-start | bytes 24584 | tf_op jit(solution)/shard_map/ppermute | solution.py:82
  28.6 3.6 %collective-permute-start.9 = (f32[4,32,16]{1,2,0:T(8,128)S(1)}, f32[4,32,16]{1,2,0:T(8,128)}, u32[]{:S(2)}, u32[]{:S(2)}) collective-permute-start(f32[4,32,16]{1,2,0:T(8,128)S(1)} %bitcast.91), channel_id=1, source_target_pairs={{1,0},{2,1},{3,2},{131,3},{130,131},{129,130},{128,129},{0,128},{5... | collective-permute-start | bytes 24584 | tf_op jit(solution)/shard_map/ppermute | solution.py:40
  33.5 1.5 fusion.24
  34.9 1.3 fusion.22
  37.1 7.9 %collective-permute-start.3 = (f32[4,32,128]{2,1,0:T(8,128)}, f32[4,32,128]{2,1,0:T(8,128)}, u32[]{:S(2)}, u32[]{:S(2)}) collective-permute-start(f32[4,32,128]{2,1,0:T(8,128)} %bitcast.6), channel_id=1, source_target_pairs={{4,0},{8,4},{12,8},{16,12},{20,16},{24,20},{28,24},{32,28},{36,32}... | collective-permute-start | bytes 196616 | tf_op jit(solution)/shard_map/ppermute | solution.py:77
  45.6 3.0 %collective-permute-start.10 = (f32[4,32,128]{2,1,0:T(8,128)}, f32[4,32,128]{2,1,0:T(8,128)}, u32[]{:S(2)}, u32[]{:S(2)}) collective-permute-start(f32[4,32,128]{2,1,0:T(8,128)} %bitcast.31), channel_id=1, source_target_pairs={{0,4},{4,8},{8,12},{12,16},{16,20},{20,24},{24,28},{28,32},{32,36}... | collective-permute-start | bytes 196616 | tf_op jit(solution)/shard_map/ppermute | solution.py:32
  48.6 1.4 fusion.12
  51.2 1.2 fusion.10
  53.4 1.4 copy.779.hns
  55.6 8.2 %shard_map.104 = (f32[4,32,16,128]{3,2,1,0:T(8,128)}, f32[4,32,16,128]{3,2,1,0:T(8,128)}, f32[4,32,1,128]{3,2,1,0:T(1,128)}, f32[4,32,1,128]{3,2,1,0:T(1,128)}, f32[4,32,16,2]{3,2,1,0:T(8,128)}) custom-call(f32[512]{0:T(512)} %reshape.106.cpl.refs_0_, f32[4,32,16,128]{3,2,1,0:T(8,128)} %x_ref.1, f32[4,32,16,128]{3,2,1,0:T(8,128)} %refs_2_.3, ...), custom_call_target="tpu_custom_call" | custom-call | tf_op jit(solution)/shard_map/pallas_call | solution.py:187
  63.9 7.7 %collective-permute-start.7 = (f32[4,32,128]{2,1,0:T(8,128)}, f32[4,32,128]{2,1,0:T(8,128)}, u32[]{:S(2)}, u32[]{:S(2)}) collective-permute-start(f32[4,32,128]{2,1,0:T(8,128)} %bitcast.104), channel_id=1, source_target_pairs={{4,0},{8,4},{12,8},{16,12},{20,16},{24,20},{28,24},{32,28},{36,32}... | collective-permute-start | bytes 196616 | tf_op jit(solution)/shard_map/ppermute | solution.py:77
  71.7 2.0 %slice_select_fusion.7 = (f32[4,32,16,1]{3,2,1,0:T(8,128)S(1)}, f32[4,32,16,1]{3,2,1,0:T(8,128)S(1)}) fusion(f32[4,32,16,2]{3,2,1,0:T(8,128)} %get-tuple-element.15, pred[]{:T(512)S(6)} %lt.44), kind=kLoop, calls=%fused_computation.26 | loop fusion | flops 4096 | bytes 32769 | tf_op jit(solution)/shard_map/jit(_where)/select_n | solution.py:81
  74.2 1.1 copy.781
  75.8 2.1 %fusion.refs_3_ = f32[4,32,16,128]{3,2,1,0:T(8,128)} fusion(f32[4,32,1,128]{3,2,1,0:T(1,128)} %bitcast.34, f32[4,32,15,128]{3,2,1,0:T(8,128)S(1)} %copy-done.4, f32[4,32,15,128]{3,2,1,0:T(8,128)S(1)} %copy-done.3, f32[4,32,1,128]{3,2,1,0:T(1,128)} %bitcast.32, f32[1,32,16,128]{3,2,1,0:T(8,128)S(1)} %fusion.10, f32[1,32,16,128]{3,2,1,0:T(8,128)} %fusion.11), kind=kLoop, calls=%fused_computation.7 | loop fusion | flops 3407872 | bytes 3670016 | tf_op jit(solution)/shard_map/stack | solution.py:264
  77.9 2.8 %collective-permute-done.4 = f32[4,32,16]{1,2,0:T(8,128)S(1)} collective-permute-done((f32[4,32,16]{1,2,0:T(8,128)S(1)}, f32[4,32,16]{1,2,0:T(8,128)S(1)}, u32[]{:S(2)}, u32[]{:S(2)}) %collective-permute-start.4) | collective-permute-done | bytes 8224 | tf_op jit(solution)/shard_map/ppermute | solution.py:81
  80.8 1.4 copy.782.hns
  82.8 8.2 %shard_map.105 = (f32[4,32,16,128]{3,2,1,0:T(8,128)}, f32[4,32,16,128]{3,2,1,0:T(8,128)}, f32[4,32,1,128]{3,2,1,0:T(1,128)}, f32[4,32,1,128]{3,2,1,0:T(1,128)}, f32[4,32,16,2]{3,2,1,0:T(8,128)}) custom-call(f32[512]{0:T(512)} %reshape.106.cpl.refs_0_, f32[4,32,16,128]{3,2,1,0:T(8,128)} %get-tuple-element.14.x_ref, f32[4,32,16,128]{3,2,1,0:T(8,128)} %refs_2_.3, ...), custom_call_target="tpu_custom_call" | custom-call | tf_op jit(solution)/shard_map/pallas_call | solution.py:187
  91.1 6.7 %gather_fusion = f32[2048,128]{1,0:T(8,128)S(1)} fusion(f32[2048,128]{1,0:T(8,128)} %bitcast.76, s32[2048]{0:T(1024)S(1)} %copy-done.13), kind=kCustom, calls=%fused_computation | custom fusion | bytes 2105344 | tf_op jit(solution)/shard_map/gather | solution.py:253
  98.5 14.8 %scatter_custom_fusion = f32[2048,128]{1,0:T(8,128)S(1)} fusion(s32[2048]{0:T(1024)S(1)} %bitcast.100, f32[2048]{0:T(1024)S(1)} %bitcast.87, s32[2048]{0:T(1024)S(1)} %bitcast.79, f32[]{:T(128)} %constant.46.clone.1), kind=kCustom, calls=%fused_computation.14 | custom fusion | flops 786432 | bytes 1065984 | tf_op jit(solution)/shard_map/scatter-add | solution.py:256
  115.9 7.7 %collective-permute-start.15 = (f32[4,32,128]{2,1,0:T(8,128)S(1)}, f32[4,32,128]{2,1,0:T(8,128)S(1)}, u32[]{:S(2)}, u32[]{:S(2)}) collective-permute-start(f32[4,32,128]{2,1,0:T(8,128)S(1)} %bitcast.85), channel_id=1, source_target_pairs={{4,0},{8,4},{12,8},{16,12},{20,16},{24,20},{28,24},{32,28},{36,32}... | collective-permute-start | bytes 196616 | tf_op jit(solution)/shard_map/ppermute | solution.py:77
  123.8 1.4 copy.793.refs_5_
  126.6 8.1 %shard_map.106 = (f32[4,32,16,128]{3,2,1,0:T(8,128)}, f32[4,32,1,128]{3,2,1,0:T(1,128)}, f32[4,32,1,128]{3,2,1,0:T(1,128)}, f32[4,32,16,2]{3,2,1,0:T(8,128)}) custom-call(f32[512]{0:T(512)} %reshape.106.cpl.refs_0_, f32[4,32,16,128]{3,2,1,0:T(8,128)} %copy-done.1, f32[4,32,16,128]{3,2,1,0:T(8,128)} %refs_2_.3, f32[4,32,16,128]{3,2,1,0:T(8,128)} %fusion.refs_3_, ...), custom_call_target="tpu_custom_call" | custom-call | tf_op jit(solution)/shard_map/pallas_call | solution.py:199
  134.6 1.9 %slice_select_fusion.3 = (f32[4,32,16,1]{3,2,1,0:T(8,128)S(1)}, f32[4,32,16,1]{3,2,1,0:T(8,128)S(1)}) fusion(f32[4,32,16,2]{3,2,1,0:T(8,128)} %get-tuple-element.22, pred[]{:T(512)S(6)} %lt.44), kind=kLoop, calls=%fused_computation.22 | loop fusion | flops 4096 | bytes 32769 | tf_op jit(solution)/shard_map/jit(_where)/select_n | solution.py:81
  137.6 2.4 %collective-permute-start.17 = (f32[4,32,16]{1,2,0:T(8,128)S(1)}, f32[4,32,16]{1,2,0:T(8,128)S(1)}, u32[]{:S(2)}, u32[]{:S(2)}) collective-permute-start(f32[4,32,16]{1,2,0:T(8,128)S(1)} %bitcast.98), channel_id=1, source_target_pairs={{1,0},{2,1},{3,2},{131,3},{130,131},{129,130},{128,129},{0,128},{5... | collective-permute-start | bytes 24584 | tf_op jit(solution)/shard_map/ppermute | solution.py:82
  140.0 9.0 %collective-permute-start.19 = (f32[4,32,128]{2,1,0:T(8,128)S(1)}, f32[4,32,128]{2,1,0:T(8,128)S(1)}, u32[]{:S(2)}, u32[]{:S(2)}) collective-permute-start(f32[4,32,128]{2,1,0:T(8,128)S(1)} %bitcast.106), channel_id=1, source_target_pairs={{4,0},{8,4},{12,8},{16,12},{20,16},{24,20},{28,24},{32,28},{36,32}... | collective-permute-start | bytes 196616 | tf_op jit(solution)/shard_map/ppermute | solution.py:77
  149.1 1.4 copy.796.refs_5_
  151.8 6.4 %shard_map.107 = (f32[4,32,16,128]{3,2,1,0:T(8,128)}, f32[4,32,1,128]{3,2,1,0:T(1,128)}, f32[4,32,1,128]{3,2,1,0:T(1,128)}, f32[4,32,16,2]{3,2,1,0:T(8,128)}) custom-call(f32[512]{0:T(512)} %reshape.106.cpl.refs_0_, f32[4,32,16,128]{3,2,1,0:T(8,128)} %get-tuple-element.21.refs_1_, f32[4,32,16,128]{3,2,1,0:T(8,128)} %refs_2_.3, ...), custom_call_target="tpu_custom_call" | custom-call | tf_op jit(solution)/shard_map/pallas_call | solution.py:199
  (118 shorter events, 19.7 us)
Async XLA Ops:
  0.6 7.2 %copy-start.19 = (f32[1,512]{1,0:T(1,128)S(1)}, f32[1,512]{1,0:T(1,128)}, u32[]{:S(2)}) copy-start(f32[1,512]{1,0:T(1,128)} %param.15) | copy-start | bytes 6148
  0.6 7.2 %copy-start.18 = (f32[1,512]{1,0:T(1,128)S(1)}, f32[1,512]{1,0:T(1,128)}, u32[]{:S(2)}) copy-start(f32[1,512]{1,0:T(1,128)} %param.14) | copy-start | bytes 6148
  2.6 53.0 %collective-permute-start.2 = (f32[4,32,128]{2,1,0:T(8,128)}, f32[4,32,128]{2,1,0:T(8,128)}, u32[]{:S(2)}, u32[]{:S(2)}) collective-permute-start(f32[4,32,128]{2,1,0:T(8,128)} %bitcast.4), channel_id=1, source_target_pairs={{0,4},{4,8},{8,12},{12,16},{16,20},{20,24},{24,28},{28,32},{32,36}... | collective-permute-start | bytes 196616 | tf_op jit(solution)/shard_map/ppermute | solution.py:76
  7.8 15.3 %copy-start.2 = (f32[4,32,16,128]{3,2,1,0:T(8,128)S(1)}, f32[4,32,16,128]{3,2,1,0:T(8,128)}, u32[]{:S(2)}) copy-start(f32[4,32,16,128]{3,2,1,0:T(8,128)} %x_ref.1) | copy-start | bytes 3145732
  10.5 44.3 %all-to-all-start = ((f32[64,32,3]{1,2,0:T(4,128)}), f32[64,32,3]{1,2,0:T(4,128)S(1)}, u32[]{:S(2)}, u32[]{:S(2)}) async-start(f32[64,32,3]{1,2,0:T(4,128)} %copy.783), calls=%async_computation | async-start | bytes 262144 | tf_op jit(solution)/shard_map/all_to_all | solution.py:244
  23.4 4.3 %copy-start = (f32[4,32,16,128]{3,2,1,0:T(8,128)S(1)}, f32[4,32,16,128]{3,2,1,0:T(8,128)}, u32[]{:S(2)}) copy-start(f32[4,32,16,128]{3,2,1,0:T(8,128)} %refs_2_.3) | copy-start | bytes 3145732
  23.9 13.2 %collective-permute-start.1 = (f32[4,32,16]{1,2,0:T(8,128)S(1)}, f32[4,32,16]{1,2,0:T(8,128)S(1)}, u32[]{:S(2)}, u32[]{:S(2)}) collective-permute-start(f32[4,32,16]{1,2,0:T(8,128)S(1)} %bitcast.92), channel_id=1, source_target_pairs={{1,0},{2,1},{3,2},{131,3},{130,131},{129,130},{128,129},{0,128},{5... | collective-permute-start | bytes 24584 | tf_op jit(solution)/shard_map/ppermute | solution.py:82
  27.6 17.4 %collective-permute-start = (f32[4,32,16]{1,2,0:T(8,128)S(1)}, f32[4,32,16]{1,2,0:T(8,128)S(1)}, u32[]{:S(2)}, u32[]{:S(2)}) collective-permute-start(f32[4,32,16]{1,2,0:T(8,128)S(1)} %bitcast.90), channel_id=1, source_target_pairs={{0,1},{1,2},{2,3},{3,131},{131,130},{130,129},{129,128},{128,0},{4... | collective-permute-start | bytes 24584 | tf_op jit(solution)/shard_map/ppermute | solution.py:81
  28.6 17.1 %collective-permute-start.9 = (f32[4,32,16]{1,2,0:T(8,128)S(1)}, f32[4,32,16]{1,2,0:T(8,128)}, u32[]{:S(2)}, u32[]{:S(2)}) collective-permute-start(f32[4,32,16]{1,2,0:T(8,128)S(1)} %bitcast.91), channel_id=1, source_target_pairs={{1,0},{2,1},{3,2},{131,3},{130,131},{129,130},{128,129},{0,128},{5... | collective-permute-start | bytes 24584 | tf_op jit(solution)/shard_map/ppermute | solution.py:40
  32.7 16.0 %collective-permute-start.8 = (f32[4,32,16]{1,2,0:T(8,128)S(1)}, f32[4,32,16]{1,2,0:T(8,128)S(1)}, u32[]{:S(2)}, u32[]{:S(2)}) collective-permute-start(f32[4,32,16]{1,2,0:T(8,128)S(1)} %bitcast.89), channel_id=1, source_target_pairs={{0,1},{1,2},{2,3},{3,131},{131,130},{130,129},{129,128},{128,0},{4... | collective-permute-start | bytes 24584 | tf_op jit(solution)/shard_map/ppermute | solution.py:39
  34.9 13.7 %copy-start.14 = (f32[4]{0:T(128)S(1)}, f32[4]{0:T(128)}, u32[]{:S(2)}) copy-start(f32[4]{0:T(128)} %constant.53.clone) | copy-start | bytes 52
  37.1 18.5 %collective-permute-start.3 = (f32[4,32,128]{2,1,0:T(8,128)}, f32[4,32,128]{2,1,0:T(8,128)}, u32[]{:S(2)}, u32[]{:S(2)}) collective-permute-start(f32[4,32,128]{2,1,0:T(8,128)} %bitcast.6), channel_id=1, source_target_pairs={{4,0},{8,4},{12,8},{16,12},{20,16},{24,20},{28,24},{32,28},{36,32}... | collective-permute-start | bytes 196616 | tf_op jit(solution)/shard_map/ppermute | solution.py:77
  45.1 30.2 %collective-permute-start.11 = (f32[4,32,128]{2,1,0:T(8,128)}, f32[4,32,128]{2,1,0:T(8,128)}, u32[]{:S(2)}, u32[]{:S(2)}) collective-permute-start(f32[4,32,128]{2,1,0:T(8,128)} %bitcast.33), channel_id=1, source_target_pairs={{4,0},{8,4},{12,8},{16,12},{20,16},{24,20},{28,24},{32,28},{36,32}... | collective-permute-start | bytes 196616 | tf_op jit(solution)/shard_map/ppermute | solution.py:33
  45.6 30.1 %collective-permute-start.10 = (f32[4,32,128]{2,1,0:T(8,128)}, f32[4,32,128]{2,1,0:T(8,128)}, u32[]{:S(2)}, u32[]{:S(2)}) collective-permute-start(f32[4,32,128]{2,1,0:T(8,128)} %bitcast.31), channel_id=1, source_target_pairs={{0,4},{4,8},{8,12},{12,16},{16,20},{20,24},{24,28},{28,32},{32,36}... | collective-permute-start | bytes 196616 | tf_op jit(solution)/shard_map/ppermute | solution.py:32
  63.9 18.3 %collective-permute-start.6 = (f32[4,32,128]{2,1,0:T(8,128)}, f32[4,32,128]{2,1,0:T(8,128)S(1)}, u32[]{:S(2)}, u32[]{:S(2)}) collective-permute-start(f32[4,32,128]{2,1,0:T(8,128)} %bitcast.105), channel_id=1, source_target_pairs={{0,4},{4,8},{8,12},{12,16},{16,20},{20,24},{24,28},{28,32},{32,36}... | collective-permute-start | bytes 196616 | tf_op jit(solution)/shard_map/ppermute | solution.py:76
  63.9 18.3 %collective-permute-start.7 = (f32[4,32,128]{2,1,0:T(8,128)}, f32[4,32,128]{2,1,0:T(8,128)}, u32[]{:S(2)}, u32[]{:S(2)}) collective-permute-start(f32[4,32,128]{2,1,0:T(8,128)} %bitcast.104), channel_id=1, source_target_pairs={{4,0},{8,4},{12,8},{16,12},{20,16},{24,20},{28,24},{32,28},{36,32}... | collective-permute-start | bytes 196616 | tf_op jit(solution)/shard_map/ppermute | solution.py:77
  75.3 2.7 %collective-permute-start.5 = (f32[4,32,16]{1,2,0:T(8,128)}, f32[4,32,16]{1,2,0:T(8,128)S(1)}, u32[]{:S(2)}, u32[]{:S(2)}) collective-permute-start(f32[4,32,16]{1,2,0:T(8,128)} %bitcast.95), channel_id=1, source_target_pairs={{1,0},{2,1},{3,2},{131,3},{130,131},{129,130},{128,129},{0,128},{5... | collective-permute-start | bytes 24584 | tf_op jit(solution)/shard_map/ppermute | solution.py:82
  75.3 5.4 %collective-permute-start.4 = (f32[4,32,16]{1,2,0:T(8,128)S(1)}, f32[4,32,16]{1,2,0:T(8,128)S(1)}, u32[]{:S(2)}, u32[]{:S(2)}) collective-permute-start(f32[4,32,16]{1,2,0:T(8,128)S(1)} %bitcast.93), channel_id=1, source_target_pairs={{0,1},{1,2},{2,3},{3,131},{131,130},{130,129},{129,128},{128,0},{4... | collective-permute-start | bytes 24584 | tf_op jit(solution)/shard_map/ppermute | solution.py:81
  75.8 4.9 %copy-start.15 = (f32[4]{0:T(128)S(1)}, f32[4]{0:T(128)}, u32[]{:S(2)}) copy-start(f32[4]{0:T(128)} %constant.53.clone) | copy-start | bytes 52
  82.8 8.3 %copy-start.13 = (s32[2048]{0:T(1024)S(1)}, s32[2048]{0:T(1024)}, u32[]{:S(2)}) copy-start(s32[2048]{0:T(1024)} %broadcast_clamp_fusion) | copy-start | bytes 24580
  97.8 15.5 %copy-start.5 = (f32[4,32,16,128]{3,2,1,0:T(8,128)S(1)}, f32[4,32,16,128]{3,2,1,0:T(8,128)}, u32[]{:S(2)}) copy-start(f32[4,32,16,128]{3,2,1,0:T(8,128)} %get-tuple-element.19) | copy-start | bytes 3145732
  113.8 9.9 %copy-start.16 = (f32[4]{0:T(128)S(1)}, f32[4]{0:T(128)}, u32[]{:S(2)}) copy-start(f32[4]{0:T(128)} %constant.53.clone) | copy-start | bytes 52
  114.8 8.9 %collective-permute-start.13 = (f32[4,32,16]{1,2,0:T(8,128)S(1)}, f32[4,32,16]{1,2,0:T(8,128)S(1)}, u32[]{:S(2)}, u32[]{:S(2)}) collective-permute-start(f32[4,32,16]{1,2,0:T(8,128)S(1)} %bitcast.97), channel_id=1, source_target_pairs={{1,0},{2,1},{3,2},{131,3},{130,131},{129,130},{128,129},{0,128},{5... | collective-permute-start | bytes 24584 | tf_op jit(solution)/shard_map/ppermute | solution.py:82
  115.7 7.9 %collective-permute-start.12 = (f32[4,32,16]{1,2,0:T(8,128)S(1)}, f32[4,32,16]{1,2,0:T(8,128)S(1)}, u32[]{:S(2)}, u32[]{:S(2)}) collective-permute-start(f32[4,32,16]{1,2,0:T(8,128)S(1)} %bitcast.94), channel_id=1, source_target_pairs={{0,1},{1,2},{2,3},{3,131},{131,130},{130,129},{129,128},{128,0},{4... | collective-permute-start | bytes 24584 | tf_op jit(solution)/shard_map/ppermute | solution.py:81
  115.8 10.1 %collective-permute-start.14 = (f32[4,32,128]{2,1,0:T(8,128)S(1)}, f32[4,32,128]{2,1,0:T(8,128)S(1)}, u32[]{:S(2)}, u32[]{:S(2)}) collective-permute-start(f32[4,32,128]{2,1,0:T(8,128)S(1)} %bitcast.86), channel_id=1, source_target_pairs={{0,4},{4,8},{8,12},{12,16},{16,20},{20,24},{24,28},{28,32},{32,36}... | collective-permute-start | bytes 196616 | tf_op jit(solution)/shard_map/ppermute | solution.py:76
  115.9 10.0 %collective-permute-start.15 = (f32[4,32,128]{2,1,0:T(8,128)S(1)}, f32[4,32,128]{2,1,0:T(8,128)S(1)}, u32[]{:S(2)}, u32[]{:S(2)}) collective-permute-start(f32[4,32,128]{2,1,0:T(8,128)S(1)} %bitcast.85), channel_id=1, source_target_pairs={{4,0},{8,4},{12,8},{16,12},{20,16},{24,20},{28,24},{32,28},{36,32}... | collective-permute-start | bytes 196616 | tf_op jit(solution)/shard_map/ppermute | solution.py:77
  136.6 3.4 %copy-start.21 = (f32[4,32,1,128]{3,2,1,0:T(1,128)S(1)}, f32[4,32,1,128]{3,2,1,0:T(1,128)}, u32[]{:S(2)}) copy-start(f32[4,32,1,128]{3,2,1,0:T(1,128)} %get-tuple-element.23) | copy-start | bytes 196612
  136.6 3.4 %copy-start.20 = (f32[4,32,1,128]{3,2,1,0:T(1,128)S(1)}, f32[4,32,1,128]{3,2,1,0:T(1,128)}, u32[]{:S(2)}) copy-start(f32[4,32,1,128]{3,2,1,0:T(1,128)} %get-tuple-element.24) | copy-start | bytes 196612
  137.6 11.4 %collective-permute-start.17 = (f32[4,32,16]{1,2,0:T(8,128)S(1)}, f32[4,32,16]{1,2,0:T(8,128)S(1)}, u32[]{:S(2)}, u32[]{:S(2)}) collective-permute-start(f32[4,32,16]{1,2,0:T(8,128)S(1)} %bitcast.98), channel_id=1, source_target_pairs={{1,0},{2,1},{3,2},{131,3},{130,131},{129,130},{128,129},{0,128},{5... | collective-permute-start | bytes 24584 | tf_op jit(solution)/shard_map/ppermute | solution.py:82
  140.0 9.0 %collective-permute-start.16 = (f32[4,32,16]{1,2,0:T(8,128)S(1)}, f32[4,32,16]{1,2,0:T(8,128)S(1)}, u32[]{:S(2)}, u32[]{:S(2)}) collective-permute-start(f32[4,32,16]{1,2,0:T(8,128)S(1)} %bitcast.96), channel_id=1, source_target_pairs={{0,1},{1,2},{2,3},{3,131},{131,130},{130,129},{129,128},{128,0},{4... | collective-permute-start | bytes 24584 | tf_op jit(solution)/shard_map/ppermute | solution.py:81
  140.0 11.2 %collective-permute-start.18 = (f32[4,32,128]{2,1,0:T(8,128)S(1)}, f32[4,32,128]{2,1,0:T(8,128)S(1)}, u32[]{:S(2)}, u32[]{:S(2)}) collective-permute-start(f32[4,32,128]{2,1,0:T(8,128)S(1)} %bitcast.107), channel_id=1, source_target_pairs={{0,4},{4,8},{8,12},{12,16},{16,20},{20,24},{24,28},{28,32},{32,36}... | collective-permute-start | bytes 196616 | tf_op jit(solution)/shard_map/ppermute | solution.py:76
  140.0 11.2 %collective-permute-start.19 = (f32[4,32,128]{2,1,0:T(8,128)S(1)}, f32[4,32,128]{2,1,0:T(8,128)S(1)}, u32[]{:S(2)}, u32[]{:S(2)}) collective-permute-start(f32[4,32,128]{2,1,0:T(8,128)S(1)} %bitcast.106), channel_id=1, source_target_pairs={{4,0},{8,4},{12,8},{16,12},{20,16},{24,20},{28,24},{32,28},{36,32}... | collective-permute-start | bytes 196616 | tf_op jit(solution)/shard_map/ppermute | solution.py:77
  (11 other events, 12.5 us)

commit v3 on v2

--- a/solution.py
+++ b/solution.py
@@ -84,7 +84,7 @@
     south_row = jnp.where(low, ccw, cw)
     north_row = jnp.where(lat_j == 0, flip * north_row, north_row)
     south_row = jnp.where(lat_j == n_lat - 1, flip * south_row, south_row)
-    return (jnp.stack([north_row, south_row], axis=-1), from_west[:, :, None, :], from_east[:, :, None, :])
+    return (jnp.stack([north_row, south_row], axis=-1), from_west, from_east)
 
 
 def edge_masks(shape):
@@ -104,8 +104,8 @@
 
 
 def write_edges(v, f, l, fc, lc, frl):
-    fc[f, l] = v[0:1, :]
-    lc[f, l] = v[-1:, :]
+    fc[f, pl.ds(l, 1), :] = v[0:1, :]
+    lc[f, pl.ds(l, 1), :] = v[-1:, :]
     frl[f, l, :, 0:1] = v[:, 0:1]
     frl[f, l, :, 1:2] = v[:, -1:]
 
@@ -121,7 +121,7 @@
         total = cs[0] + cs[1] + cs[2] + cs[3]
         for g in range(nf):
             v = xs[g]
-            north, south, west, east = neighbours_2d(v, masks, hns[g, l, :, 0:1], hns[g, l, :, 1:2], hw[g, l], he[g, l])
+            north, south, west, east = neighbours_2d(v, masks, hns[g, l, :, 0:1], hns[g, l, :, 1:2], hw[g, pl.ds(l, 1), :], he[g, pl.ds(l, 1), :])
             mixed = cpl[lev * nf * nf + g * nf] * xs[0]
             for f in range(1, nf):
                 mixed = mixed + cpl[lev * nf * nf + g * nf + f] * xs[f]
@@ -148,7 +148,7 @@
         bs = [b_ref[d, l] for d in range(4)]
         for o in range(nf):
             v = ls[o]
-            north, south, west, east = neighbours_2d(v, masks, hns[o, l, :, 0:1], hns[o, l, :, 1:2], hw[o, l], he[o, l])
+            north, south, west, east = neighbours_2d(v, masks, hns[o, l, :, 0:1], hns[o, l, :, 1:2], hw[o, pl.ds(l, 1), :], he[o, pl.ds(l, 1), :])
             back = cpl[lev * nf * nf + o] * ls[0]
             for g in range(1, nf):
                 back = back + cpl[lev * nf * nf + g * nf + o] * ls[g]
@@ -167,8 +167,8 @@
 def edge_shapes(x):
     f, l, c, r = x.shape
     return [
-        jax.ShapeDtypeStruct((f, l, 1, r), x.dtype),
-        jax.ShapeDtypeStruct((f, l, 1, r), x.dtype),
+        jax.ShapeDtypeStruct((f, l, r), x.dtype),
+        jax.ShapeDtypeStruct((f, l, r), x.dtype),
         jax.ShapeDtypeStruct((f, l, c, 2), x.dtype),
     ]
 
@@ -177,7 +177,7 @@
     specs = []
     for a in arrays:
         block = (a.shape[0], LEVEL_BLOCK) + tuple(a.shape[2:])
-        specs.append(pl.BlockSpec(block, lambda i: (0, i, 0, 0)))
+        specs.append(pl.BlockSpec(block, lambda i, n=len(block): (0, i) + (0,) * (n - 2)))
     return specs
 
 
@@ -211,7 +211,7 @@
 
 def squeezed(edges):
     fc, lc, frl = edges
-    return (fc[:, :, 0, :], lc[:, :, 0, :], frl[..., 0], frl[..., 1])
+    return (fc, lc, frl[..., 0], frl[..., 1])
 
 
 def on_device(
@@ -248,12 +248,15 @@
     lanes = x.shape[3]
     row_of = cells // lanes
     lane_of = cells % lanes
-    table = x.reshape(-1, lanes)
     lane_hit = lane_of[:, None] == jnp.arange(lanes, dtype=jnp.int32)[None, :]
-    picked = jnp.sum(jnp.where(lane_hit, table[row_of], 0.0), axis=1)
-    forcing = weights * (picked - values)
-    spread = jnp.where(lane_hit, forcing[:, None], 0.0)
-    lam = jnp.zeros_like(table).at[row_of].add(spread).reshape(x.shape)
+    spread = jnp.concatenate(
+        [jnp.where(lane_hit, weights[:, None], 0.0), jnp.where(lane_hit, (weights * values)[:, None], 0.0)],
+        axis=1,
+    )
+    sums = jnp.zeros((x.size // lanes, 2 * lanes), x.dtype).at[row_of].add(spread)
+    weight_sum = sums[:, :lanes].reshape(x.shape)
+    weighted_values = sums[:, lanes:].reshape(x.shape)
+    lam = x * weight_sum - weighted_values
 
     near_n, near_s, near_w, near_e = shifted(coefficients, halos(coefficients, plain_flip))
     row_ids = jnp.arange(coefficients.shape[3], dtype=jnp.int32)[None, :]

time: 159 us -> 159 us (level)
  starting transfers between devices: 60.7 us -> 69.1 us
  local copies, waits for them, and re-layouts: 28.5 us -> 22.7 us
  waiting for transfers between devices: 4.13 us -> 1.47 us
    ppermute x4, starting transfers between devices: 6.57 us -> 14.3 us  [edge_halos(): lax.ppermute(jnp.where(low, first_row, last_row), ('lon', 'lat'), ccw_pairs)]
    ppermute x1, starting transfers between devices: 0.56 us -> 7.74 us  [halos(): from_east = lax.ppermute(x[:, :, 0, :], 'lon', down)]
    gather x1 -> x0, local copies, waits for them, and re-layouts: 6.68 us -> none  [on_device(): picked = jnp.sum(jnp.where(lane_hit, table[row_of], 0.0), axis=1)]
    ppermute x1, starting transfers between devices: 2.97 us -> 0.01 us  [halos(): from_west = lax.ppermute(x[:, :, -1, :], 'lon', up)]
    ppermute x4, waiting for transfers between devices: 2.78 us -> 0.01 us  [edge_halos(): lax.ppermute(jnp.where(low, last_row, first_row), ('lon', 'lat'), cw_pairs)]
    select_n x1 -> x2, other arithmetic: 0.05 us -> 2.44 us  [the longest x1 2.39 us: on_device(): jnp.where(lane_hit, weights[:, None], 0.0)]
    scatter-add x1, other arithmetic: 14.8 us -> 12.9 us  [on_device(): jnp.zeros((x.size // lanes, 2 * lanes), x.dtype).at[row_of].add(spread)]
    mul x1, other arithmetic: 0.14 us -> 1.81 us  [on_device(): lam_y = lam * factors[STEPS - 1]]
  transfers between devices with their start and end apart: 21 -> 21, of which waited for: 3 -> 2; matrix products, arithmetic and copies ran while one was open for 19% -> 28% of each run, Pallas kernels for 5% -> 5%
where the time goes in v3:
time: 159 us; the launch traced here: 158 us
  starting transfers between devices  69.1 us (43%)
  other arithmetic  31.9 us (20%)
  Pallas kernels  31 us (19%)
  local copies, waits for them, and re-layouts  22.7 us (14%)
  between operations  1.82 us (1%)
    ppermute x4, starting transfers between devices, edge_halos(): from_east = lax.ppermute(first_col, 'lon', down)  30.8 us
    pallas_call x2, Pallas kernels, forward_step(): pl.pallas_call(forward_kernel, out_shape=outs, grid=(x.shape[1] // LEVEL_...  16.4 us
    pallas_call x2, Pallas kernels, backward_step(): pl.pallas_call(lambda *refs: backward_kernel(*refs, last=last), out_shape...  14.5 us
    ppermute x4, starting transfers between devices, edge_halos(): lax.ppermute(jnp.where(low, first_row, last_row), ('lon', 'lat'), ccw_pairs)  14.3 us
    scatter-add x1, other arithmetic, on_device(): jnp.zeros((x.size // lanes, 2 * lanes), x.dtype).at[row_of].add(spread)  12.9 us
    all_to_all x1, starting transfers between devices, on_device(): arrived = lax.all_to_all(send, 'lon', 0, 0, tiled=True)  10.9 us
    ppermute x1, starting transfers between devices, halos(): from_east = lax.ppermute(x[:, :, 0, :], 'lon', down)  7.74 us
    select_n x4, other arithmetic, edge_halos(): jnp.where(low, last_row, first_row)  5.97 us
  transfers between devices with their start and end apart: 21, of which 2 were waited for; matrix products, arithmetic and copies ran while one was open for 28% of the time, Pallas kernels for 5%

profile of v3, /device:TPU:0, one launch (start us, length us, event | category | flops | bytes accessed | tf_op | source)
XLA Modules:
  0.0 158.0 jit_solution(14653808014895753406)
XLA Ops:
  0.6 1.9 %slice_select_fusion.9 = (f32[4,32,16,1]{3,2,1,0:T(8,128)S(1)}, f32[4,32,16,1]{3,2,1,0:T(8,128)S(1)}) fusion(f32[4,32,16,128]{3,2,1,0:T(8,128)} %x_ref.1, pred[]{:T(512)S(6)} %lt.44), kind=kLoop, calls=%fused_computation.32 | loop fusion | flops 4096 | bytes 32769 | tf_op jit(solution)/shard_map/jit(_where)/select_n | solution.py:81
  3.6 3.6 %collective-permute-start.1 = (f32[4,32,16]{1,2,0:T(8,128)S(1)}, f32[4,32,16]{1,2,0:T(8,128)S(1)}, u32[]{:S(2)}, u32[]{:S(2)}) collective-permute-start(f32[4,32,16]{1,2,0:T(8,128)S(1)} %bitcast.72), channel_id=1, source_target_pairs={{1,0},{2,1},{3,2},{131,3},{130,131},{129,130},{128,129},{0,128},{5... | collective-permute-start | bytes 24584 | tf_op jit(solution)/shard_map/ppermute | solution.py:82
  8.7 3.6 %collective-permute-start.9 = (f32[4,32,16]{1,2,0:T(8,128)S(1)}, f32[4,32,16]{1,2,0:T(8,128)S(1)}, u32[]{:S(2)}, u32[]{:S(2)}) collective-permute-start(f32[4,32,16]{1,2,0:T(8,128)S(1)} %bitcast.71), channel_id=1, source_target_pairs={{1,0},{2,1},{3,2},{131,3},{130,131},{129,130},{128,129},{0,128},{5... | collective-permute-start | bytes 24584 | tf_op jit(solution)/shard_map/ppermute | solution.py:40
  12.3 1.9 %fusion.26 = (f32[4,32,1,128]{3,2,1,0:T(1,128)}, f32[4,32,1,128]{3,2,1,0:T(1,128)}) fusion(f32[4,32,16,128]{3,2,1,0:T(8,128)} %x_ref.1), kind=kLoop, calls=%fused_computation.78 | loop fusion | bytes 262144 | tf_op jit(solution)/shard_map/slice | solution.py:209
  14.2 1.3 collective-permute-start.2
  17.3 1.9 %select_reduce_fusion = f32[2048,3]{0,1:T(4,128)S(1)} fusion(f32[512,3]{0,1:T(4,128)S(1)} %pad_maximum_fusion.6, pred[2048,512]{1,0:T(8,128)(4,1)S(1)} %iota_compare_fusion), kind=kLoop, calls=%fused_computation.1 | loop fusion | flops 6285312 | bytes 1079296 | tf_op jit(solution)/shard_map/reduce_sum | solution.py:243
  20.0 10.9 %all-to-all-start = ((f32[64,32,3]{1,2,0:T(4,128)}), f32[64,32,3]{1,2,0:T(4,128)S(1)}, u32[]{:S(2)}, u32[]{:S(2)}) async-start(f32[64,32,3]{1,2,0:T(4,128)} %copy.793), calls=%async_computation | async-start | bytes 262144 | tf_op jit(solution)/shard_map/all_to_all | solution.py:244
  30.9 1.3 fusion.23
  32.3 1.5 fusion.25
  35.3 7.6 %collective-permute-start.3 = (f32[4,32,128]{2,1,0:T(8,128)}, f32[4,32,128]{2,1,0:T(8,128)}, u32[]{:S(2)}, u32[]{:S(2)}) collective-permute-start(f32[4,32,128]{2,1,0:T(8,128)} %bitcast.5), channel_id=1, source_target_pairs={{4,0},{8,4},{12,8},{16,12},{20,16},{24,20},{28,24},{32,28},{36,32}... | collective-permute-start | bytes 196616 | tf_op jit(solution)/shard_map/ppermute | solution.py:77
  43.0 7.7 %collective-permute-start.11 = (f32[4,32,128]{2,1,0:T(8,128)}, f32[4,32,128]{2,1,0:T(8,128)}, u32[]{:S(2)}, u32[]{:S(2)}) collective-permute-start(f32[4,32,128]{2,1,0:T(8,128)} %bitcast.27), channel_id=1, source_target_pairs={{4,0},{8,4},{12,8},{16,12},{20,16},{24,20},{28,24},{32,28},{36,32}... | collective-permute-start | bytes 196616 | tf_op jit(solution)/shard_map/ppermute | solution.py:33
  54.7 1.4 copy.789.hns
  56.4 2.4 %fusion.7 = (f32[2048,128]{1,0:T(8,128)S(1)}, f32[2048,128]{1,0:T(8,128)}) fusion(f32[2048]{0:T(1024)S(1)} %bitcast.69, s32[2048]{0:T(1024)S(1)} %bitcast.68, f32[2048]{0:T(1024)S(1)} %bitcast.70), kind=kLoop, calls=%fused_computation.17 | loop fusion | flops 786432 | bytes 2121728 | tf_op jit(solution)/shard_map/jit(_where)/select_n | solution.py:253
  58.8 12.9 %scatter_custom_fusion = f32[2048,256]{1,0:T(8,128)S(1)} fusion(s32[2048]{0:T(1024)S(1)} %bitcast.83, f32[2048,128]{1,0:T(8,128)} %get-tuple-element.63, f32[]{:T(128)} %constant.61, f32[2048,128]{1,0:T(8,128)S(1)} %get-tuple-element.62, f32[]{:T(128)} %constant.46.clone.1), kind=kCustom, calls=%fused_computation.3 | custom fusion | flops 1048576 | bytes 4194312 | tf_op jit(solution)/shard_map/scatter-add | solution.py:256
  71.7 1.5 fusion.21
  73.2 8.2 %shard_map.104 = (f32[4,32,16,128]{3,2,1,0:T(8,128)}, f32[4,32,16,128]{3,2,1,0:T(8,128)}, f32[4,32,128]{2,1,0:T(8,128)}, f32[4,32,128]{2,1,0:T(8,128)}, f32[4,32,16,2]{3,2,1,0:T(8,128)}) custom-call(f32[512]{0:T(512)} %reshape.105.cpl.refs_0_, f32[4,32,16,128]{3,2,1,0:T(8,128)} %x_ref.1, f32[4,32,16,128]{3,2,1,0:T(8,128)} %refs_2_.3, ...), custom_call_target="tpu_custom_call" | custom-call | tf_op jit(solution)/shard_map/pallas_call | solution.py:187
  81.4 1.9 %slice_select_fusion.7 = (f32[4,32,16,1]{3,2,1,0:T(8,128)S(1)}, f32[4,32,16,1]{3,2,1,0:T(8,128)S(1)}) fusion(f32[4,32,16,2]{3,2,1,0:T(8,128)} %get-tuple-element.15, pred[]{:T(512)S(6)} %lt.44), kind=kLoop, calls=%fused_computation.30 | loop fusion | flops 4096 | bytes 32769 | tf_op jit(solution)/shard_map/jit(_where)/select_n | solution.py:81
  84.4 3.6 %collective-permute-start.5 = (f32[4,32,16]{1,2,0:T(8,128)S(1)}, f32[4,32,16]{1,2,0:T(8,128)S(1)}, u32[]{:S(2)}, u32[]{:S(2)}) collective-permute-start(f32[4,32,16]{1,2,0:T(8,128)S(1)} %bitcast.76), channel_id=1, source_target_pairs={{1,0},{2,1},{3,2},{131,3},{130,131},{129,130},{128,129},{0,128},{5... | collective-permute-start | bytes 24584 | tf_op jit(solution)/shard_map/ppermute | solution.py:82
  88.0 7.7 %collective-permute-start.7 = (f32[4,32,128]{2,1,0:T(8,128)S(1)}, f32[4,32,128]{2,1,0:T(8,128)S(1)}, u32[]{:S(2)}, u32[]{:S(2)}) collective-permute-start(f32[4,32,128]{2,1,0:T(8,128)S(1)} %copy-done.19), channel_id=1, source_target_pairs={{4,0},{8,4},{12,8},{16,12},{20,16},{24,20},{28,24},{32,28},{36,32}... | collective-permute-start | bytes 196616 | tf_op jit(solution)/shard_map/ppermute | solution.py:77
  95.7 2.3 %fusion.4.refs_3_ = f32[4,32,16,128]{3,2,1,0:T(8,128)} fusion(f32[4,32,1,128]{3,2,1,0:T(1,128)} %bitcast.28, f32[4,32,15,128]{3,2,1,0:T(8,128)} %get-tuple-element.43, f32[4,32,15,128]{3,2,1,0:T(8,128)S(1)} %copy-done.4, f32[4,32,1,128]{3,2,1,0:T(1,128)} %bitcast.26, f32[1,32,16,128]{3,2,1,0:T(8,128)S(1)} %fusion.11, f32[1,32,16,128]{3,2,1,0:T(8,128)} %fusion.12), kind=kLoop, calls=%fused_computation.10 | loop fusion | flops 3407872 | bytes 3670016 | tf_op jit(solution)/shard_map/stack | solution.py:267
  98.2 1.4 copy.792.hns
  100.3 8.2 %shard_map.105 = (f32[4,32,16,128]{3,2,1,0:T(8,128)}, f32[4,32,16,128]{3,2,1,0:T(8,128)}, f32[4,32,128]{2,1,0:T(8,128)}, f32[4,32,128]{2,1,0:T(8,128)}, f32[4,32,16,2]{3,2,1,0:T(8,128)}) custom-call(f32[512]{0:T(512)} %reshape.105.cpl.refs_0_, f32[4,32,16,128]{3,2,1,0:T(8,128)} %get-tuple-element.14.x_ref, f32[4,32,16,128]{3,2,1,0:T(8,128)} %refs_2_.3, ...), custom_call_target="tpu_custom_call" | custom-call | tf_op jit(solution)/shard_map/pallas_call | solution.py:187
  108.5 1.8 %subtract_multiply_fusion.refs_1_ = f32[4,32,16,128]{3,2,1,0:T(8,128)S(1)} fusion(f32[4,32,16,128]{3,2,1,0:T(8,128)} %get-tuple-element.19, f32[4,32,16,128]{3,2,1,0:T(8,128)S(1)} %bitcast.65, f32[4,32,16,128]{3,2,1,0:T(8,128)} %get-tuple-element.12, f32[4,32,16,128]{3,2,1,0:T(8,128)S(1)} %bitcast.64), kind=kLoop, calls=%fused_computation.14 | loop fusion | flops 786432 | bytes 5242880 | tf_op jit(solution)/shard_map/mul | solution.py:273
  111.8 3.6 %collective-permute-start.13 = (f32[4,32,16]{1,2,0:T(8,128)S(1)}, f32[4,32,16]{1,2,0:T(8,128)S(1)}, u32[]{:S(2)}, u32[]{:S(2)}) collective-permute-start(f32[4,32,16]{1,2,0:T(8,128)S(1)} %bitcast.78), channel_id=1, source_target_pairs={{1,0},{2,1},{3,2},{131,3},{130,131},{129,130},{128,129},{0,128},{5... | collective-permute-start | bytes 24584 | tf_op jit(solution)/shard_map/ppermute | solution.py:82
  115.5 7.7 %collective-permute-start.15 = (f32[4,32,128]{2,1,0:T(8,128)S(1)}, f32[4,32,128]{2,1,0:T(8,128)S(1)}, u32[]{:S(2)}, u32[]{:S(2)}) collective-permute-start(f32[4,32,128]{2,1,0:T(8,128)S(1)} %bitcast.66), channel_id=1, source_target_pairs={{4,0},{8,4},{12,8},{16,12},{20,16},{24,20},{28,24},{32,28},{36,32}... | collective-permute-start | bytes 196616 | tf_op jit(solution)/shard_map/ppermute | solution.py:77
  123.4 1.4 copy.803.refs_5_
  126.1 8.1 %shard_map.106 = (f32[4,32,16,128]{3,2,1,0:T(8,128)}, f32[4,32,128]{2,1,0:T(8,128)}, f32[4,32,128]{2,1,0:T(8,128)}, f32[4,32,16,2]{3,2,1,0:T(8,128)}) custom-call(f32[512]{0:T(512)} %reshape.105.cpl.refs_0_, f32[4,32,16,128]{3,2,1,0:T(8,128)} %copy-done.1, f32[4,32,16,128]{3,2,1,0:T(8,128)} %refs_2_.3, f32[4,32,16,128]{3,2,1,0:T(8,128)} %fusion.4.refs_3_, ...), custom_call_target="tpu_custom_call" | custom-call | tf_op jit(solution)/shard_map/pallas_call | solution.py:199
  134.2 1.9 %slice_select_fusion.3 = (f32[4,32,16,1]{3,2,1,0:T(8,128)S(1)}, f32[4,32,16,1]{3,2,1,0:T(8,128)S(1)}) fusion(f32[4,32,16,2]{3,2,1,0:T(8,128)} %get-tuple-element.22, pred[]{:T(512)S(6)} %lt.44), kind=kLoop, calls=%fused_computation.26 | loop fusion | flops 4096 | bytes 32769 | tf_op jit(solution)/shard_map/jit(_where)/select_n | solution.py:81
  137.2 3.6 %collective-permute-start.17 = (f32[4,32,16]{1,2,0:T(8,128)S(1)}, f32[4,32,16]{1,2,0:T(8,128)S(1)}, u32[]{:S(2)}, u32[]{:S(2)}) collective-permute-start(f32[4,32,16]{1,2,0:T(8,128)S(1)} %bitcast.80), channel_id=1, source_target_pairs={{1,0},{2,1},{3,2},{131,3},{130,131},{129,130},{128,129},{0,128},{5... | collective-permute-start | bytes 24584 | tf_op jit(solution)/shard_map/ppermute | solution.py:82
  140.8 7.7 %collective-permute-start.19 = (f32[4,32,128]{2,1,0:T(8,128)S(1)}, f32[4,32,128]{2,1,0:T(8,128)S(1)}, u32[]{:S(2)}, u32[]{:S(2)}) collective-permute-start(f32[4,32,128]{2,1,0:T(8,128)S(1)} %copy-done.20), channel_id=1, source_target_pairs={{4,0},{8,4},{12,8},{16,12},{20,16},{24,20},{28,24},{32,28},{36,32}... | collective-permute-start | bytes 196616 | tf_op jit(solution)/shard_map/ppermute | solution.py:77
  148.6 1.4 copy.806.refs_5_
  151.4 6.4 %shard_map.107 = (f32[4,32,16,128]{3,2,1,0:T(8,128)}, f32[4,32,128]{2,1,0:T(8,128)}, f32[4,32,128]{2,1,0:T(8,128)}, f32[4,32,16,2]{3,2,1,0:T(8,128)}) custom-call(f32[512]{0:T(512)} %reshape.105.cpl.refs_0_, f32[4,32,16,128]{3,2,1,0:T(8,128)} %get-tuple-element.21.refs_1_, f32[4,32,16,128]{3,2,1,0:T(8,128)} %refs_2_.3, f32[4,32,16,128]{3,2,1,0:T(8,128)} %fusion.4.refs_3_, ...), custom_call_target="tpu_custom_call" | custom-call | tf_op jit(solution)/shard_map/pallas_call | solution.py:199
  (117 shorter events, 17.6 us)
Async XLA Ops:
  3.0 32.3 %collective-permute-start = (f32[4,32,16]{1,2,0:T(8,128)S(1)}, f32[4,32,16]{1,2,0:T(8,128)S(1)}, u32[]{:S(2)}, u32[]{:S(2)}) collective-permute-start(f32[4,32,16]{1,2,0:T(8,128)S(1)} %bitcast.74), channel_id=1, source_target_pairs={{0,1},{1,2},{2,3},{3,131},{131,130},{130,129},{129,128},{128,0},{4... | collective-permute-start | bytes 24584 | tf_op jit(solution)/shard_map/ppermute | solution.py:81
  3.6 39.3 %collective-permute-start.1 = (f32[4,32,16]{1,2,0:T(8,128)S(1)}, f32[4,32,16]{1,2,0:T(8,128)S(1)}, u32[]{:S(2)}, u32[]{:S(2)}) collective-permute-start(f32[4,32,16]{1,2,0:T(8,128)S(1)} %bitcast.72), channel_id=1, source_target_pairs={{1,0},{2,1},{3,2},{131,3},{130,131},{129,130},{128,129},{0,128},{5... | collective-permute-start | bytes 24584 | tf_op jit(solution)/shard_map/ppermute | solution.py:82
  7.5 8.0 %copy-start.13 = (s32[1,512,1]{1,2,0:T(1,128)S(1)}, s32[1,512,1]{1,2,0:T(1,128)}, u32[]{:S(2)}) copy-start(s32[1,512,1]{1,2,0:T(1,128)} %param.12) | copy-start | bytes 6148
  7.6 9.7 %copy-start.17 = (s32[1,512]{1,0:T(1,128)S(1)}, s32[1,512]{1,0:T(1,128)}, u32[]{:S(2)}) copy-start(s32[1,512]{1,0:T(1,128)} %param.13) | copy-start | bytes 6148
  7.6 9.7 %copy-start.18 = (f32[1,512]{1,0:T(1,128)S(1)}, f32[1,512]{1,0:T(1,128)}, u32[]{:S(2)}) copy-start(f32[1,512]{1,0:T(1,128)} %param.15) | copy-start | bytes 6148
  7.6 9.7 %copy-start.16 = (f32[1,512]{1,0:T(1,128)S(1)}, f32[1,512]{1,0:T(1,128)}, u32[]{:S(2)}) copy-start(f32[1,512]{1,0:T(1,128)} %param.14) | copy-start | bytes 6148
  8.1 34.9 %collective-permute-start.8 = (f32[4,32,16]{1,2,0:T(8,128)S(1)}, f32[4,32,16]{1,2,0:T(8,128)S(1)}, u32[]{:S(2)}, u32[]{:S(2)}) collective-permute-start(f32[4,32,16]{1,2,0:T(8,128)S(1)} %bitcast.73), channel_id=1, source_target_pairs={{0,1},{1,2},{2,3},{3,131},{131,130},{130,129},{129,128},{128,0},{4... | collective-permute-start | bytes 24584 | tf_op jit(solution)/shard_map/ppermute | solution.py:39
  8.7 42.0 %collective-permute-start.9 = (f32[4,32,16]{1,2,0:T(8,128)S(1)}, f32[4,32,16]{1,2,0:T(8,128)S(1)}, u32[]{:S(2)}, u32[]{:S(2)}) collective-permute-start(f32[4,32,16]{1,2,0:T(8,128)S(1)} %bitcast.71), channel_id=1, source_target_pairs={{1,0},{2,1},{3,2},{131,3},{130,131},{129,130},{128,129},{0,128},{5... | collective-permute-start | bytes 24584 | tf_op jit(solution)/shard_map/ppermute | solution.py:40
  14.2 59.0 %collective-permute-start.2 = (f32[4,32,128]{2,1,0:T(8,128)}, f32[4,32,128]{2,1,0:T(8,128)}, u32[]{:S(2)}, u32[]{:S(2)}) collective-permute-start(f32[4,32,128]{2,1,0:T(8,128)} %bitcast.4), channel_id=1, source_target_pairs={{0,4},{4,8},{8,12},{12,16},{16,20},{20,24},{24,28},{28,32},{32,36}... | collective-permute-start | bytes 196616 | tf_op jit(solution)/shard_map/ppermute | solution.py:76
  20.0 36.1 %all-to-all-start = ((f32[64,32,3]{1,2,0:T(4,128)}), f32[64,32,3]{1,2,0:T(4,128)S(1)}, u32[]{:S(2)}, u32[]{:S(2)}) async-start(f32[64,32,3]{1,2,0:T(4,128)} %copy.793), calls=%async_computation | async-start | bytes 262144 | tf_op jit(solution)/shard_map/all_to_all | solution.py:244
  32.3 18.5 %copy-start.14 = (f32[4]{0:T(128)S(1)}, f32[4]{0:T(128)}, u32[]{:S(2)}) copy-start(f32[4]{0:T(128)} %constant.53.clone) | copy-start | bytes 52
  35.3 37.8 %collective-permute-start.3 = (f32[4,32,128]{2,1,0:T(8,128)}, f32[4,32,128]{2,1,0:T(8,128)}, u32[]{:S(2)}, u32[]{:S(2)}) collective-permute-start(f32[4,32,128]{2,1,0:T(8,128)} %bitcast.5), channel_id=1, source_target_pairs={{4,0},{8,4},{12,8},{16,12},{20,16},{24,20},{28,24},{32,28},{36,32}... | collective-permute-start | bytes 196616 | tf_op jit(solution)/shard_map/ppermute | solution.py:77
  43.0 45.0 %collective-permute-start.10 = (f32[4,32,128]{2,1,0:T(8,128)}, f32[4,32,128]{2,1,0:T(8,128)}, u32[]{:S(2)}, u32[]{:S(2)}) collective-permute-start(f32[4,32,128]{2,1,0:T(8,128)} %bitcast.25), channel_id=1, source_target_pairs={{0,4},{4,8},{8,12},{12,16},{16,20},{20,24},{24,28},{28,32},{32,36}... | collective-permute-start | bytes 196616 | tf_op jit(solution)/shard_map/ppermute | solution.py:32
  43.0 52.8 %collective-permute-start.11 = (f32[4,32,128]{2,1,0:T(8,128)}, f32[4,32,128]{2,1,0:T(8,128)}, u32[]{:S(2)}, u32[]{:S(2)}) collective-permute-start(f32[4,32,128]{2,1,0:T(8,128)} %bitcast.27), channel_id=1, source_target_pairs={{4,0},{8,4},{12,8},{16,12},{20,16},{24,20},{28,24},{32,28},{36,32}... | collective-permute-start | bytes 196616 | tf_op jit(solution)/shard_map/ppermute | solution.py:33
  83.3 4.7 %copy-start.19 = (f32[4,32,128]{2,1,0:T(8,128)S(1)}, f32[4,32,128]{2,1,0:T(8,128)}, u32[]{:S(2)}) copy-start(f32[4,32,128]{2,1,0:T(8,128)} %get-tuple-element.17) | copy-start | bytes 196612
  83.3 12.4 %copy-start.4 = (f32[4,32,15,128]{3,2,1,0:T(8,128)S(1)}, f32[4,32,15,128]{3,2,1,0:T(8,128)}, u32[]{:S(2)}) copy-start(f32[4,32,15,128]{3,2,1,0:T(8,128)} %get-tuple-element.42) | copy-start | bytes 2949124
  83.8 14.2 %collective-permute-start.4 = (f32[4,32,16]{1,2,0:T(8,128)S(1)}, f32[4,32,16]{1,2,0:T(8,128)S(1)}, u32[]{:S(2)}, u32[]{:S(2)}) collective-permute-start(f32[4,32,16]{1,2,0:T(8,128)S(1)} %bitcast.75), channel_id=1, source_target_pairs={{0,1},{1,2},{2,3},{3,131},{131,130},{130,129},{129,128},{128,0},{4... | collective-permute-start | bytes 24584 | tf_op jit(solution)/shard_map/ppermute | solution.py:81
  84.4 13.7 %collective-permute-start.5 = (f32[4,32,16]{1,2,0:T(8,128)S(1)}, f32[4,32,16]{1,2,0:T(8,128)S(1)}, u32[]{:S(2)}, u32[]{:S(2)}) collective-permute-start(f32[4,32,16]{1,2,0:T(8,128)S(1)} %bitcast.76), channel_id=1, source_target_pairs={{1,0},{2,1},{3,2},{131,3},{130,131},{129,130},{128,129},{0,128},{5... | collective-permute-start | bytes 24584 | tf_op jit(solution)/shard_map/ppermute | solution.py:82
  88.0 11.6 %collective-permute-start.6 = (f32[4,32,128]{2,1,0:T(8,128)}, f32[4,32,128]{2,1,0:T(8,128)S(1)}, u32[]{:S(2)}, u32[]{:S(2)}) collective-permute-start(f32[4,32,128]{2,1,0:T(8,128)} %get-tuple-element.16), channel_id=1, source_target_pairs={{0,4},{4,8},{8,12},{12,16},{16,20},{20,24},{24,28},{28,32},{32,36}... | collective-permute-start | bytes 196616 | tf_op jit(solution)/shard_map/ppermute | solution.py:76
  88.0 11.6 %collective-permute-start.7 = (f32[4,32,128]{2,1,0:T(8,128)S(1)}, f32[4,32,128]{2,1,0:T(8,128)S(1)}, u32[]{:S(2)}, u32[]{:S(2)}) collective-permute-start(f32[4,32,128]{2,1,0:T(8,128)S(1)} %copy-done.19), channel_id=1, source_target_pairs={{4,0},{8,4},{12,8},{16,12},{20,16},{24,20},{28,24},{32,28},{36,32}... | collective-permute-start | bytes 196616 | tf_op jit(solution)/shard_map/ppermute | solution.py:77
  98.1 10.3 %copy-start.2 = (f32[2048,128]{1,0:T(8,128)S(1)}, f32[2048,128]{1,0:T(8,128)}, u32[]{:S(2)}) copy-start(f32[2048,128]{1,0:T(8,128)} %get-tuple-element.28) | copy-start | bytes 3145732
  98.2 10.3 %copy-start.3 = (f32[2048,128]{1,0:T(8,128)S(1)}, f32[2048,128]{1,0:T(8,128)}, u32[]{:S(2)}) copy-start(f32[2048,128]{1,0:T(8,128)} %get-tuple-element.29) | copy-start | bytes 3145732
  110.3 5.0 %copy-start.1 = (f32[4,32,16,128]{3,2,1,0:T(8,128)}, f32[4,32,16,128]{3,2,1,0:T(8,128)S(1)}, u32[]{:S(2)}) copy-start(f32[4,32,16,128]{3,2,1,0:T(8,128)S(1)} %subtract_multiply_fusion.refs_1_) | copy-start | bytes 3145732
  111.2 12.1 %collective-permute-start.12 = (f32[4,32,16]{1,2,0:T(8,128)S(1)}, f32[4,32,16]{1,2,0:T(8,128)S(1)}, u32[]{:S(2)}, u32[]{:S(2)}) collective-permute-start(f32[4,32,16]{1,2,0:T(8,128)S(1)} %bitcast.77), channel_id=1, source_target_pairs={{0,1},{1,2},{2,3},{3,131},{131,130},{130,129},{129,128},{128,0},{4... | collective-permute-start | bytes 24584 | tf_op jit(solution)/shard_map/ppermute | solution.py:81
  111.8 11.5 %collective-permute-start.13 = (f32[4,32,16]{1,2,0:T(8,128)S(1)}, f32[4,32,16]{1,2,0:T(8,128)S(1)}, u32[]{:S(2)}, u32[]{:S(2)}) collective-permute-start(f32[4,32,16]{1,2,0:T(8,128)S(1)} %bitcast.78), channel_id=1, source_target_pairs={{1,0},{2,1},{3,2},{131,3},{130,131},{129,130},{128,129},{0,128},{5... | collective-permute-start | bytes 24584 | tf_op jit(solution)/shard_map/ppermute | solution.py:82
  115.4 10.1 %collective-permute-start.14 = (f32[4,32,128]{2,1,0:T(8,128)S(1)}, f32[4,32,128]{2,1,0:T(8,128)S(1)}, u32[]{:S(2)}, u32[]{:S(2)}) collective-permute-start(f32[4,32,128]{2,1,0:T(8,128)S(1)} %bitcast.67), channel_id=1, source_target_pairs={{0,4},{4,8},{8,12},{12,16},{16,20},{20,24},{24,28},{28,32},{32,36}... | collective-permute-start | bytes 196616 | tf_op jit(solution)/shard_map/ppermute | solution.py:76
  115.5 10.0 %collective-permute-start.15 = (f32[4,32,128]{2,1,0:T(8,128)S(1)}, f32[4,32,128]{2,1,0:T(8,128)S(1)}, u32[]{:S(2)}, u32[]{:S(2)}) collective-permute-start(f32[4,32,128]{2,1,0:T(8,128)S(1)} %bitcast.66), channel_id=1, source_target_pairs={{4,0},{8,4},{12,8},{16,12},{20,16},{24,20},{28,24},{32,28},{36,32}... | collective-permute-start | bytes 196616 | tf_op jit(solution)/shard_map/ppermute | solution.py:77
  136.1 4.7 %copy-start.21 = (f32[4,32,128]{2,1,0:T(8,128)S(1)}, f32[4,32,128]{2,1,0:T(8,128)}, u32[]{:S(2)}) copy-start(f32[4,32,128]{2,1,0:T(8,128)} %get-tuple-element.23) | copy-start | bytes 196612
  136.6 11.9 %collective-permute-start.16 = (f32[4,32,16]{1,2,0:T(8,128)S(1)}, f32[4,32,16]{1,2,0:T(8,128)S(1)}, u32[]{:S(2)}, u32[]{:S(2)}) collective-permute-start(f32[4,32,16]{1,2,0:T(8,128)S(1)} %bitcast.79), channel_id=1, source_target_pairs={{0,1},{1,2},{2,3},{3,131},{131,130},{130,129},{129,128},{128,0},{4... | collective-permute-start | bytes 24584 | tf_op jit(solution)/shard_map/ppermute | solution.py:81
  137.2 11.3 %collective-permute-start.17 = (f32[4,32,16]{1,2,0:T(8,128)S(1)}, f32[4,32,16]{1,2,0:T(8,128)S(1)}, u32[]{:S(2)}, u32[]{:S(2)}) collective-permute-start(f32[4,32,16]{1,2,0:T(8,128)S(1)} %bitcast.80), channel_id=1, source_target_pairs={{1,0},{2,1},{3,2},{131,3},{130,131},{129,130},{128,129},{0,128},{5... | collective-permute-start | bytes 24584 | tf_op jit(solution)/shard_map/ppermute | solution.py:82
  140.8 10.0 %collective-permute-start.18 = (f32[4,32,128]{2,1,0:T(8,128)S(1)}, f32[4,32,128]{2,1,0:T(8,128)S(1)}, u32[]{:S(2)}, u32[]{:S(2)}) collective-permute-start(f32[4,32,128]{2,1,0:T(8,128)S(1)} %copy-done.21), channel_id=1, source_target_pairs={{0,4},{4,8},{8,12},{12,16},{16,20},{20,24},{24,28},{28,32},{32,36}... | collective-permute-start | bytes 196616 | tf_op jit(solution)/shard_map/ppermute | solution.py:76
  140.8 10.0 %collective-permute-start.19 = (f32[4,32,128]{2,1,0:T(8,128)S(1)}, f32[4,32,128]{2,1,0:T(8,128)S(1)}, u32[]{:S(2)}, u32[]{:S(2)}) collective-permute-start(f32[4,32,128]{2,1,0:T(8,128)S(1)} %copy-done.20), channel_id=1, source_target_pairs={{4,0},{8,4},{12,8},{16,12},{20,16},{24,20},{28,24},{32,28},{36,32}... | collective-permute-start | bytes 196616 | tf_op jit(solution)/shard_map/ppermute | solution.py:77
  (11 other events, 19.8 us)

commit v4 on v2

--- a/solution.py
+++ b/solution.py
@@ -203,6 +203,36 @@
         in_specs=[pl.BlockSpec(memory_space=pltpu.SMEM)] + level_specs(ins),
         out_specs=level_specs(outs),
     )(cpl, *ins)
+
+
+def coef_kernel(flags, c_ref, hns, hw, he, out_ref):
+    masks = edge_masks(c_ref.shape[2:])
+    top, bottom = masks[0], masks[1]
+    polar_top = jnp.logical_and(top, jnp.full(top.shape, flags[0], jnp.int32) == 1)
+    polar_bottom = jnp.logical_and(bottom, jnp.full(bottom.shape, flags[1], jnp.int32) == 1)
+
+    def body(l, carry):
+        near = [neighbours_2d(c_ref[d, l], masks, hns[d, l, :, 0:1], hns[d, l, :, 1:2], hw[d, l], he[d, l]) for d in range(4)]
+        out_ref[0, l] = jnp.where(polar_top, near[0][0], near[1][0])
+        out_ref[1, l] = jnp.where(polar_bottom, near[1][1], near[0][1])
+        out_ref[2, l] = near[3][2]
+        out_ref[3, l] = near[2][3]
+        return carry
+
+    lax.fori_loop(0, c_ref.shape[1], body, 0, unroll=UNROLL)
+
+
+def coef_neighbours(coef, halo):
+    lat_j = lax.axis_index("lat")
+    flags = jnp.stack([lat_j == 0, lat_j == lax.axis_size("lat") - 1]).astype(jnp.int32)
+    ins = [coef, *halo]
+    return pl.pallas_call(
+        coef_kernel,
+        out_shape=jax.ShapeDtypeStruct(coef.shape, coef.dtype),
+        grid=(coef.shape[1] // LEVEL_BLOCK,),
+        in_specs=[pl.BlockSpec(memory_space=pltpu.SMEM)] + level_specs(ins),
+        out_specs=level_specs([coef])[0],
+    )(flags, *ins)
 
 
 def edges_of(x):
@@ -255,18 +285,7 @@
     spread = jnp.where(lane_hit, forcing[:, None], 0.0)
     lam = jnp.zeros_like(table).at[row_of].add(spread).reshape(x.shape)
 
-    near_n, near_s, near_w, near_e = shifted(coefficients, halos(coefficients, plain_flip))
-    row_ids = jnp.arange(coefficients.shape[3], dtype=jnp.int32)[None, :]
-    polar_top = (lax.axis_index("lat") == 0) & (row_ids == 0)
-    polar_bottom = (lax.axis_index("lat") == lax.axis_size("lat") - 1) & (
-        row_ids == coefficients.shape[3] - 1
-    )
-    back_coef = jnp.stack([
-        jnp.where(polar_top, near_n[0], near_n[1]),
-        jnp.where(polar_bottom, near_s[1], near_s[0]),
-        near_w[3],
-        near_e[2],
-    ])
+    back_coef = coef_neighbours(coefficients, edge_halos(*edges_of(coefficients), plain_flip))
     lam_y = lam * factors[STEPS - 1]
     edges = edges_of(lam_y)
     for step in range(STEPS - 1, -1, -1):

time: 159 us -> 160 us (level)
  starting transfers between devices: 60.7 us -> 69.4 us
  other arithmetic: 32.2 us -> 24.2 us
  Pallas kernels: 31 us -> 36.2 us
  local copies, waits for them, and re-layouts: 28.5 us -> 25.5 us
  waiting for transfers between devices: 4.13 us -> 1.44 us
    ppermute x4 -> x5, starting transfers between devices: 6.57 us -> 17.9 us  [edge_halos(): lax.ppermute(jnp.where(low, first_row, last_row), ('lon', 'lat'), ccw_pairs)]
    ppermute x4 -> x0, starting transfers between devices: 7.17 us -> none  [the longest x1 3.57 us: halos(): lax.ppermute(jnp.where(low, first_row, last_row), ('lon', 'lat'), ccw_pairs)]
    ppermute x4 -> x5, starting transfers between devices: 32.4 us -> 38.6 us  [edge_halos(): from_east = lax.ppermute(first_col, 'lon', down)]
    pallas_call x0 -> x1, Pallas kernels: none -> 5.18 us  [coef_neighbours(): pl.pallas_call(coef_kernel, out_shape=jax.ShapeDtypeStruct(coef.shape, co...]
    slice x3 -> x0, local copies, waits for them, and re-layouts: 3.54 us -> none  [the longest x1 1.47 us: shifted(): west = jnp.concatenate([from_west[:, :, None, :], x[:, :, :-1, :]], axis=2)]
    ppermute x4 -> x5, waiting for transfers between devices: 2.78 us -> 0.01 us  [edge_halos(): lax.ppermute(jnp.where(low, last_row, first_row), ('lon', 'lat'), cw_pairs)]
    select_n x3 -> x0, other arithmetic: 2.49 us -> none  [the longest x1 1.24 us: on_device(): jnp.where(polar_bottom, near_s[1], near_s[0])]
    another operation x1 -> x0, other arithmetic: 2.11 us -> none  [on_device(): jnp.stack([jnp.where(polar_top, near_n[0], near_n[1]), jnp.where(polar_bo...]
  transfers between devices with their start and end apart: 21 -> 21, of which waited for: 3 -> 2; matrix products, arithmetic and copies ran while one was open for 19% -> 13% of each run, Pallas kernels for 5% -> 8%
where the time goes in v4:
time: 160 us; the launch traced here: 159 us
  starting transfers between devices  69.4 us (43%)
  Pallas kernels  36.2 us (23%)
  local copies, waits for them, and re-layouts  25.5 us (16%)
  other arithmetic  24.2 us (15%)
  between operations  1.89 us (1%)
    ppermute x5, starting transfers between devices, edge_halos(): from_east = lax.ppermute(first_col, 'lon', down)  38.6 us
    ppermute x5, starting transfers between devices, edge_halos(): lax.ppermute(jnp.where(low, first_row, last_row), ('lon', 'lat'), ccw_pairs)  17.9 us
    pallas_call x2, Pallas kernels, forward_step(): pl.pallas_call(forward_kernel, out_shape=outs, grid=(x.shape[1] // LEVEL_...  16.5 us
    pallas_call x2, Pallas kernels, backward_step(): pl.pallas_call(lambda *refs: backward_kernel(*refs, last=last), out_shape...  14.5 us
    scatter-add x1, other arithmetic, on_device(): lam = jnp.zeros_like(table).at[row_of].add(spread).reshape(x.shape)  13 us
    all_to_all x1, starting transfers between devices, on_device(): arrived = lax.all_to_all(send, 'lon', 0, 0, tiled=True)  10.9 us
    another operation x5, local copies, waits for them, and re-layouts, edge_halos(): jnp.stack([north_row, south_row], axis=-1)  7.21 us
    gather x1, local copies, waits for them, and re-layouts, on_device(): picked = jnp.sum(jnp.where(lane_hit, table[row_of], 0.0), axis=1)  6.68 us
  transfers between devices with their start and end apart: 21, of which 2 were waited for; matrix products, arithmetic and copies ran while one was open for 13% of the time, Pallas kernels for 8%

profile of v4, /device:TPU:0, one launch (start us, length us, event | category | flops | bytes accessed | tf_op | source)
XLA Modules:
  0.0 158.6 jit_solution(15774397488215328623)
XLA Ops:
  0.6 1.9 %slice_select_fusion.9 = (f32[4,32,16,1]{3,2,1,0:T(8,128)S(1)}, f32[4,32,16,1]{3,2,1,0:T(8,128)S(1)}) fusion(f32[4,32,16,128]{3,2,1,0:T(8,128)} %x_ref.1, pred[]{:T(512)S(6)} %lt.44), kind=kLoop, calls=%fused_computation.20 | loop fusion | flops 4096 | bytes 32769 | tf_op jit(solution)/shard_map/jit(_where)/select_n | solution.py:81
  3.6 3.6 %collective-permute-start.1 = (f32[4,32,16]{1,2,0:T(8,128)S(1)}, f32[4,32,16]{1,2,0:T(8,128)S(1)}, u32[]{:S(2)}, u32[]{:S(2)}) collective-permute-start(f32[4,32,16]{1,2,0:T(8,128)S(1)} %bitcast.101), channel_id=1, source_target_pairs={{1,0},{2,1},{3,2},{131,3},{130,131},{129,130},{128,129},{0,128},{5... | collective-permute-start | bytes 24584 | tf_op jit(solution)/shard_map/ppermute | solution.py:82
  8.7 3.6 %collective-permute-start.9 = (f32[4,32,16]{1,2,0:T(8,128)S(1)}, f32[4,32,16]{1,2,0:T(8,128)S(1)}, u32[]{:S(2)}, u32[]{:S(2)}) collective-permute-start(f32[4,32,16]{1,2,0:T(8,128)S(1)} %bitcast.100), channel_id=1, source_target_pairs={{1,0},{2,1},{3,2},{131,3},{130,131},{129,130},{128,129},{0,128},{5... | collective-permute-start | bytes 24584 | tf_op jit(solution)/shard_map/ppermute | solution.py:82
  12.2 1.3 fusion.18
  13.5 1.4 collective-permute-start.2
  15.2 0.8 iota_compare_fusion
  16.8 1.9 %select_reduce_fusion = f32[2048,3]{0,1:T(4,128)S(1)} fusion(f32[512,3]{0,1:T(4,128)S(1)} %pad_maximum_fusion.5, pred[2048,512]{1,0:T(8,128)(4,1)S(1)} %iota_compare_fusion), kind=kLoop, calls=%fused_computation.2 | loop fusion | flops 6285312 | bytes 1079296 | tf_op jit(solution)/shard_map/reduce_sum | solution.py:273
  18.7 0.7 copy.764
  19.5 10.9 %all-to-all-start = ((f32[64,32,3]{1,2,0:T(4,128)}), f32[64,32,3]{1,2,0:T(4,128)S(1)}, u32[]{:S(2)}, u32[]{:S(2)}) async-start(f32[64,32,3]{1,2,0:T(4,128)} %copy.764), calls=%async_computation | async-start | bytes 262144 | tf_op jit(solution)/shard_map/all_to_all | solution.py:274
  31.1 0.7 reshape.96.cpl.refs_0_
  31.8 7.6 %collective-permute-start.3 = (f32[4,32,128]{2,1,0:T(8,128)S(1)}, f32[4,32,128]{2,1,0:T(8,128)S(1)}, u32[]{:S(2)}, u32[]{:S(2)}) collective-permute-start(f32[4,32,128]{2,1,0:T(8,128)S(1)} %bitcast.94), channel_id=1, source_target_pairs={{4,0},{8,4},{12,8},{16,12},{20,16},{24,20},{28,24},{32,28},{36,32}... | collective-permute-start | bytes 196616 | tf_op jit(solution)/shard_map/ppermute | solution.py:77
  39.5 7.7 %collective-permute-start.11 = (f32[4,32,128]{2,1,0:T(8,128)S(1)}, f32[4,32,128]{2,1,0:T(8,128)S(1)}, u32[]{:S(2)}, u32[]{:S(2)}) collective-permute-start(f32[4,32,128]{2,1,0:T(8,128)S(1)} %bitcast.92), channel_id=1, source_target_pairs={{4,0},{8,4},{12,8},{16,12},{20,16},{24,20},{28,24},{32,28},{36,32}... | collective-permute-start | bytes 196616 | tf_op jit(solution)/shard_map/ppermute | solution.py:77
  47.3 1.4 copy.760.hns
  48.8 1.4 copy.770.hns
  51.1 8.2 %shard_map.104 = (f32[4,32,16,128]{3,2,1,0:T(8,128)}, f32[4,32,16,128]{3,2,1,0:T(8,128)}, f32[4,32,1,128]{3,2,1,0:T(1,128)}, f32[4,32,1,128]{3,2,1,0:T(1,128)}, f32[4,32,16,2]{3,2,1,0:T(8,128)}) custom-call(f32[512]{0:T(512)} %reshape.96.cpl.refs_0_, f32[4,32,16,128]{3,2,1,0:T(8,128)} %x_ref.1, f32[4,32,16,128]{3,2,1,0:T(8,128)} %refs_2_.3, ...), custom_call_target="tpu_custom_call" | custom-call | tf_op jit(solution)/shard_map/pallas_call | solution.py:187
  59.3 2.0 %slice_select_fusion.7 = (f32[4,32,16,1]{3,2,1,0:T(8,128)S(1)}, f32[4,32,16,1]{3,2,1,0:T(8,128)S(1)}) fusion(f32[4,32,16,2]{3,2,1,0:T(8,128)} %get-tuple-element.15, pred[]{:T(512)S(6)} %lt.44), kind=kLoop, calls=%fused_computation.18 | loop fusion | flops 4096 | bytes 32769 | tf_op jit(solution)/shard_map/jit(_where)/select_n | solution.py:81
  62.4 3.6 %collective-permute-start.5 = (f32[4,32,16]{1,2,0:T(8,128)S(1)}, f32[4,32,16]{1,2,0:T(8,128)S(1)}, u32[]{:S(2)}, u32[]{:S(2)}) collective-permute-start(f32[4,32,16]{1,2,0:T(8,128)S(1)} %bitcast.105), channel_id=1, source_target_pairs={{1,0},{2,1},{3,2},{131,3},{130,131},{129,130},{128,129},{0,128},{5... | collective-permute-start | bytes 24584 | tf_op jit(solution)/shard_map/ppermute | solution.py:82
  66.0 7.8 %collective-permute-start.7 = (f32[4,32,128]{2,1,0:T(8,128)S(1)}, f32[4,32,128]{2,1,0:T(8,128)S(1)}, u32[]{:S(2)}, u32[]{:S(2)}) collective-permute-start(f32[4,32,128]{2,1,0:T(8,128)S(1)} %bitcast.115), channel_id=1, source_target_pairs={{4,0},{8,4},{12,8},{16,12},{20,16},{24,20},{28,24},{32,28},{36,32}... | collective-permute-start | bytes 196616 | tf_op jit(solution)/shard_map/ppermute | solution.py:77
  74.5 5.2 %shard_map.106.refs_3_ = f32[4,32,16,128]{3,2,1,0:T(8,128)} custom-call(s32[2]{0:T(128)} %add_convert_fusion.flags, f32[4,32,16,128]{3,2,1,0:T(8,128)} %refs_2_.3, f32[4,32,16,2]{3,2,1,0:T(8,128)} %copy.770.hns, f32[4,32,1,128]{3,2,1,0:T(1,128)} %bitcast.87, f32[4,32,1,128]{3,2,1,0:T(1,128)} %bitcast.88), custom_call_target="tpu_custom_call" | custom-call | tf_op jit(solution)/shard_map/pallas_call | solution.py:229
  79.7 1.4 copy.763.hns
  81.9 8.2 %shard_map.105 = (f32[4,32,16,128]{3,2,1,0:T(8,128)}, f32[4,32,16,128]{3,2,1,0:T(8,128)}, f32[4,32,1,128]{3,2,1,0:T(1,128)}, f32[4,32,1,128]{3,2,1,0:T(1,128)}, f32[4,32,16,2]{3,2,1,0:T(8,128)}) custom-call(f32[512]{0:T(512)} %reshape.96.cpl.refs_0_, f32[4,32,16,128]{3,2,1,0:T(8,128)} %get-tuple-element.14.x_ref, f32[4,32,16,128]{3,2,1,0:T(8,128)} %refs_2_.3, ...), custom_call_target="tpu_custom_call" | custom-call | tf_op jit(solution)/shard_map/pallas_call | solution.py:187
  90.1 6.7 %gather_fusion = f32[2048,128]{1,0:T(8,128)S(1)} fusion(f32[2048,128]{1,0:T(8,128)} %bitcast.78, s32[2048]{0:T(1024)S(1)} %broadcast_clamp_fusion), kind=kCustom, calls=%fused_computation | custom fusion | bytes 2105344 | tf_op jit(solution)/shard_map/gather | solution.py:283
  97.5 13.0 %scatter_custom_fusion = f32[2048,128]{1,0:T(8,128)S(1)} fusion(s32[2048]{0:T(1024)S(1)} %bitcast.111, f32[2048]{0:T(1024)S(1)} %bitcast.98, s32[2048]{0:T(1024)S(1)} %bitcast.81, f32[]{:T(128)} %constant.44.clone.1), kind=kCustom, calls=%fused_computation.7 | custom fusion | flops 786432 | bytes 1065984 | tf_op jit(solution)/shard_map/scatter-add | solution.py:286
  112.3 3.6 %collective-permute-start.13 = (f32[4,32,16]{1,2,0:T(8,128)S(1)}, f32[4,32,16]{1,2,0:T(8,128)S(1)}, u32[]{:S(2)}, u32[]{:S(2)}) collective-permute-start(f32[4,32,16]{1,2,0:T(8,128)S(1)} %bitcast.107), channel_id=1, source_target_pairs={{1,0},{2,1},{3,2},{131,3},{130,131},{129,130},{128,129},{0,128},{5... | collective-permute-start | bytes 24584 | tf_op jit(solution)/shard_map/ppermute | solution.py:82
  116.1 7.7 %collective-permute-start.15 = (f32[4,32,128]{2,1,0:T(8,128)S(1)}, f32[4,32,128]{2,1,0:T(8,128)S(1)}, u32[]{:S(2)}, u32[]{:S(2)}) collective-permute-start(f32[4,32,128]{2,1,0:T(8,128)S(1)} %bitcast.96), channel_id=1, source_target_pairs={{4,0},{8,4},{12,8},{16,12},{20,16},{24,20},{28,24},{32,28},{36,32}... | collective-permute-start | bytes 196616 | tf_op jit(solution)/shard_map/ppermute | solution.py:77
  123.9 1.4 copy.773.refs_5_
  126.7 8.1 %shard_map.107 = (f32[4,32,16,128]{3,2,1,0:T(8,128)}, f32[4,32,1,128]{3,2,1,0:T(1,128)}, f32[4,32,1,128]{3,2,1,0:T(1,128)}, f32[4,32,16,2]{3,2,1,0:T(8,128)}) custom-call(f32[512]{0:T(512)} %reshape.96.cpl.refs_0_, f32[4,32,16,128]{3,2,1,0:T(8,128)} %copy-done.1, f32[4,32,16,128]{3,2,1,0:T(8,128)} %refs_2_.3, f32[4,32,16,128]{3,2,1,0:T(8,128)} %shard_map.106.refs_3_, ...), custom_call_target="tpu_custom_call" | custom-call | tf_op jit(solution)/shard_map/pallas_call | solution.py:199
  134.8 1.9 %slice_select_fusion.3 = (f32[4,32,16,1]{3,2,1,0:T(8,128)S(1)}, f32[4,32,16,1]{3,2,1,0:T(8,128)S(1)}) fusion(f32[4,32,16,2]{3,2,1,0:T(8,128)} %get-tuple-element.22, pred[]{:T(512)S(6)} %lt.44), kind=kLoop, calls=%fused_computation.14 | loop fusion | flops 4096 | bytes 32769 | tf_op jit(solution)/shard_map/jit(_where)/select_n | solution.py:81
  137.8 3.6 %collective-permute-start.17 = (f32[4,32,16]{1,2,0:T(8,128)S(1)}, f32[4,32,16]{1,2,0:T(8,128)S(1)}, u32[]{:S(2)}, u32[]{:S(2)}) collective-permute-start(f32[4,32,16]{1,2,0:T(8,128)S(1)} %bitcast.109), channel_id=1, source_target_pairs={{1,0},{2,1},{3,2},{131,3},{130,131},{129,130},{128,129},{0,128},{5... | collective-permute-start | bytes 24584 | tf_op jit(solution)/shard_map/ppermute | solution.py:82
  141.4 7.7 %collective-permute-start.19 = (f32[4,32,128]{2,1,0:T(8,128)S(1)}, f32[4,32,128]{2,1,0:T(8,128)S(1)}, u32[]{:S(2)}, u32[]{:S(2)}) collective-permute-start(f32[4,32,128]{2,1,0:T(8,128)S(1)} %bitcast.117), channel_id=1, source_target_pairs={{4,0},{8,4},{12,8},{16,12},{20,16},{24,20},{28,24},{32,28},{36,32}... | collective-permute-start | bytes 196616 | tf_op jit(solution)/shard_map/ppermute | solution.py:77
  149.3 1.4 copy.776.refs_5_
  152.1 6.4 %shard_map.108 = (f32[4,32,16,128]{3,2,1,0:T(8,128)}, f32[4,32,1,128]{3,2,1,0:T(1,128)}, f32[4,32,1,128]{3,2,1,0:T(1,128)}, f32[4,32,16,2]{3,2,1,0:T(8,128)}) custom-call(f32[512]{0:T(512)} %reshape.96.cpl.refs_0_, f32[4,32,16,128]{3,2,1,0:T(8,128)} %get-tuple-element.21.refs_1_, f32[4,32,16,128]{3,2,1,0:T(8,128)} %refs_2_.3, ...), custom_call_target="tpu_custom_call" | custom-call | tf_op jit(solution)/shard_map/pallas_call | solution.py:199
  (115 shorter events, 13.7 us)
Async XLA Ops:
  3.0 28.8 %collective-permute-start = (f32[4,32,16]{1,2,0:T(8,128)S(1)}, f32[4,32,16]{1,2,0:T(8,128)S(1)}, u32[]{:S(2)}, u32[]{:S(2)}) collective-permute-start(f32[4,32,16]{1,2,0:T(8,128)S(1)} %bitcast.103), channel_id=1, source_target_pairs={{0,1},{1,2},{2,3},{3,131},{131,130},{130,129},{129,128},{128,0},{4... | collective-permute-start | bytes 24584 | tf_op jit(solution)/shard_map/ppermute | solution.py:81
  3.6 35.8 %collective-permute-start.1 = (f32[4,32,16]{1,2,0:T(8,128)S(1)}, f32[4,32,16]{1,2,0:T(8,128)S(1)}, u32[]{:S(2)}, u32[]{:S(2)}) collective-permute-start(f32[4,32,16]{1,2,0:T(8,128)S(1)} %bitcast.101), channel_id=1, source_target_pairs={{1,0},{2,1},{3,2},{131,3},{130,131},{129,130},{128,129},{0,128},{5... | collective-permute-start | bytes 24584 | tf_op jit(solution)/shard_map/ppermute | solution.py:82
  7.5 7.4 %copy-start.13 = (s32[1,512,1]{1,2,0:T(1,128)S(1)}, s32[1,512,1]{1,2,0:T(1,128)}, u32[]{:S(2)}) copy-start(s32[1,512,1]{1,2,0:T(1,128)} %param.12) | copy-start | bytes 6148
  8.1 31.4 %collective-permute-start.8 = (f32[4,32,16]{1,2,0:T(8,128)S(1)}, f32[4,32,16]{1,2,0:T(8,128)S(1)}, u32[]{:S(2)}, u32[]{:S(2)}) collective-permute-start(f32[4,32,16]{1,2,0:T(8,128)S(1)} %bitcast.102), channel_id=1, source_target_pairs={{0,1},{1,2},{2,3},{3,131},{131,130},{130,129},{129,128},{128,0},{4... | collective-permute-start | bytes 24584 | tf_op jit(solution)/shard_map/ppermute | solution.py:81
  8.1 8.5 %copy-start.17 = (s32[1,512]{1,0:T(1,128)S(1)}, s32[1,512]{1,0:T(1,128)}, u32[]{:S(2)}) copy-start(s32[1,512]{1,0:T(1,128)} %param.13) | copy-start | bytes 6148
  8.1 8.6 %copy-start.18 = (f32[1,512]{1,0:T(1,128)S(1)}, f32[1,512]{1,0:T(1,128)}, u32[]{:S(2)}) copy-start(f32[1,512]{1,0:T(1,128)} %param.15) | copy-start | bytes 6148
  8.2 8.6 %copy-start.16 = (f32[1,512]{1,0:T(1,128)S(1)}, f32[1,512]{1,0:T(1,128)}, u32[]{:S(2)}) copy-start(f32[1,512]{1,0:T(1,128)} %param.14) | copy-start | bytes 6148
  8.7 38.5 %collective-permute-start.9 = (f32[4,32,16]{1,2,0:T(8,128)S(1)}, f32[4,32,16]{1,2,0:T(8,128)S(1)}, u32[]{:S(2)}, u32[]{:S(2)}) collective-permute-start(f32[4,32,16]{1,2,0:T(8,128)S(1)} %bitcast.100), channel_id=1, source_target_pairs={{1,0},{2,1},{3,2},{131,3},{130,131},{129,130},{128,129},{0,128},{5... | collective-permute-start | bytes 24584 | tf_op jit(solution)/shard_map/ppermute | solution.py:82
  13.5 36.9 %collective-permute-start.2 = (f32[4,32,128]{2,1,0:T(8,128)S(1)}, f32[4,32,128]{2,1,0:T(8,128)S(1)}, u32[]{:S(2)}, u32[]{:S(2)}) collective-permute-start(f32[4,32,128]{2,1,0:T(8,128)S(1)} %bitcast.95), channel_id=1, source_target_pairs={{0,4},{4,8},{8,12},{12,16},{16,20},{20,24},{24,28},{28,32},{32,36}... | collective-permute-start | bytes 196616 | tf_op jit(solution)/shard_map/ppermute | solution.py:76
  16.0 15.0 %copy-start.15 = (f32[32,4,4]{0,2,1:T(4,128)S(1)}, f32[32,4,4]{0,2,1:T(4,128)}, u32[]{:S(2)}) copy-start(f32[32,4,4]{0,2,1:T(4,128)} %param.11) | copy-start | bytes 6148
  16.8 30.5 %copy-start.14 = (f32[4]{0:T(128)S(1)}, f32[4]{0:T(128)}, u32[]{:S(2)}) copy-start(f32[4]{0:T(128)} %constant.51.clone) | copy-start | bytes 52
  19.5 30.8 %all-to-all-start = ((f32[64,32,3]{1,2,0:T(4,128)}), f32[64,32,3]{1,2,0:T(4,128)S(1)}, u32[]{:S(2)}, u32[]{:S(2)}) async-start(f32[64,32,3]{1,2,0:T(4,128)} %copy.764), calls=%async_computation | async-start | bytes 262144 | tf_op jit(solution)/shard_map/all_to_all | solution.py:274
  31.8 18.6 %collective-permute-start.3 = (f32[4,32,128]{2,1,0:T(8,128)S(1)}, f32[4,32,128]{2,1,0:T(8,128)S(1)}, u32[]{:S(2)}, u32[]{:S(2)}) collective-permute-start(f32[4,32,128]{2,1,0:T(8,128)S(1)} %bitcast.94), channel_id=1, source_target_pairs={{4,0},{8,4},{12,8},{16,12},{20,16},{24,20},{28,24},{32,28},{36,32}... | collective-permute-start | bytes 196616 | tf_op jit(solution)/shard_map/ppermute | solution.py:77
  39.5 26.6 %collective-permute-start.10 = (f32[4,32,128]{2,1,0:T(8,128)S(1)}, f32[4,32,128]{2,1,0:T(8,128)S(1)}, u32[]{:S(2)}, u32[]{:S(2)}) collective-permute-start(f32[4,32,128]{2,1,0:T(8,128)S(1)} %bitcast.93), channel_id=1, source_target_pairs={{0,4},{4,8},{8,12},{12,16},{16,20},{20,24},{24,28},{28,32},{32,36}... | collective-permute-start | bytes 196616 | tf_op jit(solution)/shard_map/ppermute | solution.py:76
  39.5 34.4 %collective-permute-start.11 = (f32[4,32,128]{2,1,0:T(8,128)S(1)}, f32[4,32,128]{2,1,0:T(8,128)S(1)}, u32[]{:S(2)}, u32[]{:S(2)}) collective-permute-start(f32[4,32,128]{2,1,0:T(8,128)S(1)} %bitcast.92), channel_id=1, source_target_pairs={{4,0},{8,4},{12,8},{16,12},{20,16},{24,20},{28,24},{32,28},{36,32}... | collective-permute-start | bytes 196616 | tf_op jit(solution)/shard_map/ppermute | solution.py:77
  61.3 4.7 %copy-start.20 = (f32[4,32,1,128]{3,2,1,0:T(1,128)S(1)}, f32[4,32,1,128]{3,2,1,0:T(1,128)}, u32[]{:S(2)}) copy-start(f32[4,32,1,128]{3,2,1,0:T(1,128)} %get-tuple-element.16) | copy-start | bytes 196612
  61.3 4.7 %copy-start.19 = (f32[4,32,1,128]{3,2,1,0:T(1,128)S(1)}, f32[4,32,1,128]{3,2,1,0:T(1,128)}, u32[]{:S(2)}) copy-start(f32[4,32,1,128]{3,2,1,0:T(1,128)} %get-tuple-element.17) | copy-start | bytes 196612
  61.8 17.8 %collective-permute-start.4 = (f32[4,32,16]{1,2,0:T(8,128)S(1)}, f32[4,32,16]{1,2,0:T(8,128)S(1)}, u32[]{:S(2)}, u32[]{:S(2)}) collective-permute-start(f32[4,32,16]{1,2,0:T(8,128)S(1)} %bitcast.104), channel_id=1, source_target_pairs={{0,1},{1,2},{2,3},{3,131},{131,130},{130,129},{129,128},{128,0},{4... | collective-permute-start | bytes 24584 | tf_op jit(solution)/shard_map/ppermute | solution.py:81
  62.4 17.2 %collective-permute-start.5 = (f32[4,32,16]{1,2,0:T(8,128)S(1)}, f32[4,32,16]{1,2,0:T(8,128)S(1)}, u32[]{:S(2)}, u32[]{:S(2)}) collective-permute-start(f32[4,32,16]{1,2,0:T(8,128)S(1)} %bitcast.105), channel_id=1, source_target_pairs={{1,0},{2,1},{3,2},{131,3},{130,131},{129,130},{128,129},{0,128},{5... | collective-permute-start | bytes 24584 | tf_op jit(solution)/shard_map/ppermute | solution.py:82
  66.0 15.2 %collective-permute-start.6 = (f32[4,32,128]{2,1,0:T(8,128)S(1)}, f32[4,32,128]{2,1,0:T(8,128)S(1)}, u32[]{:S(2)}, u32[]{:S(2)}) collective-permute-start(f32[4,32,128]{2,1,0:T(8,128)S(1)} %bitcast.116), channel_id=1, source_target_pairs={{0,4},{4,8},{8,12},{12,16},{16,20},{20,24},{24,28},{28,32},{32,36}... | collective-permute-start | bytes 196616 | tf_op jit(solution)/shard_map/ppermute | solution.py:76
  66.0 7.8 %copy-start.8 = (f32[4,32,128]{2,1,0:T(8,128)}, f32[4,32,128]{2,1,0:T(8,128)S(1)}, u32[]{:S(2)}) copy-start(f32[4,32,128]{2,1,0:T(8,128)S(1)} %collective-permute-done.10) | copy-start | bytes 196612
  66.0 15.1 %collective-permute-start.7 = (f32[4,32,128]{2,1,0:T(8,128)S(1)}, f32[4,32,128]{2,1,0:T(8,128)S(1)}, u32[]{:S(2)}, u32[]{:S(2)}) collective-permute-start(f32[4,32,128]{2,1,0:T(8,128)S(1)} %bitcast.115), channel_id=1, source_target_pairs={{4,0},{8,4},{12,8},{16,12},{20,16},{24,20},{28,24},{32,28},{36,32}... | collective-permute-start | bytes 196616 | tf_op jit(solution)/shard_map/ppermute | solution.py:77
  96.8 13.7 %copy-start.2 = (f32[4,32,16,128]{3,2,1,0:T(8,128)S(1)}, f32[4,32,16,128]{3,2,1,0:T(8,128)}, u32[]{:S(2)}) copy-start(f32[4,32,16,128]{3,2,1,0:T(8,128)} %get-tuple-element.19) | copy-start | bytes 3145732
  110.7 5.2 %copy-start.1 = (f32[4,32,16,128]{3,2,1,0:T(8,128)}, f32[4,32,16,128]{3,2,1,0:T(8,128)S(1)}, u32[]{:S(2)}) copy-start(f32[4,32,16,128]{3,2,1,0:T(8,128)S(1)} %mul.75.refs_1_) | copy-start | bytes 3145732
  111.5 12.3 %collective-permute-start.12 = (f32[4,32,16]{1,2,0:T(8,128)S(1)}, f32[4,32,16]{1,2,0:T(8,128)S(1)}, u32[]{:S(2)}, u32[]{:S(2)}) collective-permute-start(f32[4,32,16]{1,2,0:T(8,128)S(1)} %bitcast.106), channel_id=1, source_target_pairs={{0,1},{1,2},{2,3},{3,131},{131,130},{130,129},{129,128},{128,0},{4... | collective-permute-start | bytes 24584 | tf_op jit(solution)/shard_map/ppermute | solution.py:81
  112.3 11.5 %collective-permute-start.13 = (f32[4,32,16]{1,2,0:T(8,128)S(1)}, f32[4,32,16]{1,2,0:T(8,128)S(1)}, u32[]{:S(2)}, u32[]{:S(2)}) collective-permute-start(f32[4,32,16]{1,2,0:T(8,128)S(1)} %bitcast.107), channel_id=1, source_target_pairs={{1,0},{2,1},{3,2},{131,3},{130,131},{129,130},{128,129},{0,128},{5... | collective-permute-start | bytes 24584 | tf_op jit(solution)/shard_map/ppermute | solution.py:82
  116.0 10.1 %collective-permute-start.14 = (f32[4,32,128]{2,1,0:T(8,128)S(1)}, f32[4,32,128]{2,1,0:T(8,128)S(1)}, u32[]{:S(2)}, u32[]{:S(2)}) collective-permute-start(f32[4,32,128]{2,1,0:T(8,128)S(1)} %bitcast.97), channel_id=1, source_target_pairs={{0,4},{4,8},{8,12},{12,16},{16,20},{20,24},{24,28},{28,32},{32,36}... | collective-permute-start | bytes 196616 | tf_op jit(solution)/shard_map/ppermute | solution.py:76
  116.1 10.0 %collective-permute-start.15 = (f32[4,32,128]{2,1,0:T(8,128)S(1)}, f32[4,32,128]{2,1,0:T(8,128)S(1)}, u32[]{:S(2)}, u32[]{:S(2)}) collective-permute-start(f32[4,32,128]{2,1,0:T(8,128)S(1)} %bitcast.96), channel_id=1, source_target_pairs={{4,0},{8,4},{12,8},{16,12},{20,16},{24,20},{28,24},{32,28},{36,32}... | collective-permute-start | bytes 196616 | tf_op jit(solution)/shard_map/ppermute | solution.py:77
  137.2 11.9 %collective-permute-start.16 = (f32[4,32,16]{1,2,0:T(8,128)S(1)}, f32[4,32,16]{1,2,0:T(8,128)S(1)}, u32[]{:S(2)}, u32[]{:S(2)}) collective-permute-start(f32[4,32,16]{1,2,0:T(8,128)S(1)} %bitcast.108), channel_id=1, source_target_pairs={{0,1},{1,2},{2,3},{3,131},{131,130},{130,129},{129,128},{128,0},{4... | collective-permute-start | bytes 24584 | tf_op jit(solution)/shard_map/ppermute | solution.py:81
  137.8 11.3 %collective-permute-start.17 = (f32[4,32,16]{1,2,0:T(8,128)S(1)}, f32[4,32,16]{1,2,0:T(8,128)S(1)}, u32[]{:S(2)}, u32[]{:S(2)}) collective-permute-start(f32[4,32,16]{1,2,0:T(8,128)S(1)} %bitcast.109), channel_id=1, source_target_pairs={{1,0},{2,1},{3,2},{131,3},{130,131},{129,130},{128,129},{0,128},{5... | collective-permute-start | bytes 24584 | tf_op jit(solution)/shard_map/ppermute | solution.py:82
  141.4 10.0 %collective-permute-start.18 = (f32[4,32,128]{2,1,0:T(8,128)S(1)}, f32[4,32,128]{2,1,0:T(8,128)S(1)}, u32[]{:S(2)}, u32[]{:S(2)}) collective-permute-start(f32[4,32,128]{2,1,0:T(8,128)S(1)} %bitcast.118), channel_id=1, source_target_pairs={{0,4},{4,8},{8,12},{12,16},{16,20},{20,24},{24,28},{28,32},{32,36}... | collective-permute-start | bytes 196616 | tf_op jit(solution)/shard_map/ppermute | solution.py:76
  141.4 10.0 %collective-permute-start.19 = (f32[4,32,128]{2,1,0:T(8,128)S(1)}, f32[4,32,128]{2,1,0:T(8,128)S(1)}, u32[]{:S(2)}, u32[]{:S(2)}) collective-permute-start(f32[4,32,128]{2,1,0:T(8,128)S(1)} %bitcast.117), channel_id=1, source_target_pairs={{4,0},{8,4},{12,8},{16,12},{20,16},{24,20},{28,24},{32,28},{36,32}... | collective-permute-start | bytes 196616 | tf_op jit(solution)/shard_map/ppermute | solution.py:77
  (12 other events, 19.9 us)

commit v5 on v2

--- a/solution.py
+++ b/solution.py
@@ -136,7 +136,7 @@
     lax.fori_loop(0, x_ref.shape[1], body, 0, unroll=UNROLL)
 
 
-def backward_kernel(cpl, ly_ref, c_ref, b_ref, dp_ref, hns, hw, he, out_ref, fc, lc, frl, *, last):
+def backward_kernel(cpl, ly_ref, c_ref, b_ref, dp_ref, hns, hw, he, out_ref, *edge_refs, last):
     nf = ly_ref.shape[0]
     masks = edge_masks(ly_ref.shape[2:])
 
@@ -158,7 +158,7 @@
             else:
                 nxt = lam * dp_ref[o, l]
                 out_ref[o, l] = nxt
-                write_edges(nxt, o, l, fc, lc, frl)
+                write_edges(nxt, o, l, *edge_refs)
         return carry
 
     lax.fori_loop(0, ly_ref.shape[1], body, 0, unroll=UNROLL)
@@ -194,7 +194,7 @@
 
 
 def backward_step(cpl, ly, coef, back_coef, dprev, halo, last):
-    outs = [jax.ShapeDtypeStruct(ly.shape, ly.dtype)] + edge_shapes(ly)
+    outs = [jax.ShapeDtypeStruct(ly.shape, ly.dtype)] + ([] if last else edge_shapes(ly))
     ins = [ly, coef, back_coef, dprev, *halo]
     return pl.pallas_call(
         lambda *refs: backward_kernel(*refs, last=last),
@@ -275,7 +275,8 @@
         lam_y, *kernel_edges = backward_step(
             cpl, lam_y, coefficients, back_coef, dprev, edge_halos(*edges, wind_flip), last
         )
-        edges = squeezed(kernel_edges)
+        if not last:
+            edges = squeezed(kernel_edges)
     return (x, lam_y)
 
 

time: 159 us -> 158 us (level)
  no operation moved by 1% of the time
where the time goes in v5:
time: 158 us; the launch traced here: 157 us
  starting transfers between devices  60.6 us (38%)
  other arithmetic  31.7 us (20%)
  Pallas kernels  30.8 us (19%)
  local copies, waits for them, and re-layouts  28.5 us (18%)
  waiting for transfers between devices  4.12 us (3%)
  between operations  1.69 us (1%)
    ppermute x4, starting transfers between devices, edge_halos(): from_east = lax.ppermute(first_col, 'lon', down)  32.4 us
    pallas_call x2, Pallas kernels, forward_step(): pl.pallas_call(forward_kernel, out_shape=outs, grid=(x.shape[1] // LEVEL_...  16.5 us
    scatter-add x1, other arithmetic, on_device(): lam = jnp.zeros_like(table).at[row_of].add(spread).reshape(x.shape)  14.3 us
    pallas_call x2, Pallas kernels, backward_step(): pl.pallas_call(lambda *refs: backward_kernel(*refs, last=last), out_shape...  14.3 us
    all_to_all x1, starting transfers between devices, on_device(): arrived = lax.all_to_all(send, 'lon', 0, 0, tiled=True)  12.5 us
    gather x1, local copies, waits for them, and re-layouts, on_device(): picked = jnp.sum(jnp.where(lane_hit, table[row_of], 0.0), axis=1)  6.68 us
    ppermute x4, starting transfers between devices, edge_halos(): lax.ppermute(jnp.where(low, first_row, last_row), ('lon', 'lat'), ccw_pairs)  6.56 us
    another operation x4, local copies, waits for them, and re-layouts, edge_halos(): jnp.stack([north_row, south_row], axis=-1)  5.76 us
  transfers between devices with their start and end apart: 21, of which 3 were waited for; matrix products, arithmetic and copies ran while one was open for 19% of the time, Pallas kernels for 5%

profile of v5, /device:TPU:0, one launch (start us, length us, event | category | flops | bytes accessed | tf_op | source)
XLA Modules:
  0.0 157.5 jit_solution(977053247671254848)
XLA Ops:
  0.6 1.9 %fusion.25 = (f32[4,32,1,128]{3,2,1,0:T(1,128)}, f32[4,32,1,128]{3,2,1,0:T(1,128)}) fusion(f32[4,32,16,128]{3,2,1,0:T(8,128)} %x_ref.1), kind=kLoop, calls=%fused_computation.78 | loop fusion | bytes 262144 | tf_op jit(solution)/shard_map/slice | solution.py:209
  2.6 1.3 collective-permute-start.2
  4.6 1.0 convert_reduce_fusion
  7.8 1.9 %select_reduce_fusion = f32[2048,3]{0,1:T(4,128)S(1)} fusion(f32[512,3]{0,1:T(4,128)S(1)} %pad_maximum_fusion.6, pred[2048,512]{1,0:T(8,128)(4,1)S(1)} %iota_compare_fusion), kind=kLoop, calls=%fused_computation.2 | loop fusion | flops 6285312 | bytes 1079296 | tf_op jit(solution)/shard_map/reduce_sum | solution.py:243
  10.5 12.5 %all-to-all-start = ((f32[64,32,3]{1,2,0:T(4,128)}), f32[64,32,3]{1,2,0:T(4,128)S(1)}, u32[]{:S(2)}, u32[]{:S(2)}) async-start(f32[64,32,3]{1,2,0:T(4,128)} %copy.783), calls=%async_computation | async-start | bytes 262144 | tf_op jit(solution)/shard_map/all_to_all | solution.py:244
  23.9 3.2 %collective-permute-start.1 = (f32[4,32,16]{1,2,0:T(8,128)S(1)}, f32[4,32,16]{1,2,0:T(8,128)S(1)}, u32[]{:S(2)}, u32[]{:S(2)}) collective-permute-start(f32[4,32,16]{1,2,0:T(8,128)S(1)} %bitcast.92), channel_id=1, source_target_pairs={{1,0},{2,1},{3,2},{131,3},{130,131},{129,130},{128,129},{0,128},{5... | collective-permute-start | bytes 24584 | tf_op jit(solution)/shard_map/ppermute | solution.py:82
  28.6 3.6 %collective-permute-start.9 = (f32[4,32,16]{1,2,0:T(8,128)S(1)}, f32[4,32,16]{1,2,0:T(8,128)}, u32[]{:S(2)}, u32[]{:S(2)}) collective-permute-start(f32[4,32,16]{1,2,0:T(8,128)S(1)} %bitcast.91), channel_id=1, source_target_pairs={{1,0},{2,1},{3,2},{131,3},{130,131},{129,130},{128,129},{0,128},{5... | collective-permute-start | bytes 24584 | tf_op jit(solution)/shard_map/ppermute | solution.py:40
  33.5 1.5 fusion.24
  35.0 1.3 fusion.22
  37.2 7.9 %collective-permute-start.3 = (f32[4,32,128]{2,1,0:T(8,128)}, f32[4,32,128]{2,1,0:T(8,128)}, u32[]{:S(2)}, u32[]{:S(2)}) collective-permute-start(f32[4,32,128]{2,1,0:T(8,128)} %bitcast.6), channel_id=1, source_target_pairs={{4,0},{8,4},{12,8},{16,12},{20,16},{24,20},{28,24},{32,28},{36,32}... | collective-permute-start | bytes 196616 | tf_op jit(solution)/shard_map/ppermute | solution.py:77
  45.7 3.0 %collective-permute-start.10 = (f32[4,32,128]{2,1,0:T(8,128)}, f32[4,32,128]{2,1,0:T(8,128)}, u32[]{:S(2)}, u32[]{:S(2)}) collective-permute-start(f32[4,32,128]{2,1,0:T(8,128)} %bitcast.31), channel_id=1, source_target_pairs={{0,4},{4,8},{8,12},{12,16},{16,20},{20,24},{24,28},{28,32},{32,36}... | collective-permute-start | bytes 196616 | tf_op jit(solution)/shard_map/ppermute | solution.py:32
  48.7 1.5 fusion.12
  51.2 1.2 fusion.10
  53.4 1.4 copy.779.hns
  55.7 8.2 %shard_map.104 = (f32[4,32,16,128]{3,2,1,0:T(8,128)}, f32[4,32,16,128]{3,2,1,0:T(8,128)}, f32[4,32,1,128]{3,2,1,0:T(1,128)}, f32[4,32,1,128]{3,2,1,0:T(1,128)}, f32[4,32,16,2]{3,2,1,0:T(8,128)}) custom-call(f32[512]{0:T(512)} %reshape.106.cpl.refs_0_, f32[4,32,16,128]{3,2,1,0:T(8,128)} %x_ref.1, f32[4,32,16,128]{3,2,1,0:T(8,128)} %refs_2_.3, ...), custom_call_target="tpu_custom_call" | custom-call | tf_op jit(solution)/shard_map/pallas_call | solution.py:187
  64.0 7.7 %collective-permute-start.7 = (f32[4,32,128]{2,1,0:T(8,128)}, f32[4,32,128]{2,1,0:T(8,128)}, u32[]{:S(2)}, u32[]{:S(2)}) collective-permute-start(f32[4,32,128]{2,1,0:T(8,128)} %bitcast.104), channel_id=1, source_target_pairs={{4,0},{8,4},{12,8},{16,12},{20,16},{24,20},{28,24},{32,28},{36,32}... | collective-permute-start | bytes 196616 | tf_op jit(solution)/shard_map/ppermute | solution.py:77
  71.7 2.0 %slice_select_fusion.7 = (f32[4,32,16,1]{3,2,1,0:T(8,128)S(1)}, f32[4,32,16,1]{3,2,1,0:T(8,128)S(1)}) fusion(f32[4,32,16,2]{3,2,1,0:T(8,128)} %get-tuple-element.14, pred[]{:T(512)S(6)} %lt.44), kind=kLoop, calls=%fused_computation.26 | loop fusion | flops 4096 | bytes 32769 | tf_op jit(solution)/shard_map/jit(_where)/select_n | solution.py:81
  74.2 1.1 copy.781
  75.8 2.1 %fusion.refs_3_ = f32[4,32,16,128]{3,2,1,0:T(8,128)} fusion(f32[4,32,1,128]{3,2,1,0:T(1,128)} %bitcast.34, f32[4,32,15,128]{3,2,1,0:T(8,128)S(1)} %copy-done.4, f32[4,32,15,128]{3,2,1,0:T(8,128)S(1)} %copy-done.3, f32[4,32,1,128]{3,2,1,0:T(1,128)} %bitcast.32, f32[1,32,16,128]{3,2,1,0:T(8,128)S(1)} %fusion.10, f32[1,32,16,128]{3,2,1,0:T(8,128)} %fusion.11), kind=kLoop, calls=%fused_computation.7 | loop fusion | flops 3407872 | bytes 3670016 | tf_op jit(solution)/shard_map/stack | solution.py:264
  78.0 2.8 %collective-permute-done.4 = f32[4,32,16]{1,2,0:T(8,128)S(1)} collective-permute-done((f32[4,32,16]{1,2,0:T(8,128)S(1)}, f32[4,32,16]{1,2,0:T(8,128)S(1)}, u32[]{:S(2)}, u32[]{:S(2)}) %collective-permute-start.4) | collective-permute-done | bytes 8224 | tf_op jit(solution)/shard_map/ppermute | solution.py:81
  80.8 1.4 copy.782.hns
  82.9 8.3 %shard_map.105 = (f32[4,32,16,128]{3,2,1,0:T(8,128)}, f32[4,32,16,128]{3,2,1,0:T(8,128)}, f32[4,32,1,128]{3,2,1,0:T(1,128)}, f32[4,32,1,128]{3,2,1,0:T(1,128)}, f32[4,32,16,2]{3,2,1,0:T(8,128)}) custom-call(f32[512]{0:T(512)} %reshape.106.cpl.refs_0_, f32[4,32,16,128]{3,2,1,0:T(8,128)} %get-tuple-element.13.x_ref, f32[4,32,16,128]{3,2,1,0:T(8,128)} %refs_2_.3, ...), custom_call_target="tpu_custom_call" | custom-call | tf_op jit(solution)/shard_map/pallas_call | solution.py:187
  91.2 6.7 %gather_fusion = f32[2048,128]{1,0:T(8,128)S(1)} fusion(f32[2048,128]{1,0:T(8,128)} %bitcast.76, s32[2048]{0:T(1024)S(1)} %copy-done.13), kind=kCustom, calls=%fused_computation | custom fusion | bytes 2105344 | tf_op jit(solution)/shard_map/gather | solution.py:253
  98.5 14.3 %scatter_custom_fusion = f32[2048,128]{1,0:T(8,128)S(1)} fusion(s32[2048]{0:T(1024)S(1)} %bitcast.100, f32[2048]{0:T(1024)S(1)} %bitcast.87, s32[2048]{0:T(1024)S(1)} %bitcast.79, f32[]{:T(128)} %constant.46.clone.1), kind=kCustom, calls=%fused_computation.14 | custom fusion | flops 786432 | bytes 1065984 | tf_op jit(solution)/shard_map/scatter-add | solution.py:256
  115.4 7.7 %collective-permute-start.15 = (f32[4,32,128]{2,1,0:T(8,128)S(1)}, f32[4,32,128]{2,1,0:T(8,128)S(1)}, u32[]{:S(2)}, u32[]{:S(2)}) collective-permute-start(f32[4,32,128]{2,1,0:T(8,128)S(1)} %bitcast.85), channel_id=1, source_target_pairs={{4,0},{8,4},{12,8},{16,12},{20,16},{24,20},{28,24},{32,28},{36,32}... | collective-permute-start | bytes 196616 | tf_op jit(solution)/shard_map/ppermute | solution.py:77
  123.3 1.4 copy.793.refs_5_
  126.1 8.1 %shard_map.106 = (f32[4,32,16,128]{3,2,1,0:T(8,128)}, f32[4,32,1,128]{3,2,1,0:T(1,128)}, f32[4,32,1,128]{3,2,1,0:T(1,128)}, f32[4,32,16,2]{3,2,1,0:T(8,128)}) custom-call(f32[512]{0:T(512)} %reshape.106.cpl.refs_0_, f32[4,32,16,128]{3,2,1,0:T(8,128)} %copy-done.1, f32[4,32,16,128]{3,2,1,0:T(8,128)} %refs_2_.3, f32[4,32,16,128]{3,2,1,0:T(8,128)} %fusion.refs_3_, ...), custom_call_target="tpu_custom_call" | custom-call | tf_op jit(solution)/shard_map/pallas_call | solution.py:199
  134.2 1.9 %slice_select_fusion.3 = (f32[4,32,16,1]{3,2,1,0:T(8,128)S(1)}, f32[4,32,16,1]{3,2,1,0:T(8,128)S(1)}) fusion(f32[4,32,16,2]{3,2,1,0:T(8,128)} %get-tuple-element.21, pred[]{:T(512)S(6)} %lt.44), kind=kLoop, calls=%fused_computation.22 | loop fusion | flops 4096 | bytes 32769 | tf_op jit(solution)/shard_map/jit(_where)/select_n | solution.py:81
  137.1 2.4 %collective-permute-start.17 = (f32[4,32,16]{1,2,0:T(8,128)S(1)}, f32[4,32,16]{1,2,0:T(8,128)S(1)}, u32[]{:S(2)}, u32[]{:S(2)}) collective-permute-start(f32[4,32,16]{1,2,0:T(8,128)S(1)} %bitcast.98), channel_id=1, source_target_pairs={{1,0},{2,1},{3,2},{131,3},{130,131},{129,130},{128,129},{0,128},{5... | collective-permute-start | bytes 24584 | tf_op jit(solution)/shard_map/ppermute | solution.py:82
  139.5 9.0 %collective-permute-start.19 = (f32[4,32,128]{2,1,0:T(8,128)S(1)}, f32[4,32,128]{2,1,0:T(8,128)S(1)}, u32[]{:S(2)}, u32[]{:S(2)}) collective-permute-start(f32[4,32,128]{2,1,0:T(8,128)S(1)} %bitcast.106), channel_id=1, source_target_pairs={{4,0},{8,4},{12,8},{16,12},{20,16},{24,20},{28,24},{32,28},{36,32}... | collective-permute-start | bytes 196616 | tf_op jit(solution)/shard_map/ppermute | solution.py:77
  148.6 1.4 copy.796.refs_5_
  151.3 6.2 %shard_map.107 = f32[4,32,16,128]{3,2,1,0:T(8,128)} custom-call(f32[512]{0:T(512)} %reshape.106.cpl.refs_0_, f32[4,32,16,128]{3,2,1,0:T(8,128)} %get-tuple-element.20.refs_1_, f32[4,32,16,128]{3,2,1,0:T(8,128)} %refs_2_.3, f32[4,32,16,128]{3,2,1,0:T(8,128)} %fusion.refs_3_, f32[4,32,16,128]{3,2,1,0:T(8,128)} %get-tuple-element.19.refs_4_, ...), custom_call_target="tpu_custom_call" | custom-call | tf_op jit(solution)/shard_map/pallas_call | solution.py:199
  (118 shorter events, 19.7 us)
Async XLA Ops:
  0.6 7.2 %copy-start.19 = (f32[1,512]{1,0:T(1,128)S(1)}, f32[1,512]{1,0:T(1,128)}, u32[]{:S(2)}) copy-start(f32[1,512]{1,0:T(1,128)} %param.15) | copy-start | bytes 6148
  0.6 7.2 %copy-start.18 = (f32[1,512]{1,0:T(1,128)S(1)}, f32[1,512]{1,0:T(1,128)}, u32[]{:S(2)}) copy-start(f32[1,512]{1,0:T(1,128)} %param.14) | copy-start | bytes 6148
  2.6 53.1 %collective-permute-start.2 = (f32[4,32,128]{2,1,0:T(8,128)}, f32[4,32,128]{2,1,0:T(8,128)}, u32[]{:S(2)}, u32[]{:S(2)}) collective-permute-start(f32[4,32,128]{2,1,0:T(8,128)} %bitcast.4), channel_id=1, source_target_pairs={{0,4},{4,8},{8,12},{12,16},{16,20},{20,24},{24,28},{28,32},{32,36}... | collective-permute-start | bytes 196616 | tf_op jit(solution)/shard_map/ppermute | solution.py:76
  7.8 15.3 %copy-start.2 = (f32[4,32,16,128]{3,2,1,0:T(8,128)S(1)}, f32[4,32,16,128]{3,2,1,0:T(8,128)}, u32[]{:S(2)}) copy-start(f32[4,32,16,128]{3,2,1,0:T(8,128)} %x_ref.1) | copy-start | bytes 3145732
  10.5 44.3 %all-to-all-start = ((f32[64,32,3]{1,2,0:T(4,128)}), f32[64,32,3]{1,2,0:T(4,128)S(1)}, u32[]{:S(2)}, u32[]{:S(2)}) async-start(f32[64,32,3]{1,2,0:T(4,128)} %copy.783), calls=%async_computation | async-start | bytes 262144 | tf_op jit(solution)/shard_map/all_to_all | solution.py:244
  23.4 4.3 %copy-start = (f32[4,32,16,128]{3,2,1,0:T(8,128)S(1)}, f32[4,32,16,128]{3,2,1,0:T(8,128)}, u32[]{:S(2)}) copy-start(f32[4,32,16,128]{3,2,1,0:T(8,128)} %refs_2_.3) | copy-start | bytes 3145732
  23.9 13.3 %collective-permute-start.1 = (f32[4,32,16]{1,2,0:T(8,128)S(1)}, f32[4,32,16]{1,2,0:T(8,128)S(1)}, u32[]{:S(2)}, u32[]{:S(2)}) collective-permute-start(f32[4,32,16]{1,2,0:T(8,128)S(1)} %bitcast.92), channel_id=1, source_target_pairs={{1,0},{2,1},{3,2},{131,3},{130,131},{129,130},{128,129},{0,128},{5... | collective-permute-start | bytes 24584 | tf_op jit(solution)/shard_map/ppermute | solution.py:82
  27.7 17.5 %collective-permute-start = (f32[4,32,16]{1,2,0:T(8,128)S(1)}, f32[4,32,16]{1,2,0:T(8,128)S(1)}, u32[]{:S(2)}, u32[]{:S(2)}) collective-permute-start(f32[4,32,16]{1,2,0:T(8,128)S(1)} %bitcast.90), channel_id=1, source_target_pairs={{0,1},{1,2},{2,3},{3,131},{131,130},{130,129},{129,128},{128,0},{4... | collective-permute-start | bytes 24584 | tf_op jit(solution)/shard_map/ppermute | solution.py:81
  28.6 17.1 %collective-permute-start.9 = (f32[4,32,16]{1,2,0:T(8,128)S(1)}, f32[4,32,16]{1,2,0:T(8,128)}, u32[]{:S(2)}, u32[]{:S(2)}) collective-permute-start(f32[4,32,16]{1,2,0:T(8,128)S(1)} %bitcast.91), channel_id=1, source_target_pairs={{1,0},{2,1},{3,2},{131,3},{130,131},{129,130},{128,129},{0,128},{5... | collective-permute-start | bytes 24584 | tf_op jit(solution)/shard_map/ppermute | solution.py:40
  32.7 16.0 %collective-permute-start.8 = (f32[4,32,16]{1,2,0:T(8,128)S(1)}, f32[4,32,16]{1,2,0:T(8,128)S(1)}, u32[]{:S(2)}, u32[]{:S(2)}) collective-permute-start(f32[4,32,16]{1,2,0:T(8,128)S(1)} %bitcast.89), channel_id=1, source_target_pairs={{0,1},{1,2},{2,3},{3,131},{131,130},{130,129},{129,128},{128,0},{4... | collective-permute-start | bytes 24584 | tf_op jit(solution)/shard_map/ppermute | solution.py:39
  35.0 13.7 %copy-start.14 = (f32[4]{0:T(128)S(1)}, f32[4]{0:T(128)}, u32[]{:S(2)}) copy-start(f32[4]{0:T(128)} %constant.53.clone) | copy-start | bytes 52
  37.2 18.5 %collective-permute-start.3 = (f32[4,32,128]{2,1,0:T(8,128)}, f32[4,32,128]{2,1,0:T(8,128)}, u32[]{:S(2)}, u32[]{:S(2)}) collective-permute-start(f32[4,32,128]{2,1,0:T(8,128)} %bitcast.6), channel_id=1, source_target_pairs={{4,0},{8,4},{12,8},{16,12},{20,16},{24,20},{28,24},{32,28},{36,32}... | collective-permute-start | bytes 196616 | tf_op jit(solution)/shard_map/ppermute | solution.py:77
  45.1 30.2 %collective-permute-start.11 = (f32[4,32,128]{2,1,0:T(8,128)}, f32[4,32,128]{2,1,0:T(8,128)}, u32[]{:S(2)}, u32[]{:S(2)}) collective-permute-start(f32[4,32,128]{2,1,0:T(8,128)} %bitcast.33), channel_id=1, source_target_pairs={{4,0},{8,4},{12,8},{16,12},{20,16},{24,20},{28,24},{32,28},{36,32}... | collective-permute-start | bytes 196616 | tf_op jit(solution)/shard_map/ppermute | solution.py:33
  45.7 30.1 %collective-permute-start.10 = (f32[4,32,128]{2,1,0:T(8,128)}, f32[4,32,128]{2,1,0:T(8,128)}, u32[]{:S(2)}, u32[]{:S(2)}) collective-permute-start(f32[4,32,128]{2,1,0:T(8,128)} %bitcast.31), channel_id=1, source_target_pairs={{0,4},{4,8},{8,12},{12,16},{16,20},{20,24},{24,28},{28,32},{32,36}... | collective-permute-start | bytes 196616 | tf_op jit(solution)/shard_map/ppermute | solution.py:32
  63.9 18.3 %collective-permute-start.6 = (f32[4,32,128]{2,1,0:T(8,128)}, f32[4,32,128]{2,1,0:T(8,128)S(1)}, u32[]{:S(2)}, u32[]{:S(2)}) collective-permute-start(f32[4,32,128]{2,1,0:T(8,128)} %bitcast.105), channel_id=1, source_target_pairs={{0,4},{4,8},{8,12},{12,16},{16,20},{20,24},{24,28},{28,32},{32,36}... | collective-permute-start | bytes 196616 | tf_op jit(solution)/shard_map/ppermute | solution.py:76
  64.0 18.3 %collective-permute-start.7 = (f32[4,32,128]{2,1,0:T(8,128)}, f32[4,32,128]{2,1,0:T(8,128)}, u32[]{:S(2)}, u32[]{:S(2)}) collective-permute-start(f32[4,32,128]{2,1,0:T(8,128)} %bitcast.104), channel_id=1, source_target_pairs={{4,0},{8,4},{12,8},{16,12},{20,16},{24,20},{28,24},{32,28},{36,32}... | collective-permute-start | bytes 196616 | tf_op jit(solution)/shard_map/ppermute | solution.py:77
  75.3 2.7 %collective-permute-start.5 = (f32[4,32,16]{1,2,0:T(8,128)}, f32[4,32,16]{1,2,0:T(8,128)S(1)}, u32[]{:S(2)}, u32[]{:S(2)}) collective-permute-start(f32[4,32,16]{1,2,0:T(8,128)} %bitcast.95), channel_id=1, source_target_pairs={{1,0},{2,1},{3,2},{131,3},{130,131},{129,130},{128,129},{0,128},{5... | collective-permute-start | bytes 24584 | tf_op jit(solution)/shard_map/ppermute | solution.py:82
  75.3 5.4 %collective-permute-start.4 = (f32[4,32,16]{1,2,0:T(8,128)S(1)}, f32[4,32,16]{1,2,0:T(8,128)S(1)}, u32[]{:S(2)}, u32[]{:S(2)}) collective-permute-start(f32[4,32,16]{1,2,0:T(8,128)S(1)} %bitcast.93), channel_id=1, source_target_pairs={{0,1},{1,2},{2,3},{3,131},{131,130},{130,129},{129,128},{128,0},{4... | collective-permute-start | bytes 24584 | tf_op jit(solution)/shard_map/ppermute | solution.py:81
  75.8 4.9 %copy-start.15 = (f32[4]{0:T(128)S(1)}, f32[4]{0:T(128)}, u32[]{:S(2)}) copy-start(f32[4]{0:T(128)} %constant.53.clone) | copy-start | bytes 52
  82.9 8.3 %copy-start.13 = (s32[2048]{0:T(1024)S(1)}, s32[2048]{0:T(1024)}, u32[]{:S(2)}) copy-start(s32[2048]{0:T(1024)} %broadcast_clamp_fusion) | copy-start | bytes 24580
  97.8 14.9 %copy-start.5 = (f32[4,32,16,128]{3,2,1,0:T(8,128)S(1)}, f32[4,32,16,128]{3,2,1,0:T(8,128)}, u32[]{:S(2)}) copy-start(f32[4,32,16,128]{3,2,1,0:T(8,128)} %get-tuple-element.18) | copy-start | bytes 3145732
  113.3 9.9 %copy-start.16 = (f32[4]{0:T(128)S(1)}, f32[4]{0:T(128)}, u32[]{:S(2)}) copy-start(f32[4]{0:T(128)} %constant.53.clone) | copy-start | bytes 52
  114.3 8.9 %collective-permute-start.13 = (f32[4,32,16]{1,2,0:T(8,128)S(1)}, f32[4,32,16]{1,2,0:T(8,128)S(1)}, u32[]{:S(2)}, u32[]{:S(2)}) collective-permute-start(f32[4,32,16]{1,2,0:T(8,128)S(1)} %bitcast.97), channel_id=1, source_target_pairs={{1,0},{2,1},{3,2},{131,3},{130,131},{129,130},{128,129},{0,128},{5... | collective-permute-start | bytes 24584 | tf_op jit(solution)/shard_map/ppermute | solution.py:82
  115.2 7.9 %collective-permute-start.12 = (f32[4,32,16]{1,2,0:T(8,128)S(1)}, f32[4,32,16]{1,2,0:T(8,128)S(1)}, u32[]{:S(2)}, u32[]{:S(2)}) collective-permute-start(f32[4,32,16]{1,2,0:T(8,128)S(1)} %bitcast.94), channel_id=1, source_target_pairs={{0,1},{1,2},{2,3},{3,131},{131,130},{130,129},{129,128},{128,0},{4... | collective-permute-start | bytes 24584 | tf_op jit(solution)/shard_map/ppermute | solution.py:81
  115.3 10.1 %collective-permute-start.14 = (f32[4,32,128]{2,1,0:T(8,128)S(1)}, f32[4,32,128]{2,1,0:T(8,128)S(1)}, u32[]{:S(2)}, u32[]{:S(2)}) collective-permute-start(f32[4,32,128]{2,1,0:T(8,128)S(1)} %bitcast.86), channel_id=1, source_target_pairs={{0,4},{4,8},{8,12},{12,16},{16,20},{20,24},{24,28},{28,32},{32,36}... | collective-permute-start | bytes 196616 | tf_op jit(solution)/shard_map/ppermute | solution.py:76
  115.4 10.0 %collective-permute-start.15 = (f32[4,32,128]{2,1,0:T(8,128)S(1)}, f32[4,32,128]{2,1,0:T(8,128)S(1)}, u32[]{:S(2)}, u32[]{:S(2)}) collective-permute-start(f32[4,32,128]{2,1,0:T(8,128)S(1)} %bitcast.85), channel_id=1, source_target_pairs={{4,0},{8,4},{12,8},{16,12},{20,16},{24,20},{28,24},{32,28},{36,32}... | collective-permute-start | bytes 196616 | tf_op jit(solution)/shard_map/ppermute | solution.py:77
  136.1 3.4 %copy-start.21 = (f32[4,32,1,128]{3,2,1,0:T(1,128)S(1)}, f32[4,32,1,128]{3,2,1,0:T(1,128)}, u32[]{:S(2)}) copy-start(f32[4,32,1,128]{3,2,1,0:T(1,128)} %get-tuple-element.22) | copy-start | bytes 196612
  136.1 3.4 %copy-start.20 = (f32[4,32,1,128]{3,2,1,0:T(1,128)S(1)}, f32[4,32,1,128]{3,2,1,0:T(1,128)}, u32[]{:S(2)}) copy-start(f32[4,32,1,128]{3,2,1,0:T(1,128)} %get-tuple-element.23) | copy-start | bytes 196612
  137.1 11.4 %collective-permute-start.17 = (f32[4,32,16]{1,2,0:T(8,128)S(1)}, f32[4,32,16]{1,2,0:T(8,128)S(1)}, u32[]{:S(2)}, u32[]{:S(2)}) collective-permute-start(f32[4,32,16]{1,2,0:T(8,128)S(1)} %bitcast.98), channel_id=1, source_target_pairs={{1,0},{2,1},{3,2},{131,3},{130,131},{129,130},{128,129},{0,128},{5... | collective-permute-start | bytes 24584 | tf_op jit(solution)/shard_map/ppermute | solution.py:82
  139.5 9.0 %collective-permute-start.16 = (f32[4,32,16]{1,2,0:T(8,128)S(1)}, f32[4,32,16]{1,2,0:T(8,128)S(1)}, u32[]{:S(2)}, u32[]{:S(2)}) collective-permute-start(f32[4,32,16]{1,2,0:T(8,128)S(1)} %bitcast.96), channel_id=1, source_target_pairs={{0,1},{1,2},{2,3},{3,131},{131,130},{130,129},{129,128},{128,0},{4... | collective-permute-start | bytes 24584 | tf_op jit(solution)/shard_map/ppermute | solution.py:81
  139.5 11.1 %collective-permute-start.18 = (f32[4,32,128]{2,1,0:T(8,128)S(1)}, f32[4,32,128]{2,1,0:T(8,128)S(1)}, u32[]{:S(2)}, u32[]{:S(2)}) collective-permute-start(f32[4,32,128]{2,1,0:T(8,128)S(1)} %bitcast.107), channel_id=1, source_target_pairs={{0,4},{4,8},{8,12},{12,16},{16,20},{20,24},{24,28},{28,32},{32,36}... | collective-permute-start | bytes 196616 | tf_op jit(solution)/shard_map/ppermute | solution.py:76
  139.5 11.1 %collective-permute-start.19 = (f32[4,32,128]{2,1,0:T(8,128)S(1)}, f32[4,32,128]{2,1,0:T(8,128)S(1)}, u32[]{:S(2)}, u32[]{:S(2)}) collective-permute-start(f32[4,32,128]{2,1,0:T(8,128)S(1)} %bitcast.106), channel_id=1, source_target_pairs={{4,0},{8,4},{12,8},{16,12},{20,16},{24,20},{28,24},{32,28},{36,32}... | collective-permute-start | bytes 196616 | tf_op jit(solution)/shard_map/ppermute | solution.py:77
  (11 other events, 12.5 us)
